TPU v7x, 1024 devices: a whole 8x8x8 slice. The times are simulated.
1024 devices in a mesh: view: 4 (over y_hi, core), row: 32 (over x, y_lo), col: 8 (over z).
Axes of the slice: x: 8, y: 8 (y_hi: 2, y_lo: 4; y = y_hi * 4 + y_lo), z: 8, core: 2. Of those that a mesh axis runs over, the one named last changes fastest.
Arguments:
- estimate: float32 [256, 512, 128], P('col', 'row'), may hold values from 0.5 to 2
- views: bfloat16 [8, 256, 512, 128], P('view', 'col', 'row'), may hold values from 0.3 to 41.5, as said below
- kernel_xdir: float32 [8, 31], P('view'), may hold values from 0.2 to 1.2, as said below
- kernel_ydir: float32 [8, 31], P('view'), may hold values from 0.2 to 1.2, as said below
- kernel_axial: float32 [8, 121], P('view'), may hold values from 0.2 to 1.2, as said below
Outputs:
- restored: float32 [256, 512, 128], P('col', 'row')
Inputs may be any that keep to these rules, and one draw needn't show every extreme that they name: `kernel_xdir`: every tap is positive. `kernel_ydir`: every tap is positive. `kernel_axial`: every tap is positive. `views`: every value is positive.
All inputs are finite; a program needn't handle non-finite values.
Results may differ from a plain program's by a relative error of at most 0.00035.
Values may be sent and summed in bfloat16 or wider, within the bound.
No kernel may reach another device: no remote copies, remote signals or barrier semaphores. Data moves between devices by JAX's collectives and lax.ppermute only.
A program may use at most 32 MiB of HBM per device.

v0:
```python
import jax
import jax.numpy as jnp
from jax import lax
from jax.sharding import PartitionSpec as P

ITERS = 2


def extended(shard, sides, width):
    for axis, dim in sides:
        count, length = (lax.axis_size(axis), shard.shape[dim])
        up = [(i, (i + 1) % count) for i in range(count - 1)]
        down = [(j, i) for i, j in up]
        last = lax.slice_in_dim(shard, length - width, length, axis=dim)
        initial = lax.slice_in_dim(shard, 0, width, axis=dim)
        before = lax.ppermute(last, axis, up)
        after = lax.ppermute(initial, axis, down)
        shard = jnp.concatenate([before, shard, after], axis=dim)
    return shard


def toeplitz_band(kernel, height, breadth, offset):
    extent = height + breadth
    zeros_pad = jnp.zeros((extent,), kernel.dtype)
    padded = jnp.concatenate([zeros_pad, kernel, zeros_pad])
    leading = lax.slice_in_dim(padded, extent + offset, extent + offset + breadth)
    trailing = lax.slice_in_dim(padded, extent + offset - height, extent + offset)
    ribbon = jnp.concatenate([leading, trailing])
    tiled = jnp.tile(ribbon, height)[: height * (extent - 1)]
    return tiled.reshape(height, extent - 1)[:, :breadth]


def normalized(kernel):
    return (kernel / jnp.sum(kernel, axis=1, keepdims=True)).astype(jnp.bfloat16)


def on_device(estimate, views, kernel_xdir, kernel_ydir, kernel_axial):
    planes_local, height, across = estimate.shape
    planes = planes_local * lax.axis_size("col")
    view_count = views.shape[0]
    total_views = view_count * lax.axis_size("view")
    radius_lat = kernel_xdir.shape[1] // 2
    radius_ax = kernel_axial.shape[1] // 2
    taps_xdir = normalized(kernel_xdir)
    taps_ydir = normalized(kernel_ydir)
    taps_axial = normalized(kernel_axial)
    framed_rows = height + 2 * radius_lat
    bands_x = jnp.stack(
        [
            toeplitz_band(taps_xdir[member], across, across, radius_lat)
            for member in range(view_count)
        ]
    )
    bands_y = jnp.stack(
        [toeplitz_band(taps_ydir[member], height, framed_rows, 0) for member in range(view_count)]
    )
    bands_yback = jnp.stack(
        [
            toeplitz_band(taps_ydir[member][::-1], height, framed_rows, 0)
            for member in range(view_count)
        ]
    )
    bands_z = jnp.stack(
        [
            toeplitz_band(taps_axial[member], planes, planes, radius_ax)
            for member in range(view_count)
        ]
    )

    def framed(field):
        return extended(field, (("row", 2),), radius_lat)

    def to_columns(field):
        return lax.all_to_all(field, "col", split_axis=3, concat_axis=1, tiled=True)

    view_columns = to_columns(views)
    column_shape = view_columns.shape
    column_width = column_shape[2] * column_shape[3]
    view_columns = view_columns.reshape(view_count, planes, column_width)

    def correct(coarse, opening, amount):
        chosen = slice(opening, opening + amount)
        matrix_x = bands_x[chosen]
        matrix_y = bands_y[chosen]
        matrix_yback = bands_yback[chosen]
        matrix_z = bands_z[chosen]
        smeared = jnp.einsum(
            "zyj,vij->vzyi", coarse, matrix_x, preferred_element_type=jnp.float32
        ).astype(jnp.bfloat16)
        lateral = jnp.einsum(
            "vij,vzjx->vzix", matrix_y, framed(smeared), preferred_element_type=jnp.float32
        ).astype(jnp.bfloat16)
        columns = to_columns(lateral)
        blurred = jnp.einsum(
            "vij,vjm->vim",
            matrix_z,
            columns.reshape(amount, planes, column_width),
            preferred_element_type=jnp.float32,
        )
        quotient = (view_columns[chosen] / blurred).astype(jnp.bfloat16)
        returned = jnp.einsum(
            "vij,vim->vjm", matrix_z, quotient, preferred_element_type=jnp.float32
        ).astype(jnp.bfloat16)
        slab_back = lax.all_to_all(
            returned.reshape(columns.shape), "col", split_axis=1, concat_axis=3, tiled=True
        )
        backward = jnp.einsum(
            "vij,vzjx->vzix", matrix_yback, framed(slab_back), preferred_element_type=jnp.float32
        ).astype(jnp.bfloat16)
        return jnp.einsum("vzyi,vij->zyj", backward, matrix_x, preferred_element_type=jnp.float32)

    restored = estimate
    for iteration in range(ITERS):
        coarse = restored.astype(jnp.bfloat16)
        accumulated = correct(coarse, 0, 1)
        member = 1
        accumulated = accumulated + correct(coarse, member, 1)
        summed = lax.psum(accumulated, "view")
        restored = restored * summed / total_views
    return restored


def solution(mesh):
    placed = (
        P("col", "row", None),
        P("view", "col", "row", None),
        P("view", None),
        P("view", None),
        P("view", None),
    )
    return jax.shard_map(
        on_device, mesh=mesh, in_specs=placed, out_specs=P("col", "row", None), check_vma=False
    )
```

profile of v0, /device:TPU:1, one launch (start us, length us, event | category | flops | bytes accessed | tf_op | source)
XLA Modules:
  0.0 375.2 jit_solution(9866903478189476165)
XLA Ops:
  6.5 1.0 convert_element_type.175
  8.5 1.3 collective-permute-start.1
  9.8 4.8 %collective-permute-start = (bf16[1,32,15,128]{3,1,2,0:T(8,128)(2,1)S(1)}, bf16[1,32,15,128]{3,1,2,0:T(8,128)(2,1)S(1)}, u32[]{:S(2)}, u32[]{:S(2)}) collective-permute-start(bf16[1,32,15,128]{3,1,2,0:T(8,128)(2,1)S(1)} %get-tuple-element.21), channel_id=1, source_target_pairs={{0,8},{8,16},{16,24},{24,32},{32,40},{40,48},{48,56},{56,64},{64,7... | collective-permute-start | bytes 368648 | tf_op jit(solution)/shard_map/ppermute | solution.py:16
  15.2 1.3 collective-permute-start.5
  16.5 4.0 %collective-permute-start.4 = (bf16[1,32,15,128]{3,1,2,0:T(8,128)(2,1)S(1)}, bf16[1,32,15,128]{3,1,2,0:T(8,128)(2,1)S(1)}, u32[]{:S(2)}, u32[]{:S(2)}) collective-permute-start(bf16[1,32,15,128]{3,1,2,0:T(8,128)(2,1)S(1)} %get-tuple-element.17), channel_id=1, source_target_pairs={{0,8},{8,16},{16,24},{24,32},{32,40},{40,48},{48,56},{56,64},{64,7... | collective-permute-start | bytes 368648 | tf_op jit(solution)/shard_map/ppermute | solution.py:16
  23.4 1.2 reshape.261
  24.6 16.4 %all-to-all-start.1 = ((bf16[8,2,4096]{2,1,0:T(2,128)(2,1)}), bf16[8,2,4096]{2,1,0:T(2,128)(2,1)S(1)}, u32[]{:S(2)}, u32[]{:S(2)}) async-start(bf16[8,2,4096]{2,1,0:T(2,128)(2,1)} %reshape.261), calls=%async_computation.1 | async-start | bytes 262144 | tf_op jit(solution)/shard_map/all_to_all | solution.py:74
  41.8 1.2 reshape.265
  43.0 6.1 %all-to-all-done.1 = bf16[8,2,4096]{2,1,0:T(2,128)(2,1)S(1)} async-done(((bf16[8,2,4096]{2,1,0:T(2,128)(2,1)}), bf16[8,2,4096]{2,1,0:T(2,128)(2,1)S(1)}, u32[]{:S(2)}, u32[]{:S(2)}) %all-to-all-start.1) | async-done | bytes 131104 | tf_op jit(solution)/shard_map/all_to_all | solution.py:74
  49.1 3.4 all-to-all-start.3
  52.5 1.5 copy.140
  54.0 1.7 reshape.259
  55.7 4.7 %all-to-all-done.3 = bf16[8,2,4096]{2,1,0:T(2,128)(2,1)S(1)} async-done(((bf16[8,2,4096]{2,1,0:T(2,128)(2,1)}), bf16[8,2,4096]{2,1,0:T(2,128)(2,1)S(1)}, u32[]{:S(2)}, u32[]{:S(2)}) %all-to-all-start.3) | async-done | bytes 131104 | tf_op jit(solution)/shard_map/all_to_all | solution.py:74
  60.4 3.9 %all-to-all-start = ((bf16[8,2,8192]{2,1,0:T(2,128)(2,1)}), bf16[8,2,8192]{2,1,0:T(2,128)(2,1)S(1)}, u32[]{:S(2)}, u32[]{:S(2)}) async-start(bf16[8,2,8192]{2,1,0:T(2,128)(2,1)} %reshape.259), calls=%async_computation | async-start | bytes 524288 | tf_op jit(solution)/shard_map/all_to_all | solution.py:74
  66.5 1.0 reshape.227
  68.0 1.0 reshape.236
  69.0 4.5 %all-to-all-done = bf16[8,2,8192]{2,1,0:T(2,128)(2,1)S(1)} async-done(((bf16[8,2,8192]{2,1,0:T(2,128)(2,1)}), bf16[8,2,8192]{2,1,0:T(2,128)(2,1)S(1)}, u32[]{:S(2)}, u32[]{:S(2)}) %all-to-all-start) | async-done | bytes 262176 | tf_op jit(solution)/shard_map/all_to_all | solution.py:74
  75.5 0.8 copy-done.4
  76.7 0.9 copy.149
  77.7 1.7 reshape.263
  79.4 3.4 all-to-all-start.2
  83.6 0.8 copy-done.3
  84.8 0.9 copy.162
  85.8 1.7 reshape.267
  87.5 3.1 all-to-all-done.2
  90.6 3.4 all-to-all-start.4
  94.3 0.7 reshape.264
  95.0 1.2 copy.192
  96.6 1.3 collective-permute-start.3
  97.9 4.0 %collective-permute-start.2 = (bf16[1,32,15,128]{3,2,1,0:T(8,128)(2,1)S(1)}, bf16[1,32,15,128]{3,2,1,0:T(8,128)(2,1)S(1)}, u32[]{:S(2)}, u32[]{:S(2)}) collective-permute-start(bf16[1,32,15,128]{3,2,1,0:T(8,128)(2,1)S(1)} %get-tuple-element.19), channel_id=1, source_target_pairs={{0,8},{8,16},{16,24},{24,32},{32,40},{40,48},{48,56},{56,64},{64,7... | collective-permute-start | bytes 368648 | tf_op jit(solution)/shard_map/ppermute | solution.py:16
  102.7 1.2 copy.193
  104.3 1.3 collective-permute-start.7
  105.6 6.3 %collective-permute-start.6 = (bf16[1,32,15,128]{3,2,1,0:T(8,128)(2,1)S(1)}, bf16[1,32,15,128]{3,2,1,0:T(8,128)(2,1)S(1)}, u32[]{:S(2)}, u32[]{:S(2)}) collective-permute-start(bf16[1,32,15,128]{3,2,1,0:T(8,128)(2,1)S(1)} %get-tuple-element.15), channel_id=1, source_target_pairs={{0,8},{8,16},{16,24},{24,32},{32,40},{40,48},{48,56},{56,64},{64,7... | collective-permute-start | bytes 368648 | tf_op jit(solution)/shard_map/ppermute | solution.py:16
  112.4 1.5 collective-permute-done.6
  113.9 1.0 convolution_add_fusion.1
  115.0 90.2 %all-reduce.15.cloned.1.call-done = f32[32,16,128]{2,1,0:T(8,128)} async-done(((f32[32,16,128]{2,1,0:T(8,128)}), f32[32,16,128]{2,1,0:T(8,128)}) %all-reduce.15.cloned.1.call-update) | async-done | bytes 262160 | tf_op jit(solution)/shard_map/psum | solution.py:118
  205.2 1.0 fusion.66
  206.6 1.3 collective-permute-start.9
  207.9 4.0 %collective-permute-start.8 = (bf16[1,32,15,128]{3,1,2,0:T(8,128)(2,1)S(1)}, bf16[1,32,15,128]{3,1,2,0:T(8,128)(2,1)S(1)}, u32[]{:S(2)}, u32[]{:S(2)}) collective-permute-start(bf16[1,32,15,128]{3,1,2,0:T(8,128)(2,1)S(1)} %get-tuple-element.13), channel_id=1, source_target_pairs={{0,8},{8,16},{16,24},{24,32},{32,40},{40,48},{48,56},{56,64},{64,7... | collective-permute-start | bytes 368648 | tf_op jit(solution)/shard_map/ppermute | solution.py:16
  212.0 1.3 collective-permute-start.13
  213.3 4.0 %collective-permute-start.12 = (bf16[1,32,15,128]{3,1,2,0:T(8,128)(2,1)S(1)}, bf16[1,32,15,128]{3,1,2,0:T(8,128)(2,1)S(1)}, u32[]{:S(2)}, u32[]{:S(2)}) collective-permute-start(bf16[1,32,15,128]{3,1,2,0:T(8,128)(2,1)S(1)} %get-tuple-element.9), channel_id=1, source_target_pairs={{0,8},{8,16},{16,24},{24,32},{32,40},{40,48},{48,56},{56,64},{64,7... | collective-permute-start | bytes 368648 | tf_op jit(solution)/shard_map/ppermute | solution.py:16
  218.0 1.2 reshape.269
  219.2 7.8 %all-to-all-start.5 = ((bf16[8,2,4096]{2,1,0:T(2,128)(2,1)}), bf16[8,2,4096]{2,1,0:T(2,128)(2,1)S(1)}, u32[]{:S(2)}, u32[]{:S(2)}) async-start(bf16[8,2,4096]{2,1,0:T(2,128)(2,1)} %reshape.269), calls=%async_computation.5 | async-start | bytes 262144 | tf_op jit(solution)/shard_map/all_to_all | solution.py:74
  227.8 1.2 reshape.273
  228.9 6.0 %all-to-all-done.5 = bf16[8,2,4096]{2,1,0:T(2,128)(2,1)S(1)} async-done(((bf16[8,2,4096]{2,1,0:T(2,128)(2,1)}), bf16[8,2,4096]{2,1,0:T(2,128)(2,1)S(1)}, u32[]{:S(2)}, u32[]{:S(2)}) %all-to-all-start.5) | async-done | bytes 131104 | tf_op jit(solution)/shard_map/all_to_all | solution.py:74
  235.0 3.4 all-to-all-start.7
  239.7 0.9 copy.174
  240.7 1.7 reshape.271
  242.4 3.8 %all-to-all-done.7 = bf16[8,2,4096]{2,1,0:T(2,128)(2,1)S(1)} async-done(((bf16[8,2,4096]{2,1,0:T(2,128)(2,1)}), bf16[8,2,4096]{2,1,0:T(2,128)(2,1)S(1)}, u32[]{:S(2)}, u32[]{:S(2)}) %all-to-all-start.7) | async-done | bytes 131104 | tf_op jit(solution)/shard_map/all_to_all | solution.py:74
  246.2 3.6 all-to-all-start.6
  251.2 0.9 copy.186
  252.1 1.7 reshape.275
  253.8 3.8 %all-to-all-done.6 = bf16[8,2,4096]{2,1,0:T(2,128)(2,1)S(1)} async-done(((bf16[8,2,4096]{2,1,0:T(2,128)(2,1)}), bf16[8,2,4096]{2,1,0:T(2,128)(2,1)S(1)}, u32[]{:S(2)}, u32[]{:S(2)}) %all-to-all-start.6) | async-done | bytes 131104 | tf_op jit(solution)/shard_map/all_to_all | solution.py:104
  257.6 3.4 all-to-all-start.8
  261.7 1.2 copy.194
  263.4 1.3 collective-permute-start.11
  264.7 4.0 %collective-permute-start.10 = (bf16[1,32,15,128]{3,2,1,0:T(8,128)(2,1)S(1)}, bf16[1,32,15,128]{3,2,1,0:T(8,128)(2,1)S(1)}, u32[]{:S(2)}, u32[]{:S(2)}) collective-permute-start(bf16[1,32,15,128]{3,2,1,0:T(8,128)(2,1)S(1)} %get-tuple-element.11), channel_id=1, source_target_pairs={{0,8},{8,16},{16,24},{24,32},{32,40},{40,48},{48,56},{56,64},{64,7... | collective-permute-start | bytes 368648 | tf_op jit(solution)/shard_map/ppermute | solution.py:16
  269.5 1.2 copy.195
  271.2 1.3 collective-permute-start.15
  272.5 4.0 %collective-permute-start.14 = (bf16[1,32,15,128]{3,2,1,0:T(8,128)(2,1)S(1)}, bf16[1,32,15,128]{3,2,1,0:T(8,128)(2,1)S(1)}, u32[]{:S(2)}, u32[]{:S(2)}) collective-permute-start(bf16[1,32,15,128]{3,2,1,0:T(8,128)(2,1)S(1)} %get-tuple-element.7), channel_id=1, source_target_pairs={{0,8},{8,16},{16,24},{24,32},{32,40},{40,48},{48,56},{56,64},{64,7... | collective-permute-start | bytes 368648 | tf_op jit(solution)/shard_map/ppermute | solution.py:16
  276.9 2.9 collective-permute-done.14
  279.8 1.0 convolution_add_fusion
  280.8 85.6 %all-reduce.17.cloned.1.call-done = f32[32,16,128]{2,1,0:T(8,128)} async-done(((f32[32,16,128]{2,1,0:T(8,128)}), f32[32,16,128]{2,1,0:T(8,128)}) %all-reduce.17.cloned.1.call-update) | async-done | bytes 262160 | tf_op jit(solution)/shard_map/psum | solution.py:118
  366.5 1.7 multiply_multiply_fusion
  (142 shorter events, 21.1 us)
Async XLA Ops:
  6.5 1.0 copy-start.5
  8.5 14.2 %collective-permute-start.1 = (bf16[1,32,15,128]{3,1,2,0:T(8,128)(2,1)S(1)}, bf16[1,32,15,128]{3,1,2,0:T(8,128)(2,1)S(1)}, u32[]{:S(2)}, u32[]{:S(2)}) collective-permute-start(bf16[1,32,15,128]{3,1,2,0:T(8,128)(2,1)S(1)} %get-tuple-element.22), channel_id=1, source_target_pairs={{8,0},{16,8},{24,16},{32,24},{40,32},{48,40},{56,48},{64,56},{72,6... | collective-permute-start | bytes 368648 | tf_op jit(solution)/shard_map/ppermute | solution.py:17
  9.8 12.9 %collective-permute-start = (bf16[1,32,15,128]{3,1,2,0:T(8,128)(2,1)S(1)}, bf16[1,32,15,128]{3,1,2,0:T(8,128)(2,1)S(1)}, u32[]{:S(2)}, u32[]{:S(2)}) collective-permute-start(bf16[1,32,15,128]{3,1,2,0:T(8,128)(2,1)S(1)} %get-tuple-element.21), channel_id=1, source_target_pairs={{0,8},{8,16},{16,24},{24,32},{32,40},{40,48},{48,56},{56,64},{64,7... | collective-permute-start | bytes 368648 | tf_op jit(solution)/shard_map/ppermute | solution.py:16
  15.2 5.3 %copy-start.6 = (f32[2,31]{1,0:T(2,128)S(1)}, f32[2,31]{1,0:T(2,128)}, u32[]{:S(2)}) copy-start(f32[2,31]{1,0:T(2,128)} %param.8) | copy-start | bytes 748
  15.2 25.8 %collective-permute-start.5 = (bf16[1,32,15,128]{3,1,2,0:T(8,128)(2,1)S(1)}, bf16[1,32,15,128]{3,1,2,0:T(8,128)(2,1)S(1)}, u32[]{:S(2)}, u32[]{:S(2)}) collective-permute-start(bf16[1,32,15,128]{3,1,2,0:T(8,128)(2,1)S(1)} %get-tuple-element.18), channel_id=1, source_target_pairs={{8,0},{16,8},{24,16},{32,24},{40,32},{48,40},{56,48},{64,56},{72,6... | collective-permute-start | bytes 368648 | tf_op jit(solution)/shard_map/ppermute | solution.py:17
  16.5 24.6 %collective-permute-start.4 = (bf16[1,32,15,128]{3,1,2,0:T(8,128)(2,1)S(1)}, bf16[1,32,15,128]{3,1,2,0:T(8,128)(2,1)S(1)}, u32[]{:S(2)}, u32[]{:S(2)}) collective-permute-start(bf16[1,32,15,128]{3,1,2,0:T(8,128)(2,1)S(1)} %get-tuple-element.17), channel_id=1, source_target_pairs={{0,8},{8,16},{16,24},{24,32},{32,40},{40,48},{48,56},{56,64},{64,7... | collective-permute-start | bytes 368648 | tf_op jit(solution)/shard_map/ppermute | solution.py:16
  20.8 0.7 copy-start.8
  21.6 0.7 copy-start.7
  24.6 24.5 %all-to-all-start.1 = ((bf16[8,2,4096]{2,1,0:T(2,128)(2,1)}), bf16[8,2,4096]{2,1,0:T(2,128)(2,1)S(1)}, u32[]{:S(2)}, u32[]{:S(2)}) async-start(bf16[8,2,4096]{2,1,0:T(2,128)(2,1)} %reshape.261), calls=%async_computation.1 | async-start | bytes 262144 | tf_op jit(solution)/shard_map/all_to_all | solution.py:74
  43.0 9.5 %copy-start.2 = (bf16[2,32,16,128]{3,2,1,0:T(8,128)(2,1)S(1)}, bf16[2,32,16,128]{3,2,1,0:T(8,128)(2,1)}, u32[]{:S(2)}) copy-start(bf16[2,32,16,128]{3,2,1,0:T(8,128)(2,1)} %param.6) | copy-start | bytes 786436
  49.1 11.3 %all-to-all-start.3 = ((bf16[8,2,4096]{2,1,0:T(2,128)(2,1)}), bf16[8,2,4096]{2,1,0:T(2,128)(2,1)S(1)}, u32[]{:S(2)}, u32[]{:S(2)}) async-start(bf16[8,2,4096]{2,1,0:T(2,128)(2,1)} %reshape.265), calls=%async_computation.3 | async-start | bytes 262144 | tf_op jit(solution)/shard_map/all_to_all | solution.py:74
  60.4 13.1 %all-to-all-start = ((bf16[8,2,8192]{2,1,0:T(2,128)(2,1)}), bf16[8,2,8192]{2,1,0:T(2,128)(2,1)S(1)}, u32[]{:S(2)}, u32[]{:S(2)}) async-start(bf16[8,2,8192]{2,1,0:T(2,128)(2,1)} %reshape.259), calls=%async_computation | async-start | bytes 524288 | tf_op jit(solution)/shard_map/all_to_all | solution.py:74
  75.3 0.9 copy-start.4
  79.4 11.2 %all-to-all-start.2 = ((bf16[8,2,4096]{2,1,0:T(2,128)(2,1)}), bf16[8,2,4096]{2,1,0:T(2,128)(2,1)S(1)}, u32[]{:S(2)}, u32[]{:S(2)}) async-start(bf16[8,2,4096]{2,1,0:T(2,128)(2,1)} %reshape.263), calls=%async_computation.2 | async-start | bytes 262144 | tf_op jit(solution)/shard_map/all_to_all | solution.py:104
  83.4 0.9 copy-start.3
  90.6 11.4 %all-to-all-start.4 = ((bf16[8,2,4096]{2,1,0:T(2,128)(2,1)}), bf16[8,2,4096]{2,1,0:T(2,128)(2,1)S(1)}, u32[]{:S(2)}, u32[]{:S(2)}) async-start(bf16[8,2,4096]{2,1,0:T(2,128)(2,1)} %reshape.267), calls=%async_computation.4 | async-start | bytes 262144 | tf_op jit(solution)/shard_map/all_to_all | solution.py:104
  94.1 111.1 %all-reduce.15.cloned.1.call-start = ((), (), s32[]{:S(2)}) async-start(), calls=%async_computation.9 | async-start | bytes 524288 | tf_op jit(solution)/shard_map/psum | solution.py:118
  96.6 15.4 %collective-permute-start.3 = (bf16[1,32,15,128]{3,2,1,0:T(8,128)(2,1)S(1)}, bf16[1,32,15,128]{3,2,1,0:T(8,128)(2,1)S(1)}, u32[]{:S(2)}, u32[]{:S(2)}) collective-permute-start(bf16[1,32,15,128]{3,2,1,0:T(8,128)(2,1)S(1)} %get-tuple-element.20), channel_id=1, source_target_pairs={{8,0},{16,8},{24,16},{32,24},{40,32},{48,40},{56,48},{64,56},{72,6... | collective-permute-start | bytes 368648 | tf_op jit(solution)/shard_map/ppermute | solution.py:17
  97.9 14.1 %collective-permute-start.2 = (bf16[1,32,15,128]{3,2,1,0:T(8,128)(2,1)S(1)}, bf16[1,32,15,128]{3,2,1,0:T(8,128)(2,1)S(1)}, u32[]{:S(2)}, u32[]{:S(2)}) collective-permute-start(bf16[1,32,15,128]{3,2,1,0:T(8,128)(2,1)S(1)} %get-tuple-element.19), channel_id=1, source_target_pairs={{0,8},{8,16},{16,24},{24,32},{32,40},{40,48},{48,56},{56,64},{64,7... | collective-permute-start | bytes 368648 | tf_op jit(solution)/shard_map/ppermute | solution.py:16
  104.3 8.1 %collective-permute-start.7 = (bf16[1,32,15,128]{3,2,1,0:T(8,128)(2,1)S(1)}, bf16[1,32,15,128]{3,2,1,0:T(8,128)(2,1)S(1)}, u32[]{:S(2)}, u32[]{:S(2)}) collective-permute-start(bf16[1,32,15,128]{3,2,1,0:T(8,128)(2,1)S(1)} %get-tuple-element.16), channel_id=1, source_target_pairs={{8,0},{16,8},{24,16},{32,24},{40,32},{48,40},{56,48},{64,56},{72,6... | collective-permute-start | bytes 368648 | tf_op jit(solution)/shard_map/ppermute | solution.py:17
  105.6 8.3 %collective-permute-start.6 = (bf16[1,32,15,128]{3,2,1,0:T(8,128)(2,1)S(1)}, bf16[1,32,15,128]{3,2,1,0:T(8,128)(2,1)S(1)}, u32[]{:S(2)}, u32[]{:S(2)}) collective-permute-start(bf16[1,32,15,128]{3,2,1,0:T(8,128)(2,1)S(1)} %get-tuple-element.15), channel_id=1, source_target_pairs={{0,8},{8,16},{16,24},{24,32},{32,40},{40,48},{48,56},{56,64},{64,7... | collective-permute-start | bytes 368648 | tf_op jit(solution)/shard_map/ppermute | solution.py:16
  114.9 90.3 %copy-start = (f32[32,16,128]{2,1,0:T(8,128)S(1)}, f32[32,16,128]{2,1,0:T(8,128)}, u32[]{:S(2)}) copy-start(f32[32,16,128]{2,1,0:T(8,128)} %param.5) | copy-start | bytes 786436
  206.6 10.6 %collective-permute-start.9 = (bf16[1,32,15,128]{3,1,2,0:T(8,128)(2,1)S(1)}, bf16[1,32,15,128]{3,1,2,0:T(8,128)(2,1)S(1)}, u32[]{:S(2)}, u32[]{:S(2)}) collective-permute-start(bf16[1,32,15,128]{3,1,2,0:T(8,128)(2,1)S(1)} %get-tuple-element.14), channel_id=1, source_target_pairs={{8,0},{16,8},{24,16},{32,24},{40,32},{48,40},{56,48},{64,56},{72,6... | collective-permute-start | bytes 368648 | tf_op jit(solution)/shard_map/ppermute | solution.py:17
  207.9 9.4 %collective-permute-start.8 = (bf16[1,32,15,128]{3,1,2,0:T(8,128)(2,1)S(1)}, bf16[1,32,15,128]{3,1,2,0:T(8,128)(2,1)S(1)}, u32[]{:S(2)}, u32[]{:S(2)}) collective-permute-start(bf16[1,32,15,128]{3,1,2,0:T(8,128)(2,1)S(1)} %get-tuple-element.13), channel_id=1, source_target_pairs={{0,8},{8,16},{16,24},{24,32},{32,40},{40,48},{48,56},{56,64},{64,7... | collective-permute-start | bytes 368648 | tf_op jit(solution)/shard_map/ppermute | solution.py:16
  212.0 15.0 %collective-permute-start.13 = (bf16[1,32,15,128]{3,1,2,0:T(8,128)(2,1)S(1)}, bf16[1,32,15,128]{3,1,2,0:T(8,128)(2,1)S(1)}, u32[]{:S(2)}, u32[]{:S(2)}) collective-permute-start(bf16[1,32,15,128]{3,1,2,0:T(8,128)(2,1)S(1)} %get-tuple-element.10), channel_id=1, source_target_pairs={{8,0},{16,8},{24,16},{32,24},{40,32},{48,40},{56,48},{64,56},{72,6... | collective-permute-start | bytes 368648 | tf_op jit(solution)/shard_map/ppermute | solution.py:17
  213.3 13.7 %collective-permute-start.12 = (bf16[1,32,15,128]{3,1,2,0:T(8,128)(2,1)S(1)}, bf16[1,32,15,128]{3,1,2,0:T(8,128)(2,1)S(1)}, u32[]{:S(2)}, u32[]{:S(2)}) collective-permute-start(bf16[1,32,15,128]{3,1,2,0:T(8,128)(2,1)S(1)} %get-tuple-element.9), channel_id=1, source_target_pairs={{0,8},{8,16},{16,24},{24,32},{32,40},{40,48},{48,56},{56,64},{64,7... | collective-permute-start | bytes 368648 | tf_op jit(solution)/shard_map/ppermute | solution.py:16
  219.2 15.8 %all-to-all-start.5 = ((bf16[8,2,4096]{2,1,0:T(2,128)(2,1)}), bf16[8,2,4096]{2,1,0:T(2,128)(2,1)S(1)}, u32[]{:S(2)}, u32[]{:S(2)}) async-start(bf16[8,2,4096]{2,1,0:T(2,128)(2,1)} %reshape.269), calls=%async_computation.5 | async-start | bytes 262144 | tf_op jit(solution)/shard_map/all_to_all | solution.py:74
  235.0 11.2 %all-to-all-start.7 = ((bf16[8,2,4096]{2,1,0:T(2,128)(2,1)}), bf16[8,2,4096]{2,1,0:T(2,128)(2,1)S(1)}, u32[]{:S(2)}, u32[]{:S(2)}) async-start(bf16[8,2,4096]{2,1,0:T(2,128)(2,1)} %reshape.273), calls=%async_computation.7 | async-start | bytes 262144 | tf_op jit(solution)/shard_map/all_to_all | solution.py:74
  246.2 11.4 %all-to-all-start.6 = ((bf16[8,2,4096]{2,1,0:T(2,128)(2,1)}), bf16[8,2,4096]{2,1,0:T(2,128)(2,1)S(1)}, u32[]{:S(2)}, u32[]{:S(2)}) async-start(bf16[8,2,4096]{2,1,0:T(2,128)(2,1)} %reshape.271), calls=%async_computation.6 | async-start | bytes 262144 | tf_op jit(solution)/shard_map/all_to_all | solution.py:104
  257.6 11.2 %all-to-all-start.8 = ((bf16[8,2,4096]{2,1,0:T(2,128)(2,1)}), bf16[8,2,4096]{2,1,0:T(2,128)(2,1)S(1)}, u32[]{:S(2)}, u32[]{:S(2)}) async-start(bf16[8,2,4096]{2,1,0:T(2,128)(2,1)} %reshape.275), calls=%async_computation.8 | async-start | bytes 262144 | tf_op jit(solution)/shard_map/all_to_all | solution.py:104
  261.0 105.5 %all-reduce.17.cloned.1.call-start = ((), (), s32[]{:S(2)}) async-start(), calls=%async_computation.10 | async-start | bytes 524288 | tf_op jit(solution)/shard_map/psum | solution.py:118
  263.4 13.1 %collective-permute-start.11 = (bf16[1,32,15,128]{3,2,1,0:T(8,128)(2,1)S(1)}, bf16[1,32,15,128]{3,2,1,0:T(8,128)(2,1)S(1)}, u32[]{:S(2)}, u32[]{:S(2)}) collective-permute-start(bf16[1,32,15,128]{3,2,1,0:T(8,128)(2,1)S(1)} %get-tuple-element.12), channel_id=1, source_target_pairs={{8,0},{16,8},{24,16},{32,24},{40,32},{48,40},{56,48},{64,56},{72,6... | collective-permute-start | bytes 368648 | tf_op jit(solution)/shard_map/ppermute | solution.py:17
  264.7 11.8 %collective-permute-start.10 = (bf16[1,32,15,128]{3,2,1,0:T(8,128)(2,1)S(1)}, bf16[1,32,15,128]{3,2,1,0:T(8,128)(2,1)S(1)}, u32[]{:S(2)}, u32[]{:S(2)}) collective-permute-start(bf16[1,32,15,128]{3,2,1,0:T(8,128)(2,1)S(1)} %get-tuple-element.11), channel_id=1, source_target_pairs={{0,8},{8,16},{16,24},{24,32},{32,40},{40,48},{48,56},{56,64},{64,7... | collective-permute-start | bytes 368648 | tf_op jit(solution)/shard_map/ppermute | solution.py:16
  271.2 5.7 %collective-permute-start.15 = (bf16[1,32,15,128]{3,2,1,0:T(8,128)(2,1)S(1)}, bf16[1,32,15,128]{3,2,1,0:T(8,128)(2,1)S(1)}, u32[]{:S(2)}, u32[]{:S(2)}) collective-permute-start(bf16[1,32,15,128]{3,2,1,0:T(8,128)(2,1)S(1)} %get-tuple-element.8), channel_id=1, source_target_pairs={{8,0},{16,8},{24,16},{32,24},{40,32},{48,40},{56,48},{64,56},{72,6... | collective-permute-start | bytes 368648 | tf_op jit(solution)/shard_map/ppermute | solution.py:17
  272.5 7.3 %collective-permute-start.14 = (bf16[1,32,15,128]{3,2,1,0:T(8,128)(2,1)S(1)}, bf16[1,32,15,128]{3,2,1,0:T(8,128)(2,1)S(1)}, u32[]{:S(2)}, u32[]{:S(2)}) collective-permute-start(bf16[1,32,15,128]{3,2,1,0:T(8,128)(2,1)S(1)} %get-tuple-element.7), channel_id=1, source_target_pairs={{0,8},{8,16},{16,24},{24,32},{32,40},{40,48},{48,56},{56,64},{64,7... | collective-permute-start | bytes 368648 | tf_op jit(solution)/shard_map/ppermute | solution.py:16
  280.8 85.7 %copy-start.1 = (f32[32,16,128]{2,1,0:T(8,128)S(1)}, f32[32,16,128]{2,1,0:T(8,128)}, u32[]{:S(2)}) copy-start(f32[32,16,128]{2,1,0:T(8,128)} %all-reduce.15.cloned.1.call-done) | copy-start | bytes 786436
Sparse Core Ops, SparseCore 0:
  115.1 90.0 all-reduce.14
  280.9 85.4 all-reduce.16
where the time goes:
time: 382 us; the launch traced here: 375 us
  waiting for transfers between devices  213 us (56%)
  starting transfers between devices  94.3 us (25%)
  local copies, waits for them, and re-layouts  42.8 us (11%)
  between operations  14.6 us (4%)
  matrix products  6.28 us (2%)
  other arithmetic  4.74 us (1%)
    psum x2, waiting for transfers between devices, on_device(): summed = lax.psum(accumulated, 'view')  176 us
    ppermute x8, starting transfers between devices, extended(): before = lax.ppermute(last, axis, up)  35.1 us
    all_to_all x5, starting transfers between devices, to_columns(): return lax.all_to_all(field, 'col', split_axis=3, concat_axis=1, tiled=True)  34.9 us
    all_to_all x5, waiting for transfers between devices, to_columns(): return lax.all_to_all(field, 'col', split_axis=3, concat_axis=1, tiled=True)  25 us
    unnamed x45, local copies, waits for them, and re-layouts  22.1 us
    all_to_all x4, starting transfers between devices, correct(): lax.all_to_all(returned.reshape(columns.shape), 'col', split_axis=1, conc...  13.8 us
    ppermute x8, starting transfers between devices, extended(): after = lax.ppermute(initial, axis, down)  10.3 us
  transfers between devices with their start and end apart: 27, of which 15 were waited for; matrix products, arithmetic and copies ran while one was open for 10% of the time, Pallas kernels for 0%

commit v1 on v0

--- a/solution.py
+++ b/solution.py
@@ -17,6 +17,17 @@
         after = lax.ppermute(initial, axis, down)
         shard = jnp.concatenate([before, shard, after], axis=dim)
     return shard
+
+
+def butterfly_sum(value, axis):
+    count = lax.axis_size(axis)
+    assert count & (count - 1) == 0
+    stride = 1
+    while stride < count:
+        pairs = [(i, i ^ stride) for i in range(count)]
+        value = value + lax.ppermute(value, axis, pairs)
+        stride *= 2
+    return value
 
 
 def toeplitz_band(kernel, height, breadth, offset):
@@ -112,10 +123,8 @@
     restored = estimate
     for iteration in range(ITERS):
         coarse = restored.astype(jnp.bfloat16)
-        accumulated = correct(coarse, 0, 1)
-        member = 1
-        accumulated = accumulated + correct(coarse, member, 1)
-        summed = lax.psum(accumulated, "view")
+        accumulated = correct(coarse, 0, view_count)
+        summed = butterfly_sum(accumulated, "view")
         restored = restored * summed / total_views
     return restored
 

time: 382 us -> 227 us (0.59)
  the two profiles are of different devices: /device:TPU:1 before, /device:TPU:90 now
where the time goes in v1:
time: 227 us; the launch traced here: 226 us
  waiting for transfers between devices  84.3 us (37%)
  starting transfers between devices  56.8 us (25%)
  blocking collectives  41 us (18%)
  local copies, waits for them, and re-layouts  38.7 us (17%)
  matrix products  3.03 us (1%)
    ppermute x4, waiting for transfers between devices, butterfly_sum(): value = value + lax.ppermute(value, axis, pairs)  38.1 us
    ppermute x4, waiting for transfers between devices, extended(): before = lax.ppermute(last, axis, up)  27.7 us
    all_to_all x2, blocking collectives, correct(): lax.all_to_all(returned.reshape(columns.shape), 'col', split_axis=1, conc...  26.3 us
    all_to_all x2, starting transfers between devices, to_columns(): return lax.all_to_all(field, 'col', split_axis=3, concat_axis=1, tiled=True)  23.7 us
    unnamed x41, local copies, waits for them, and re-layouts  16.2 us
    ppermute x4, starting transfers between devices, extended(): before = lax.ppermute(last, axis, up)  15 us
    all_to_all x1, blocking collectives, to_columns(): return lax.all_to_all(field, 'col', split_axis=3, concat_axis=1, tiled=True)  14.7 us
    ppermute x4, starting transfers between devices, extended(): after = lax.ppermute(initial, axis, down)  9.82 us
  transfers between devices with their start and end apart: 14, of which 13 were waited for; matrix products, arithmetic and copies ran while one was open for 5% of the time, Pallas kernels for 0%

profile of v1, /device:TPU:90, one launch (start us, length us, event | category | flops | bytes accessed | tf_op | source)
XLA Modules:
  0.0 226.5 jit_solution(18053304665997397006)
XLA Ops:
  0.0 2.7 %copy.75 = bf16[2,32,16,128]{1,2,0,3:T(8,128)(2,1)S(1)} copy(bf16[2,32,16,128]{3,2,1,0:T(8,128)(2,1)} %param.6) | data formatting | bytes 524288 | tf_op args[1]
  2.7 1.7 reshape.76
  4.4 16.8 %all-to-all-start = ((bf16[8,2,8192]{2,1,0:T(2,128)(2,1)}), bf16[8,2,8192]{2,1,0:T(2,128)(2,1)S(1)}, u32[]{:S(2)}, u32[]{:S(2)}) async-start(bf16[8,2,8192]{2,1,0:T(2,128)(2,1)} %reshape.76), calls=%async_computation | async-start | bytes 524288 | tf_op jit(solution)/shard_map/all_to_all | solution.py:85
  22.7 3.2 %collective-permute-start.1 = (bf16[2,32,15,128]{3,1,2,0:T(8,128)(2,1)S(1)}, bf16[2,32,15,128]{3,1,2,0:T(8,128)(2,1)S(1)}, u32[]{:S(2)}, u32[]{:S(2)}) collective-permute-start(bf16[2,32,15,128]{3,1,2,0:T(8,128)(2,1)S(1)} %get-tuple-element.12), channel_id=1, source_target_pairs={{8,0},{16,8},{24,16},{32,24},{40,32},{48,40},{56,48},{64,56},{72,6... | collective-permute-start | bytes 737288 | tf_op jit(solution)/shard_map/ppermute | solution.py:17
  25.9 2.7 %collective-permute-start = (bf16[2,32,15,128]{3,1,2,0:T(8,128)(2,1)S(1)}, bf16[2,32,15,128]{3,1,2,0:T(8,128)(2,1)S(1)}, u32[]{:S(2)}, u32[]{:S(2)}) collective-permute-start(bf16[2,32,15,128]{3,1,2,0:T(8,128)(2,1)S(1)} %get-tuple-element.11), channel_id=1, source_target_pairs={{0,8},{8,16},{16,24},{24,32},{32,40},{40,48},{48,56},{56,64},{64,7... | collective-permute-start | bytes 737288 | tf_op jit(solution)/shard_map/ppermute | solution.py:16
  29.4 0.4 reshape.56
  30.5 0.4 reshape.55
  31.0 1.0 collective-permute-done.1
  32.0 6.6 %collective-permute-done = bf16[2,32,15,128]{3,1,2,0:T(8,128)(2,1)S(1)} collective-permute-done((bf16[2,32,15,128]{3,1,2,0:T(8,128)(2,1)S(1)}, bf16[2,32,15,128]{3,1,2,0:T(8,128)(2,1)S(1)}, u32[]{:S(2)}, u32[]{:S(2)}) %collective-permute-start) | collective-permute-done | bytes 245792 | tf_op jit(solution)/shard_map/ppermute | solution.py:16
  38.7 0.3 fusion.2
  39.0 1.5 copy.80
  40.5 1.7 reshape.78
  42.2 6.9 %all-to-all-start.1 = ((bf16[8,2,8192]{2,1,0:T(2,128)(2,1)}), bf16[8,2,8192]{2,1,0:T(2,128)(2,1)S(1)}, u32[]{:S(2)}, u32[]{:S(2)}) async-start(bf16[8,2,8192]{2,1,0:T(2,128)(2,1)} %reshape.78), calls=%async_computation.1 | async-start | bytes 524288 | tf_op jit(solution)/shard_map/all_to_all | solution.py:85
  49.2 0.5 reshape.77
  49.7 0.4 copy.76
  50.3 0.9 copy.77
  51.2 0.6 reshape.67
  52.0 9.2 %all-to-all-done.1 = bf16[8,2,8192]{2,1,0:T(2,128)(2,1)S(1)} async-done(((bf16[8,2,8192]{2,1,0:T(2,128)(2,1)}), bf16[8,2,8192]{2,1,0:T(2,128)(2,1)S(1)}, u32[]{:S(2)}, u32[]{:S(2)}) %all-to-all-start.1) | async-done | bytes 262176 | tf_op jit(solution)/shard_map/all_to_all | solution.py:85
  61.2 0.5 reshape.79
  61.7 0.7 copy.82
  62.4 0.7 reshape.61
  63.1 0.5 convolution_convert_fusion.5
  63.6 3.0 %copy.86 = bf16[2,256,16,16]{3,2,0,1:T(8,128)(2,1)S(1)} copy(bf16[2,256,16,16]{1,3,2,0:T(8,128)(2,1)S(1)} %bitcast.165) | data formatting | bytes 524288 | tf_op jit(solution)/shard_map/reshape | solution.py:116
  66.6 2.2 reshape.80
  68.8 13.2 %all_to_all.75 = bf16[8,2,8192]{2,1,0:T(2,128)(2,1)S(1)} all-to-all(bf16[8,2,8192]{2,1,0:T(2,128)(2,1)S(1)} %reshape.80), channel_id=1, replica_groups=mesh['view'=4,'row'=32,'col'=8] {'col'}, dimensions={0} | all-to-all | bytes 524288 | tf_op jit(solution)/shard_map/all_to_all | solution.py:115
  81.9 1.4 reshape.81
  83.4 2.3 %copy.88 = bf16[2,32,16,8,16]{1,4,3,2,0:T(8,128)(2,1)S(1)} copy(bf16[2,32,16,8,16]{4,2,0,1,3:T(8,128)(2,1)S(1)} %bitcast.150) | data formatting | bytes 524288 | tf_op jit(solution)/shard_map/all_to_all | solution.py:115
  85.7 0.5 copy.89
  86.3 2.1 collective-permute-start.3
  88.4 3.9 %collective-permute-start.2 = (bf16[2,32,15,128]{3,2,0,1:T(8,128)(2,1)S(1)}, bf16[2,32,15,128]{3,2,0,1:T(8,128)(2,1)S(1)}, u32[]{:S(2)}, u32[]{:S(2)}) collective-permute-start(bf16[2,32,15,128]{3,2,0,1:T(8,128)(2,1)S(1)} %get-tuple-element.9), channel_id=1, source_target_pairs={{0,8},{8,16},{16,24},{24,32},{32,40},{40,48},{48,56},{56,64},{64,7... | collective-permute-start | bytes 737288 | tf_op jit(solution)/shard_map/ppermute | solution.py:16
  92.8 2.0 collective-permute-done.3
  94.7 7.1 %collective-permute-done.2 = bf16[2,32,15,128]{3,2,0,1:T(8,128)(2,1)S(1)} collective-permute-done((bf16[2,32,15,128]{3,2,0,1:T(8,128)(2,1)S(1)}, bf16[2,32,15,128]{3,2,0,1:T(8,128)(2,1)S(1)}, u32[]{:S(2)}, u32[]{:S(2)}) %collective-permute-start.2) | collective-permute-done | bytes 245792 | tf_op jit(solution)/shard_map/ppermute | solution.py:16
  101.9 0.5 fusion.5
  102.3 1.9 collective-permute-start.4
  104.3 1.5 collective-permute-done.4
  105.8 2.5 %collective-permute-start.5 = (f32[32,16,128]{2,1,0:T(8,128)S(1)}, f32[32,16,128]{2,1,0:T(8,128)S(1)}, u32[]{:S(2)}, u32[]{:S(2)}) collective-permute-start(f32[32,16,128]{2,1,0:T(8,128)S(1)} %add.36), channel_id=1, source_target_pairs={{0,512},{256,768},{512,0},{768,256},{1,513},{257,769},{513,1},{769... | collective-permute-start | bytes 786440 | tf_op jit(solution)/shard_map/ppermute | solution.py:28
  108.3 17.2 %collective-permute-done.5 = f32[32,16,128]{2,1,0:T(8,128)S(1)} collective-permute-done((f32[32,16,128]{2,1,0:T(8,128)S(1)}, f32[32,16,128]{2,1,0:T(8,128)S(1)}, u32[]{:S(2)}, u32[]{:S(2)}) %collective-permute-start.5) | collective-permute-done | bytes 262176 | tf_op jit(solution)/shard_map/ppermute | solution.py:28
  125.9 2.6 %collective-permute-start.7 = (bf16[2,32,15,128]{3,1,2,0:T(8,128)(2,1)S(1)}, bf16[2,32,15,128]{3,1,2,0:T(8,128)(2,1)S(1)}, u32[]{:S(2)}, u32[]{:S(2)}) collective-permute-start(bf16[2,32,15,128]{3,1,2,0:T(8,128)(2,1)S(1)} %get-tuple-element.8), channel_id=1, source_target_pairs={{8,0},{16,8},{24,16},{32,24},{40,32},{48,40},{56,48},{64,56},{72,6... | collective-permute-start | bytes 737288 | tf_op jit(solution)/shard_map/ppermute | solution.py:17
  128.5 3.5 %collective-permute-start.6 = (bf16[2,32,15,128]{3,1,2,0:T(8,128)(2,1)S(1)}, bf16[2,32,15,128]{3,1,2,0:T(8,128)(2,1)S(1)}, u32[]{:S(2)}, u32[]{:S(2)}) collective-permute-start(bf16[2,32,15,128]{3,1,2,0:T(8,128)(2,1)S(1)} %get-tuple-element.7), channel_id=1, source_target_pairs={{0,8},{8,16},{16,24},{24,32},{32,40},{40,48},{48,56},{56,64},{64,7... | collective-permute-start | bytes 737288 | tf_op jit(solution)/shard_map/ppermute | solution.py:16
  132.0 3.0 %collective-permute-done.7 = bf16[2,32,15,128]{3,1,2,0:T(8,128)(2,1)S(1)} collective-permute-done((bf16[2,32,15,128]{3,1,2,0:T(8,128)(2,1)S(1)}, bf16[2,32,15,128]{3,1,2,0:T(8,128)(2,1)S(1)}, u32[]{:S(2)}, u32[]{:S(2)}) %collective-permute-start.7) | collective-permute-done | bytes 245792 | tf_op jit(solution)/shard_map/ppermute | solution.py:17
  135.0 5.3 %collective-permute-done.6 = bf16[2,32,15,128]{3,1,2,0:T(8,128)(2,1)S(1)} collective-permute-done((bf16[2,32,15,128]{3,1,2,0:T(8,128)(2,1)S(1)}, bf16[2,32,15,128]{3,1,2,0:T(8,128)(2,1)S(1)}, u32[]{:S(2)}, u32[]{:S(2)}) %collective-permute-start.6) | collective-permute-done | bytes 245792 | tf_op jit(solution)/shard_map/ppermute | solution.py:16
  140.7 1.5 copy.94
  142.2 1.0 reshape.82
  143.2 14.7 %all_to_all.76 = bf16[8,2,8192]{2,1,0:T(2,128)(2,1)S(1)} all-to-all(bf16[8,2,8192]{2,1,0:T(2,128)(2,1)S(1)} %reshape.82), channel_id=1, replica_groups=mesh['view'=4,'row'=32,'col'=8] {'col'}, dimensions={0} | all-to-all | bytes 524288 | tf_op jit(solution)/shard_map/all_to_all | solution.py:85
  157.9 0.5 reshape.83
  158.4 0.7 copy.96
  159.1 0.7 reshape.65
  159.8 0.5 convolution_convert_fusion.1
  160.3 3.0 %copy.100 = bf16[2,256,16,16]{3,2,0,1:T(8,128)(2,1)S(1)} copy(bf16[2,256,16,16]{1,3,2,0:T(8,128)(2,1)S(1)} %bitcast.164) | data formatting | bytes 524288 | tf_op jit(solution)/shard_map/reshape | solution.py:116
  163.3 2.2 reshape.84
  165.5 13.1 %all_to_all.77 = bf16[8,2,8192]{2,1,0:T(2,128)(2,1)S(1)} all-to-all(bf16[8,2,8192]{2,1,0:T(2,128)(2,1)S(1)} %reshape.84), channel_id=1, replica_groups=mesh['view'=4,'row'=32,'col'=8] {'col'}, dimensions={0} | all-to-all | bytes 524288 | tf_op jit(solution)/shard_map/all_to_all | solution.py:115
  178.6 1.4 reshape.85
  180.0 2.3 %copy.102 = bf16[2,32,16,8,16]{1,4,3,2,0:T(8,128)(2,1)S(1)} copy(bf16[2,32,16,8,16]{4,2,0,1,3:T(8,128)(2,1)S(1)} %bitcast.152) | data formatting | bytes 524288 | tf_op jit(solution)/shard_map/all_to_all | solution.py:115
  182.4 0.5 copy.103
  183.0 2.1 collective-permute-start.9
  185.1 4.8 %collective-permute-start.8 = (bf16[2,32,15,128]{3,2,0,1:T(8,128)(2,1)S(1)}, bf16[2,32,15,128]{3,2,0,1:T(8,128)(2,1)S(1)}, u32[]{:S(2)}, u32[]{:S(2)}) collective-permute-start(bf16[2,32,15,128]{3,2,0,1:T(8,128)(2,1)S(1)} %get-tuple-element.5), channel_id=1, source_target_pairs={{0,8},{8,16},{16,24},{24,32},{32,40},{40,48},{48,56},{56,64},{64,7... | collective-permute-start | bytes 737288 | tf_op jit(solution)/shard_map/ppermute | solution.py:16
  190.0 3.4 %collective-permute-done.9 = bf16[2,32,15,128]{3,2,0,1:T(8,128)(2,1)S(1)} collective-permute-done((bf16[2,32,15,128]{3,2,0,1:T(8,128)(2,1)S(1)}, bf16[2,32,15,128]{3,2,0,1:T(8,128)(2,1)S(1)}, u32[]{:S(2)}, u32[]{:S(2)}) %collective-permute-start.9) | collective-permute-done | bytes 245792 | tf_op jit(solution)/shard_map/ppermute | solution.py:17
  193.3 8.6 %collective-permute-done.8 = bf16[2,32,15,128]{3,2,0,1:T(8,128)(2,1)S(1)} collective-permute-done((bf16[2,32,15,128]{3,2,0,1:T(8,128)(2,1)S(1)}, bf16[2,32,15,128]{3,2,0,1:T(8,128)(2,1)S(1)}, u32[]{:S(2)}, u32[]{:S(2)}) %collective-permute-start.8) | collective-permute-done | bytes 245792 | tf_op jit(solution)/shard_map/ppermute | solution.py:16
  202.0 0.5 fusion.9
  202.4 1.9 collective-permute-start.10
  204.4 1.5 collective-permute-done.10
  205.9 1.9 collective-permute-start.11
  207.8 17.8 %collective-permute-done.11 = f32[32,16,128]{2,1,0:T(8,128)S(1)} collective-permute-done((f32[32,16,128]{2,1,0:T(8,128)S(1)}, f32[32,16,128]{2,1,0:T(8,128)S(1)}, u32[]{:S(2)}, u32[]{:S(2)}) %collective-permute-start.11) | collective-permute-done | bytes 262176 | tf_op jit(solution)/shard_map/ppermute | solution.py:28
  225.7 0.8 multiply_multiply_fusion
  (84 shorter events, 4.8 us)
Async XLA Ops:
  0.0 21.2 %copy-start = (f32[32,16,128]{2,1,0:T(8,128)S(1)}, f32[32,16,128]{2,1,0:T(8,128)}, u32[]{:S(2)}) copy-start(f32[32,16,128]{2,1,0:T(8,128)} %param.5) | copy-start | bytes 786436
  0.0 21.2 %copy-start.7 = (f32[2,31]{1,0:T(2,128)S(1)}, f32[2,31]{1,0:T(2,128)}, u32[]{:S(2)}) copy-start(f32[2,31]{1,0:T(2,128)} %param.7) | copy-start | bytes 748
  4.4 24.2 %copy-start.8 = (f32[2,31]{1,0:T(2,128)S(1)}, f32[2,31]{1,0:T(2,128)}, u32[]{:S(2)}) copy-start(f32[2,31]{1,0:T(2,128)} %param.8) | copy-start | bytes 748
  4.4 24.6 %copy-start.9 = (f32[2,121]{1,0:T(2,128)S(1)}, f32[2,121]{1,0:T(2,128)}, u32[]{:S(2)}) copy-start(f32[2,121]{1,0:T(2,128)} %param.9) | copy-start | bytes 2908
  4.4 37.8 %all-to-all-start = ((bf16[8,2,8192]{2,1,0:T(2,128)(2,1)}), bf16[8,2,8192]{2,1,0:T(2,128)(2,1)S(1)}, u32[]{:S(2)}, u32[]{:S(2)}) async-start(bf16[8,2,8192]{2,1,0:T(2,128)(2,1)} %reshape.76), calls=%async_computation | async-start | bytes 524288 | tf_op jit(solution)/shard_map/all_to_all | solution.py:85
  22.4 7.6 %copy-start.10 = (pred[62]{0:T(512)(128)(4,1)S(1)}, pred[62]{0:T(512)(128)(4,1)}, u32[]{:S(2)}) copy-start(pred[62]{0:T(512)(128)(4,1)} %constant.14.clone.1) | copy-start | bytes 190
  22.7 9.3 %collective-permute-start.1 = (bf16[2,32,15,128]{3,1,2,0:T(8,128)(2,1)S(1)}, bf16[2,32,15,128]{3,1,2,0:T(8,128)(2,1)S(1)}, u32[]{:S(2)}, u32[]{:S(2)}) collective-permute-start(bf16[2,32,15,128]{3,1,2,0:T(8,128)(2,1)S(1)} %get-tuple-element.12), channel_id=1, source_target_pairs={{8,0},{16,8},{24,16},{32,24},{40,32},{48,40},{56,48},{64,56},{72,6... | collective-permute-start | bytes 737288 | tf_op jit(solution)/shard_map/ppermute | solution.py:17
  25.9 12.8 %collective-permute-start = (bf16[2,32,15,128]{3,1,2,0:T(8,128)(2,1)S(1)}, bf16[2,32,15,128]{3,1,2,0:T(8,128)(2,1)S(1)}, u32[]{:S(2)}, u32[]{:S(2)}) collective-permute-start(bf16[2,32,15,128]{3,1,2,0:T(8,128)(2,1)S(1)} %get-tuple-element.11), channel_id=1, source_target_pairs={{0,8},{8,16},{16,24},{24,32},{32,40},{40,48},{48,56},{56,64},{64,7... | collective-permute-start | bytes 737288 | tf_op jit(solution)/shard_map/ppermute | solution.py:16
  42.2 19.0 %all-to-all-start.1 = ((bf16[8,2,8192]{2,1,0:T(2,128)(2,1)}), bf16[8,2,8192]{2,1,0:T(2,128)(2,1)S(1)}, u32[]{:S(2)}, u32[]{:S(2)}) async-start(bf16[8,2,8192]{2,1,0:T(2,128)(2,1)} %reshape.78), calls=%async_computation.1 | async-start | bytes 524288 | tf_op jit(solution)/shard_map/all_to_all | solution.py:85
  52.0 11.1 %copy-start.5 = (f32[2,256,256]{2,1,0:T(8,128)}, f32[2,256,256]{2,1,0:T(8,128)S(1)}, u32[]{:S(2)}) copy-start(f32[2,256,256]{2,1,0:T(8,128)S(1)} %copy.84) | copy-start | bytes 1572868
  86.3 39.2 %copy-start.1 = (f32[32,16,128]{2,1,0:T(8,128)S(1)}, f32[32,16,128]{2,1,0:T(8,128)}, u32[]{:S(2)}) copy-start(f32[32,16,128]{2,1,0:T(8,128)} %param.5) | copy-start | bytes 786436
  86.3 8.4 %collective-permute-start.3 = (bf16[2,32,15,128]{3,2,0,1:T(8,128)(2,1)S(1)}, bf16[2,32,15,128]{3,2,0,1:T(8,128)(2,1)S(1)}, u32[]{:S(2)}, u32[]{:S(2)}) collective-permute-start(bf16[2,32,15,128]{3,2,0,1:T(8,128)(2,1)S(1)} %get-tuple-element.10), channel_id=1, source_target_pairs={{8,0},{16,8},{24,16},{32,24},{40,32},{48,40},{56,48},{64,56},{72,6... | collective-permute-start | bytes 737288 | tf_op jit(solution)/shard_map/ppermute | solution.py:17
  88.4 13.4 %collective-permute-start.2 = (bf16[2,32,15,128]{3,2,0,1:T(8,128)(2,1)S(1)}, bf16[2,32,15,128]{3,2,0,1:T(8,128)(2,1)S(1)}, u32[]{:S(2)}, u32[]{:S(2)}) collective-permute-start(bf16[2,32,15,128]{3,2,0,1:T(8,128)(2,1)S(1)} %get-tuple-element.9), channel_id=1, source_target_pairs={{0,8},{8,16},{16,24},{24,32},{32,40},{40,48},{48,56},{56,64},{64,7... | collective-permute-start | bytes 737288 | tf_op jit(solution)/shard_map/ppermute | solution.py:16
  102.3 3.4 %collective-permute-start.4 = (f32[32,16,128]{2,1,0:T(8,128)S(1)}, f32[32,16,128]{2,1,0:T(8,128)S(1)}, u32[]{:S(2)}, u32[]{:S(2)}) collective-permute-start(f32[32,16,128]{2,1,0:T(8,128)S(1)} %fusion.5), channel_id=1, source_target_pairs={{0,256},{256,0},{512,768},{768,512},{1,257},{257,1},{513,769},{769... | collective-permute-start | bytes 786440 | tf_op jit(solution)/shard_map/ppermute | solution.py:28
  105.8 19.8 %collective-permute-start.5 = (f32[32,16,128]{2,1,0:T(8,128)S(1)}, f32[32,16,128]{2,1,0:T(8,128)S(1)}, u32[]{:S(2)}, u32[]{:S(2)}) collective-permute-start(f32[32,16,128]{2,1,0:T(8,128)S(1)} %add.36), channel_id=1, source_target_pairs={{0,512},{256,768},{512,0},{768,256},{1,513},{257,769},{513,1},{769... | collective-permute-start | bytes 786440 | tf_op jit(solution)/shard_map/ppermute | solution.py:28
  125.6 14.8 %copy-start.3 = (f32[32,16,128]{2,1,0:T(8,128)}, f32[32,16,128]{2,1,0:T(8,128)S(1)}, u32[]{:S(2)}) copy-start(f32[32,16,128]{2,1,0:T(8,128)S(1)} %collective-permute-done.5) | copy-start | bytes 786436
  125.9 9.0 %collective-permute-start.7 = (bf16[2,32,15,128]{3,1,2,0:T(8,128)(2,1)S(1)}, bf16[2,32,15,128]{3,1,2,0:T(8,128)(2,1)S(1)}, u32[]{:S(2)}, u32[]{:S(2)}) collective-permute-start(bf16[2,32,15,128]{3,1,2,0:T(8,128)(2,1)S(1)} %get-tuple-element.8), channel_id=1, source_target_pairs={{8,0},{16,8},{24,16},{32,24},{40,32},{48,40},{56,48},{64,56},{72,6... | collective-permute-start | bytes 737288 | tf_op jit(solution)/shard_map/ppermute | solution.py:17
  128.5 11.8 %collective-permute-start.6 = (bf16[2,32,15,128]{3,1,2,0:T(8,128)(2,1)S(1)}, bf16[2,32,15,128]{3,1,2,0:T(8,128)(2,1)S(1)}, u32[]{:S(2)}, u32[]{:S(2)}) collective-permute-start(bf16[2,32,15,128]{3,1,2,0:T(8,128)(2,1)S(1)} %get-tuple-element.7), channel_id=1, source_target_pairs={{0,8},{8,16},{16,24},{24,32},{32,40},{40,48},{48,56},{56,64},{64,7... | collective-permute-start | bytes 737288 | tf_op jit(solution)/shard_map/ppermute | solution.py:16
  158.4 1.4 copy-start.6
  183.0 42.7 %copy-start.2 = (f32[32,16,128]{2,1,0:T(8,128)S(1)}, f32[32,16,128]{2,1,0:T(8,128)}, u32[]{:S(2)}) copy-start(f32[32,16,128]{2,1,0:T(8,128)} %param.5) | copy-start | bytes 786436
  183.0 42.7 %copy-start.4 = (f32[32,16,128]{2,1,0:T(8,128)S(1)}, f32[32,16,128]{2,1,0:T(8,128)}, u32[]{:S(2)}) copy-start(f32[32,16,128]{2,1,0:T(8,128)} %copy-done.3) | copy-start | bytes 786436
  183.0 10.3 %collective-permute-start.9 = (bf16[2,32,15,128]{3,2,0,1:T(8,128)(2,1)S(1)}, bf16[2,32,15,128]{3,2,0,1:T(8,128)(2,1)S(1)}, u32[]{:S(2)}, u32[]{:S(2)}) collective-permute-start(bf16[2,32,15,128]{3,2,0,1:T(8,128)(2,1)S(1)} %get-tuple-element.6), channel_id=1, source_target_pairs={{8,0},{16,8},{24,16},{32,24},{40,32},{48,40},{56,48},{64,56},{72,6... | collective-permute-start | bytes 737288 | tf_op jit(solution)/shard_map/ppermute | solution.py:17
  185.1 16.9 %collective-permute-start.8 = (bf16[2,32,15,128]{3,2,0,1:T(8,128)(2,1)S(1)}, bf16[2,32,15,128]{3,2,0,1:T(8,128)(2,1)S(1)}, u32[]{:S(2)}, u32[]{:S(2)}) collective-permute-start(bf16[2,32,15,128]{3,2,0,1:T(8,128)(2,1)S(1)} %get-tuple-element.5), channel_id=1, source_target_pairs={{0,8},{8,16},{16,24},{24,32},{32,40},{40,48},{48,56},{56,64},{64,7... | collective-permute-start | bytes 737288 | tf_op jit(solution)/shard_map/ppermute | solution.py:16
  202.4 3.4 %collective-permute-start.10 = (f32[32,16,128]{2,1,0:T(8,128)S(1)}, f32[32,16,128]{2,1,0:T(8,128)S(1)}, u32[]{:S(2)}, u32[]{:S(2)}) collective-permute-start(f32[32,16,128]{2,1,0:T(8,128)S(1)} %fusion.9), channel_id=1, source_target_pairs={{0,256},{256,0},{512,768},{768,512},{1,257},{257,1},{513,769},{769... | collective-permute-start | bytes 786440 | tf_op jit(solution)/shard_map/ppermute | solution.py:28
  205.9 19.8 %collective-permute-start.11 = (f32[32,16,128]{2,1,0:T(8,128)S(1)}, f32[32,16,128]{2,1,0:T(8,128)S(1)}, u32[]{:S(2)}, u32[]{:S(2)}) collective-permute-start(f32[32,16,128]{2,1,0:T(8,128)S(1)} %add.38), channel_id=1, source_target_pairs={{0,512},{256,768},{512,0},{768,256},{1,513},{257,769},{513,1},{769... | collective-permute-start | bytes 786440 | tf_op jit(solution)/shard_map/ppermute | solution.py:28

commit v2 on v1

--- a/solution.py
+++ b/solution.py
@@ -81,6 +81,9 @@
     def framed(field):
         return extended(field, (("row", 2),), radius_lat)
 
+    def framed_rows_of(field):
+        return extended(field, (("row", 1),), radius_lat)
+
     def to_columns(field):
         return lax.all_to_all(field, "col", split_axis=3, concat_axis=1, tiled=True)
 
@@ -89,17 +92,17 @@
     column_width = column_shape[2] * column_shape[3]
     view_columns = view_columns.reshape(view_count, planes, column_width)
 
-    def correct(coarse, opening, amount):
+    def correct(coarse_framed, opening, amount):
         chosen = slice(opening, opening + amount)
         matrix_x = bands_x[chosen]
         matrix_y = bands_y[chosen]
         matrix_yback = bands_yback[chosen]
         matrix_z = bands_z[chosen]
         smeared = jnp.einsum(
-            "zyj,vij->vzyi", coarse, matrix_x, preferred_element_type=jnp.float32
+            "zyj,vij->vzyi", coarse_framed, matrix_x, preferred_element_type=jnp.float32
         ).astype(jnp.bfloat16)
         lateral = jnp.einsum(
-            "vij,vzjx->vzix", matrix_y, framed(smeared), preferred_element_type=jnp.float32
+            "vij,vzjx->vzix", matrix_y, smeared, preferred_element_type=jnp.float32
         ).astype(jnp.bfloat16)
         columns = to_columns(lateral)
         blurred = jnp.einsum(
@@ -120,12 +123,35 @@
         ).astype(jnp.bfloat16)
         return jnp.einsum("vzyi,vij->zyj", backward, matrix_x, preferred_element_type=jnp.float32)
 
-    restored = estimate
+    half = planes_local // 2
+    core_bit = lax.axis_index("view") % 2
+    view_size = lax.axis_size("view")
+    to_core = [(i, i ^ 1) for i in range(view_size)]
+    to_far = [(i, i ^ 2) for i in range(view_size)]
+
+    def pick(field, which):
+        return lax.dynamic_slice_in_dim(field, which * half, half, axis=0)
+
+    def joined(mine, theirs):
+        return jnp.where(
+            core_bit == 0,
+            jnp.concatenate([mine, theirs], axis=0),
+            jnp.concatenate([theirs, mine], axis=0),
+        )
+
+    restored_mine = pick(estimate, core_bit)
+    coarse = estimate.astype(jnp.bfloat16)
     for iteration in range(ITERS):
-        coarse = restored.astype(jnp.bfloat16)
-        accumulated = correct(coarse, 0, view_count)
-        summed = butterfly_sum(accumulated, "view")
-        restored = restored * summed / total_views
+        if iteration:
+            coarse_mine = restored_mine.astype(jnp.bfloat16)
+            coarse = joined(coarse_mine, lax.ppermute(coarse_mine, "view", to_core))
+        accumulated = correct(framed_rows_of(coarse), 0, view_count)
+        paired = pick(accumulated, core_bit) + lax.ppermute(
+            pick(accumulated, 1 - core_bit), "view", to_core
+        )
+        summed = paired + lax.ppermute(paired, "view", to_far)
+        restored_mine = restored_mine * summed / total_views
+    restored = joined(restored_mine, lax.ppermute(restored_mine, "view", to_core))
     return restored
 
 

time: 227 us -> 215 us (0.947)
  the two profiles are of different devices: /device:TPU:90 before, /device:TPU:113 now
where the time goes in v2:
time: 215 us; the launch traced here: 211 us
  starting transfers between devices  73.6 us (34%)
  waiting for transfers between devices  49.7 us (23%)
  blocking collectives  40.4 us (19%)
  local copies, waits for them, and re-layouts  40.1 us (19%)
  matrix products  4.38 us (2%)
    all_to_all x2, blocking collectives, correct(): lax.all_to_all(returned.reshape(columns.shape), 'col', split_axis=1, conc...  25.8 us
    all_to_all x2, starting transfers between devices, to_columns(): return lax.all_to_all(field, 'col', split_axis=3, concat_axis=1, tiled=True)  22.7 us
    ppermute x4, starting transfers between devices, extended(): before = lax.ppermute(last, axis, up)  22.1 us
    ppermute x4, waiting for transfers between devices, extended(): before = lax.ppermute(last, axis, up)  17.6 us
    ppermute x2, waiting for transfers between devices, on_device(): summed = paired + lax.ppermute(paired, 'view', to_far)  17 us
    unnamed x51, local copies, waits for them, and re-layouts  16.2 us
    all_to_all x1, blocking collectives, to_columns(): return lax.all_to_all(field, 'col', split_axis=3, concat_axis=1, tiled=True)  14.6 us
    ppermute x4, starting transfers between devices, extended(): after = lax.ppermute(initial, axis, down)  10.3 us
  transfers between devices with their start and end apart: 16, of which 14 were waited for; matrix products, arithmetic and copies ran while one was open for 6% of the time, Pallas kernels for 0%

profile of v2, /device:TPU:113, one launch (start us, length us, event | category | flops | bytes accessed | tf_op | source)
XLA Modules:
  0.0 210.7 jit_solution(8492074741927800022)
XLA Ops:
  0.0 2.7 %copy.59 = bf16[2,32,16,128]{1,2,0,3:T(8,128)(2,1)S(1)} copy(bf16[2,32,16,128]{3,2,1,0:T(8,128)(2,1)} %param.6) | data formatting | bytes 524288 | tf_op args[1]
  2.8 1.7 reshape.76
  4.4 16.4 %all-to-all-start = ((bf16[8,2,8192]{2,1,0:T(2,128)(2,1)}), bf16[8,2,8192]{2,1,0:T(2,128)(2,1)S(1)}, u32[]{:S(2)}, u32[]{:S(2)}) async-start(bf16[8,2,8192]{2,1,0:T(2,128)(2,1)} %reshape.76), calls=%async_computation | async-start | bytes 524288 | tf_op jit(solution)/shard_map/all_to_all | solution.py:88
  20.9 2.9 %collective-permute-start.1 = (bf16[32,15,128]{2,1,0:T(8,128)(2,1)S(1)}, bf16[32,15,128]{2,1,0:T(8,128)(2,1)S(1)}, u32[]{:S(2)}, u32[]{:S(2)}) collective-permute-start(bf16[32,15,128]{2,1,0:T(8,128)(2,1)S(1)} %get-tuple-element.14), channel_id=1, source_target_pairs={{8,0},{16,8},{24,16},{32,24},{40,32},{48,40},{56,48},{64,56},{72,6... | collective-permute-start | bytes 368648 | tf_op jit(solution)/shard_map/ppermute | solution.py:17
  23.8 5.1 %collective-permute-start = (bf16[32,15,128]{2,1,0:T(8,128)(2,1)S(1)}, bf16[32,15,128]{2,1,0:T(8,128)(2,1)S(1)}, u32[]{:S(2)}, u32[]{:S(2)}) collective-permute-start(bf16[32,15,128]{2,1,0:T(8,128)(2,1)S(1)} %get-tuple-element.13), channel_id=1, source_target_pairs={{0,8},{8,16},{16,24},{24,32},{32,40},{40,48},{48,56},{56,64},{64,7... | collective-permute-start | bytes 368648 | tf_op jit(solution)/shard_map/ppermute | solution.py:16
  32.5 1.2 collective-permute-done
  33.8 0.7 fusion.14
  34.5 1.5 copy.62
  36.0 1.7 reshape.78
  37.6 6.3 %all-to-all-start.1 = ((bf16[8,2,8192]{2,1,0:T(2,128)(2,1)}), bf16[8,2,8192]{2,1,0:T(2,128)(2,1)S(1)}, u32[]{:S(2)}, u32[]{:S(2)}) async-start(bf16[8,2,8192]{2,1,0:T(2,128)(2,1)} %reshape.78), calls=%async_computation.1 | async-start | bytes 524288 | tf_op jit(solution)/shard_map/all_to_all | solution.py:88
  44.0 0.7 slice_bitcast_fusion.1
  45.8 0.9 copy.61
  46.7 0.6 reshape.67
  47.3 1.0 copy.66
  48.3 5.5 %all-to-all-done.1 = bf16[8,2,8192]{2,1,0:T(2,128)(2,1)S(1)} async-done(((bf16[8,2,8192]{2,1,0:T(2,128)(2,1)}), bf16[8,2,8192]{2,1,0:T(2,128)(2,1)S(1)}, u32[]{:S(2)}, u32[]{:S(2)}) %all-to-all-start.1) | async-done | bytes 262176 | tf_op jit(solution)/shard_map/all_to_all | solution.py:88
  53.8 0.5 reshape.79
  54.3 0.7 copy.64
  55.0 0.7 reshape.61
  55.7 1.5 convolution_convert_fusion.5
  57.2 3.0 %copy.68 = bf16[2,256,16,16]{3,2,0,1:T(8,128)(2,1)S(1)} copy(bf16[2,256,16,16]{1,3,2,0:T(8,128)(2,1)S(1)} %bitcast.181) | data formatting | bytes 524288 | tf_op jit(solution)/shard_map/reshape | solution.py:119
  60.2 2.2 %reshape.80 = bf16[8,2,8192]{2,1,0:T(2,128)(2,1)S(1)} reshape(bf16[256,2,16,16]{3,2,1,0:T(8,128)(2,1)S(1)} %bitcast.165) | data formatting | bytes 524288
  62.4 12.2 %all_to_all.75 = bf16[8,2,8192]{2,1,0:T(2,128)(2,1)S(1)} all-to-all(bf16[8,2,8192]{2,1,0:T(2,128)(2,1)S(1)} %reshape.80), channel_id=1, replica_groups=mesh['view'=4,'row'=32,'col'=8] {'col'}, dimensions={0} | all-to-all | bytes 524288 | tf_op jit(solution)/shard_map/all_to_all | solution.py:118
  74.6 1.4 reshape.81
  76.0 2.3 %copy.70 = bf16[2,32,16,8,16]{1,4,3,2,0:T(8,128)(2,1)S(1)} copy(bf16[2,32,16,8,16]{4,2,0,1,3:T(8,128)(2,1)S(1)} %bitcast.166) | data formatting | bytes 524288 | tf_op jit(solution)/shard_map/all_to_all | solution.py:118
  78.3 0.5 copy.71
  79.0 2.5 %collective-permute-start.3 = (bf16[2,32,15,128]{3,2,0,1:T(8,128)(2,1)S(1)}, bf16[2,32,15,128]{3,2,0,1:T(8,128)(2,1)S(1)}, u32[]{:S(2)}, u32[]{:S(2)}) collective-permute-start(bf16[2,32,15,128]{3,2,0,1:T(8,128)(2,1)S(1)} %get-tuple-element.10), channel_id=1, source_target_pairs={{8,0},{16,8},{24,16},{32,24},{40,32},{48,40},{56,48},{64,56},{72,6... | collective-permute-start | bytes 737288 | tf_op jit(solution)/shard_map/ppermute | solution.py:17
  81.6 5.4 %collective-permute-start.2 = (bf16[2,32,15,128]{3,2,0,1:T(8,128)(2,1)S(1)}, bf16[2,32,15,128]{3,2,0,1:T(8,128)(2,1)S(1)}, u32[]{:S(2)}, u32[]{:S(2)}) collective-permute-start(bf16[2,32,15,128]{3,2,0,1:T(8,128)(2,1)S(1)} %get-tuple-element.9), channel_id=1, source_target_pairs={{0,8},{8,16},{16,24},{24,32},{32,40},{40,48},{48,56},{56,64},{64,7... | collective-permute-start | bytes 737288 | tf_op jit(solution)/shard_map/ppermute | solution.py:16
  87.4 1.5 collective-permute-done.3
  88.9 7.2 %collective-permute-done.2 = bf16[2,32,15,128]{3,2,0,1:T(8,128)(2,1)S(1)} collective-permute-done((bf16[2,32,15,128]{3,2,0,1:T(8,128)(2,1)S(1)}, bf16[2,32,15,128]{3,2,0,1:T(8,128)(2,1)S(1)}, u32[]{:S(2)}, u32[]{:S(2)}) %collective-permute-start.2) | collective-permute-done | bytes 245792 | tf_op jit(solution)/shard_map/ppermute | solution.py:16
  96.6 3.6 %collective-permute-start.4 = (f32[16,16,128]{2,1,0:T(8,128)S(1)}, f32[16,16,128]{2,1,0:T(8,128)S(1)}, u32[]{:S(2)}, u32[]{:S(2)}) collective-permute-start(f32[16,16,128]{2,1,0:T(8,128)S(1)} %constant_dynamic-slice_fusion.1), channel_id=1, source_target_pairs={{0,256},{256,0},{512,768},{768,512},{1,257},{257,1},{513,769},{769... | collective-permute-start | bytes 393224 | tf_op jit(solution)/shard_map/ppermute | solution.py:149
  100.2 1.0 collective-permute-done.4
  101.2 2.2 %collective-permute-start.5 = (f32[16,16,128]{2,1,0:T(8,128)S(1)}, f32[16,16,128]{2,1,0:T(8,128)S(1)}, u32[]{:S(2)}, u32[]{:S(2)}) collective-permute-start(f32[16,16,128]{2,1,0:T(8,128)S(1)} %dynamic-slice_add_fusion.1), channel_id=1, source_target_pairs={{0,512},{256,768},{512,0},{768,256},{1,513},{257,769},{513,1},{769... | collective-permute-start | bytes 393224 | tf_op jit(solution)/shard_map/ppermute | solution.py:152
  103.3 8.5 %collective-permute-done.5 = f32[16,16,128]{2,1,0:T(8,128)S(1)} collective-permute-done((f32[16,16,128]{2,1,0:T(8,128)S(1)}, f32[16,16,128]{2,1,0:T(8,128)S(1)}, u32[]{:S(2)}, u32[]{:S(2)}) %collective-permute-start.5) | collective-permute-done | bytes 131104 | tf_op jit(solution)/shard_map/ppermute | solution.py:152
  111.9 3.3 %collective-permute-start.6 = (bf16[16,16,128]{2,1,0:T(8,128)(2,1)S(1)}, bf16[16,16,128]{2,1,0:T(8,128)(2,1)S(1)}, u32[]{:S(2)}, u32[]{:S(2)}) collective-permute-start(bf16[16,16,128]{2,1,0:T(8,128)(2,1)S(1)} %get-tuple-element.5), channel_id=1, source_target_pairs={{0,256},{256,0},{512,768},{768,512},{1,257},{257,1},{513,769},{769... | collective-permute-start | bytes 196616 | tf_op jit(solution)/shard_map/ppermute | solution.py:147
  115.2 0.9 collective-permute-done.6
  116.2 3.0 %collective-permute-start.8 = (bf16[32,15,128]{2,1,0:T(8,128)(2,1)S(1)}, bf16[32,15,128]{2,1,0:T(8,128)(2,1)S(1)}, u32[]{:S(2)}, u32[]{:S(2)}) collective-permute-start(bf16[32,15,128]{2,1,0:T(8,128)(2,1)S(1)} %get-tuple-element.12), channel_id=1, source_target_pairs={{8,0},{16,8},{24,16},{32,24},{40,32},{48,40},{56,48},{64,56},{72,6... | collective-permute-start | bytes 368648 | tf_op jit(solution)/shard_map/ppermute | solution.py:17
  119.2 5.5 %collective-permute-start.7 = (bf16[32,15,128]{2,1,0:T(8,128)(2,1)S(1)}, bf16[32,15,128]{2,1,0:T(8,128)(2,1)S(1)}, u32[]{:S(2)}, u32[]{:S(2)}) collective-permute-start(bf16[32,15,128]{2,1,0:T(8,128)(2,1)S(1)} %get-tuple-element.11), channel_id=1, source_target_pairs={{0,8},{8,16},{16,24},{24,32},{32,40},{40,48},{48,56},{56,64},{64,7... | collective-permute-start | bytes 368648 | tf_op jit(solution)/shard_map/ppermute | solution.py:16
  124.6 1.3 collective-permute-done.8
  126.0 3.3 %collective-permute-done.7 = bf16[32,15,128]{2,1,0:T(8,128)(2,1)S(1)} collective-permute-done((bf16[32,15,128]{2,1,0:T(8,128)(2,1)S(1)}, bf16[32,15,128]{2,1,0:T(8,128)(2,1)S(1)}, u32[]{:S(2)}, u32[]{:S(2)}) %collective-permute-start.7) | collective-permute-done | bytes 122912 | tf_op jit(solution)/shard_map/ppermute | solution.py:16
  129.2 0.7 fusion.15
  130.0 1.5 copy.74
  131.5 1.0 reshape.82
  132.4 14.6 %all_to_all.76 = bf16[8,2,8192]{2,1,0:T(2,128)(2,1)S(1)} all-to-all(bf16[8,2,8192]{2,1,0:T(2,128)(2,1)S(1)} %reshape.82), channel_id=1, replica_groups=mesh['view'=4,'row'=32,'col'=8] {'col'}, dimensions={0} | all-to-all | bytes 524288 | tf_op jit(solution)/shard_map/all_to_all | solution.py:88
  147.0 0.5 reshape.83
  147.6 0.7 copy.76
  148.3 0.7 reshape.65
  149.0 0.5 convolution_convert_fusion.3
  149.5 3.0 %copy.80 = bf16[2,256,16,16]{3,2,0,1:T(8,128)(2,1)S(1)} copy(bf16[2,256,16,16]{1,3,2,0:T(8,128)(2,1)S(1)} %bitcast.180) | data formatting | bytes 524288 | tf_op jit(solution)/shard_map/reshape | solution.py:119
  152.5 2.2 %reshape.84 = bf16[8,2,8192]{2,1,0:T(2,128)(2,1)S(1)} reshape(bf16[256,2,16,16]{3,2,1,0:T(8,128)(2,1)S(1)} %bitcast.167) | data formatting | bytes 524288
  154.7 13.6 %all_to_all.77 = bf16[8,2,8192]{2,1,0:T(2,128)(2,1)S(1)} all-to-all(bf16[8,2,8192]{2,1,0:T(2,128)(2,1)S(1)} %reshape.84), channel_id=1, replica_groups=mesh['view'=4,'row'=32,'col'=8] {'col'}, dimensions={0} | all-to-all | bytes 524288 | tf_op jit(solution)/shard_map/all_to_all | solution.py:118
  168.3 1.4 reshape.85
  169.7 2.3 %copy.82 = bf16[2,32,16,8,16]{1,4,3,2,0:T(8,128)(2,1)S(1)} copy(bf16[2,32,16,8,16]{4,2,0,1,3:T(8,128)(2,1)S(1)} %bitcast.168) | data formatting | bytes 524288 | tf_op jit(solution)/shard_map/all_to_all | solution.py:118
  172.1 0.5 copy.83
  172.7 1.9 collective-permute-start.10
  174.6 6.1 %collective-permute-start.9 = (bf16[2,32,15,128]{3,2,0,1:T(8,128)(2,1)S(1)}, bf16[2,32,15,128]{3,2,0,1:T(8,128)(2,1)S(1)}, u32[]{:S(2)}, u32[]{:S(2)}) collective-permute-start(bf16[2,32,15,128]{3,2,0,1:T(8,128)(2,1)S(1)} %get-tuple-element.7), channel_id=1, source_target_pairs={{0,8},{8,16},{16,24},{24,32},{32,40},{40,48},{48,56},{56,64},{64,7... | collective-permute-start | bytes 737288 | tf_op jit(solution)/shard_map/ppermute | solution.py:16
  180.7 2.9 %collective-permute-done.10 = bf16[2,32,15,128]{3,2,0,1:T(8,128)(2,1)S(1)} collective-permute-done((bf16[2,32,15,128]{3,2,0,1:T(8,128)(2,1)S(1)}, bf16[2,32,15,128]{3,2,0,1:T(8,128)(2,1)S(1)}, u32[]{:S(2)}, u32[]{:S(2)}) %collective-permute-start.10) | collective-permute-done | bytes 245792 | tf_op jit(solution)/shard_map/ppermute | solution.py:17
  183.6 6.0 %collective-permute-done.9 = bf16[2,32,15,128]{3,2,0,1:T(8,128)(2,1)S(1)} collective-permute-done((bf16[2,32,15,128]{3,2,0,1:T(8,128)(2,1)S(1)}, bf16[2,32,15,128]{3,2,0,1:T(8,128)(2,1)S(1)}, u32[]{:S(2)}, u32[]{:S(2)}) %collective-permute-start.9) | collective-permute-done | bytes 245792 | tf_op jit(solution)/shard_map/ppermute | solution.py:16
  190.1 3.2 %collective-permute-start.11 = (f32[16,16,128]{2,1,0:T(8,128)S(1)}, f32[16,16,128]{2,1,0:T(8,128)S(1)}, u32[]{:S(2)}, u32[]{:S(2)}) collective-permute-start(f32[16,16,128]{2,1,0:T(8,128)S(1)} %constant_dynamic-slice_fusion), channel_id=1, source_target_pairs={{0,256},{256,0},{512,768},{768,512},{1,257},{257,1},{513,769},{769... | collective-permute-start | bytes 393224 | tf_op jit(solution)/shard_map/ppermute | solution.py:149
  193.3 1.0 collective-permute-done.11
  194.3 1.9 collective-permute-start.12
  196.2 8.6 %collective-permute-done.12 = f32[16,16,128]{2,1,0:T(8,128)S(1)} collective-permute-done((f32[16,16,128]{2,1,0:T(8,128)S(1)}, f32[16,16,128]{2,1,0:T(8,128)S(1)}, u32[]{:S(2)}, u32[]{:S(2)}) %collective-permute-start.12) | collective-permute-done | bytes 131104 | tf_op jit(solution)/shard_map/ppermute | solution.py:152
  204.8 4.2 %collective-permute-start.13 = (f32[16,16,128]{2,1,0:T(8,128)S(1)}, f32[16,16,128]{2,1,0:T(8,128)S(1)}, u32[]{:S(2)}, u32[]{:S(2)}) collective-permute-start(f32[16,16,128]{2,1,0:T(8,128)S(1)} %multiply_multiply_fusion), channel_id=1, source_target_pairs={{0,256},{256,0},{512,768},{768,512},{1,257},{257,1},{513,769},{769... | collective-permute-start | bytes 393224 | tf_op jit(solution)/shard_map/ppermute | solution.py:154
  209.0 1.0 collective-permute-done.13
  210.0 0.7 maximum_select_fusion
  (98 shorter events, 6.4 us)
Async XLA Ops:
  0.0 20.8 %copy-start = (f32[32,16,128]{2,1,0:T(8,128)S(1)}, f32[32,16,128]{2,1,0:T(8,128)}, u32[]{:S(2)}) copy-start(f32[32,16,128]{2,1,0:T(8,128)} %param.5) | copy-start | bytes 786436
  2.7 26.2 %copy-start.12 = (f32[2,31]{1,0:T(2,128)S(1)}, f32[2,31]{1,0:T(2,128)}, u32[]{:S(2)}) copy-start(f32[2,31]{1,0:T(2,128)} %param.8) | copy-start | bytes 748
  2.7 26.6 %copy-start.15 = (pred[62]{0:T(512)(128)(4,1)S(1)}, pred[62]{0:T(512)(128)(4,1)}, u32[]{:S(2)}) copy-start(pred[62]{0:T(512)(128)(4,1)} %constant.39.clone.1) | copy-start | bytes 190
  2.8 27.0 %copy-start.13 = (f32[2,31]{1,0:T(2,128)S(1)}, f32[2,31]{1,0:T(2,128)}, u32[]{:S(2)}) copy-start(f32[2,31]{1,0:T(2,128)} %param.7) | copy-start | bytes 748
  2.8 28.1 %copy-start.14 = (f32[2,121]{1,0:T(2,128)S(1)}, f32[2,121]{1,0:T(2,128)}, u32[]{:S(2)}) copy-start(f32[2,121]{1,0:T(2,128)} %param.9) | copy-start | bytes 2908
  4.4 33.2 %all-to-all-start = ((bf16[8,2,8192]{2,1,0:T(2,128)(2,1)}), bf16[8,2,8192]{2,1,0:T(2,128)(2,1)S(1)}, u32[]{:S(2)}, u32[]{:S(2)}) async-start(bf16[8,2,8192]{2,1,0:T(2,128)(2,1)} %reshape.76), calls=%async_computation | async-start | bytes 524288 | tf_op jit(solution)/shard_map/all_to_all | solution.py:88
  20.9 11.6 %collective-permute-start.1 = (bf16[32,15,128]{2,1,0:T(8,128)(2,1)S(1)}, bf16[32,15,128]{2,1,0:T(8,128)(2,1)S(1)}, u32[]{:S(2)}, u32[]{:S(2)}) collective-permute-start(bf16[32,15,128]{2,1,0:T(8,128)(2,1)S(1)} %get-tuple-element.14), channel_id=1, source_target_pairs={{8,0},{16,8},{24,16},{32,24},{40,32},{48,40},{56,48},{64,56},{72,6... | collective-permute-start | bytes 368648 | tf_op jit(solution)/shard_map/ppermute | solution.py:17
  23.8 9.9 %collective-permute-start = (bf16[32,15,128]{2,1,0:T(8,128)(2,1)S(1)}, bf16[32,15,128]{2,1,0:T(8,128)(2,1)S(1)}, u32[]{:S(2)}, u32[]{:S(2)}) collective-permute-start(bf16[32,15,128]{2,1,0:T(8,128)(2,1)S(1)} %get-tuple-element.13), channel_id=1, source_target_pairs={{0,8},{8,16},{16,24},{24,32},{32,40},{40,48},{48,56},{56,64},{64,7... | collective-permute-start | bytes 368648 | tf_op jit(solution)/shard_map/ppermute | solution.py:16
  30.5 3.3 %copy-start.6 = (bf16[1,128,128]{2,1,0:T(8,128)(2,1)}, bf16[1,128,128]{2,1,0:T(8,128)(2,1)S(1)}, u32[]{:S(2)}) copy-start(bf16[1,128,128]{2,1,0:T(8,128)(2,1)S(1)} %slice_bitcast_fusion.2) | copy-start | bytes 98308
  31.8 23.9 %copy-start.3 = (bf16[1,256,256]{2,1,0:T(8,128)(2,1)}, bf16[1,256,256]{2,1,0:T(8,128)(2,1)S(1)}, u32[]{:S(2)}) copy-start(bf16[1,256,256]{2,1,0:T(8,128)(2,1)S(1)} %slice_bitcast_fusion) | copy-start | bytes 393220
  32.5 1.3 copy-start.9
  37.6 16.2 %all-to-all-start.1 = ((bf16[8,2,8192]{2,1,0:T(2,128)(2,1)}), bf16[8,2,8192]{2,1,0:T(2,128)(2,1)S(1)}, u32[]{:S(2)}, u32[]{:S(2)}) async-start(bf16[8,2,8192]{2,1,0:T(2,128)(2,1)} %reshape.78), calls=%async_computation.1 | async-start | bytes 524288 | tf_op jit(solution)/shard_map/all_to_all | solution.py:88
  54.3 1.4 copy-start.1
  78.3 17.8 %copy-start.7 = (bf16[1,128,128]{2,1,0:T(8,128)(2,1)S(1)}, bf16[1,128,128]{2,1,0:T(8,128)(2,1)}, u32[]{:S(2)}) copy-start(bf16[1,128,128]{2,1,0:T(8,128)(2,1)} %copy-done.6) | copy-start | bytes 98308
  78.3 17.8 %copy-start.10 = (bf16[1,128,128]{2,1,0:T(8,128)(2,1)S(1)}, bf16[1,128,128]{2,1,0:T(8,128)(2,1)}, u32[]{:S(2)}) copy-start(bf16[1,128,128]{2,1,0:T(8,128)(2,1)} %copy-done.9) | copy-start | bytes 98308
  79.0 9.9 %collective-permute-start.3 = (bf16[2,32,15,128]{3,2,0,1:T(8,128)(2,1)S(1)}, bf16[2,32,15,128]{3,2,0,1:T(8,128)(2,1)S(1)}, u32[]{:S(2)}, u32[]{:S(2)}) collective-permute-start(bf16[2,32,15,128]{3,2,0,1:T(8,128)(2,1)S(1)} %get-tuple-element.10), channel_id=1, source_target_pairs={{8,0},{16,8},{24,16},{32,24},{40,32},{48,40},{56,48},{64,56},{72,6... | collective-permute-start | bytes 737288 | tf_op jit(solution)/shard_map/ppermute | solution.py:17
  81.6 14.5 %collective-permute-start.2 = (bf16[2,32,15,128]{3,2,0,1:T(8,128)(2,1)S(1)}, bf16[2,32,15,128]{3,2,0,1:T(8,128)(2,1)S(1)}, u32[]{:S(2)}, u32[]{:S(2)}) collective-permute-start(bf16[2,32,15,128]{3,2,0,1:T(8,128)(2,1)S(1)} %get-tuple-element.9), channel_id=1, source_target_pairs={{0,8},{8,16},{16,24},{24,32},{32,40},{40,48},{48,56},{56,64},{64,7... | collective-permute-start | bytes 737288 | tf_op jit(solution)/shard_map/ppermute | solution.py:16
  96.6 4.6 %collective-permute-start.4 = (f32[16,16,128]{2,1,0:T(8,128)S(1)}, f32[16,16,128]{2,1,0:T(8,128)S(1)}, u32[]{:S(2)}, u32[]{:S(2)}) collective-permute-start(f32[16,16,128]{2,1,0:T(8,128)S(1)} %constant_dynamic-slice_fusion.1), channel_id=1, source_target_pairs={{0,256},{256,0},{512,768},{768,512},{1,257},{257,1},{513,769},{769... | collective-permute-start | bytes 393224 | tf_op jit(solution)/shard_map/ppermute | solution.py:149
  101.2 10.6 %collective-permute-start.5 = (f32[16,16,128]{2,1,0:T(8,128)S(1)}, f32[16,16,128]{2,1,0:T(8,128)S(1)}, u32[]{:S(2)}, u32[]{:S(2)}) collective-permute-start(f32[16,16,128]{2,1,0:T(8,128)S(1)} %dynamic-slice_add_fusion.1), channel_id=1, source_target_pairs={{0,512},{256,768},{512,0},{768,256},{1,513},{257,769},{513,1},{769... | collective-permute-start | bytes 393224 | tf_op jit(solution)/shard_map/ppermute | solution.py:152
  111.9 4.2 %collective-permute-start.6 = (bf16[16,16,128]{2,1,0:T(8,128)(2,1)S(1)}, bf16[16,16,128]{2,1,0:T(8,128)(2,1)S(1)}, u32[]{:S(2)}, u32[]{:S(2)}) collective-permute-start(bf16[16,16,128]{2,1,0:T(8,128)(2,1)S(1)} %get-tuple-element.5), channel_id=1, source_target_pairs={{0,256},{256,0},{512,768},{768,512},{1,257},{257,1},{513,769},{769... | collective-permute-start | bytes 196616 | tf_op jit(solution)/shard_map/ppermute | solution.py:147
  116.2 9.8 %collective-permute-start.8 = (bf16[32,15,128]{2,1,0:T(8,128)(2,1)S(1)}, bf16[32,15,128]{2,1,0:T(8,128)(2,1)S(1)}, u32[]{:S(2)}, u32[]{:S(2)}) collective-permute-start(bf16[32,15,128]{2,1,0:T(8,128)(2,1)S(1)} %get-tuple-element.12), channel_id=1, source_target_pairs={{8,0},{16,8},{24,16},{32,24},{40,32},{48,40},{56,48},{64,56},{72,6... | collective-permute-start | bytes 368648 | tf_op jit(solution)/shard_map/ppermute | solution.py:17
  119.2 10.1 %collective-permute-start.7 = (bf16[32,15,128]{2,1,0:T(8,128)(2,1)S(1)}, bf16[32,15,128]{2,1,0:T(8,128)(2,1)S(1)}, u32[]{:S(2)}, u32[]{:S(2)}) collective-permute-start(bf16[32,15,128]{2,1,0:T(8,128)(2,1)S(1)} %get-tuple-element.11), channel_id=1, source_target_pairs={{0,8},{8,16},{16,24},{24,32},{32,40},{40,48},{48,56},{56,64},{64,7... | collective-permute-start | bytes 368648 | tf_op jit(solution)/shard_map/ppermute | solution.py:16
  147.5 1.4 copy-start.2
  147.6 1.4 copy-start.4
  147.6 1.4 copy-start.5
  172.0 17.6 %copy-start.8 = (bf16[1,128,128]{2,1,0:T(8,128)(2,1)S(1)}, bf16[1,128,128]{2,1,0:T(8,128)(2,1)}, u32[]{:S(2)}) copy-start(bf16[1,128,128]{2,1,0:T(8,128)(2,1)} %copy-done.6) | copy-start | bytes 98308
  172.0 17.6 %copy-start.11 = (bf16[1,128,128]{2,1,0:T(8,128)(2,1)S(1)}, bf16[1,128,128]{2,1,0:T(8,128)(2,1)}, u32[]{:S(2)}) copy-start(bf16[1,128,128]{2,1,0:T(8,128)(2,1)} %copy-done.9) | copy-start | bytes 98308
  172.7 10.9 %collective-permute-start.10 = (bf16[2,32,15,128]{3,2,0,1:T(8,128)(2,1)S(1)}, bf16[2,32,15,128]{3,2,0,1:T(8,128)(2,1)S(1)}, u32[]{:S(2)}, u32[]{:S(2)}) collective-permute-start(bf16[2,32,15,128]{3,2,0,1:T(8,128)(2,1)S(1)} %get-tuple-element.8), channel_id=1, source_target_pairs={{8,0},{16,8},{24,16},{32,24},{40,32},{48,40},{56,48},{64,56},{72,6... | collective-permute-start | bytes 737288 | tf_op jit(solution)/shard_map/ppermute | solution.py:17
  174.6 15.0 %collective-permute-start.9 = (bf16[2,32,15,128]{3,2,0,1:T(8,128)(2,1)S(1)}, bf16[2,32,15,128]{3,2,0,1:T(8,128)(2,1)S(1)}, u32[]{:S(2)}, u32[]{:S(2)}) collective-permute-start(bf16[2,32,15,128]{3,2,0,1:T(8,128)(2,1)S(1)} %get-tuple-element.7), channel_id=1, source_target_pairs={{0,8},{8,16},{16,24},{24,32},{32,40},{40,48},{48,56},{56,64},{64,7... | collective-permute-start | bytes 737288 | tf_op jit(solution)/shard_map/ppermute | solution.py:16
  190.1 4.2 %collective-permute-start.11 = (f32[16,16,128]{2,1,0:T(8,128)S(1)}, f32[16,16,128]{2,1,0:T(8,128)S(1)}, u32[]{:S(2)}, u32[]{:S(2)}) collective-permute-start(f32[16,16,128]{2,1,0:T(8,128)S(1)} %constant_dynamic-slice_fusion), channel_id=1, source_target_pairs={{0,256},{256,0},{512,768},{768,512},{1,257},{257,1},{513,769},{769... | collective-permute-start | bytes 393224 | tf_op jit(solution)/shard_map/ppermute | solution.py:149
  194.3 10.5 %collective-permute-start.12 = (f32[16,16,128]{2,1,0:T(8,128)S(1)}, f32[16,16,128]{2,1,0:T(8,128)S(1)}, u32[]{:S(2)}, u32[]{:S(2)}) collective-permute-start(f32[16,16,128]{2,1,0:T(8,128)S(1)} %dynamic-slice_add_fusion), channel_id=1, source_target_pairs={{0,512},{256,768},{512,0},{768,256},{1,513},{257,769},{513,1},{769... | collective-permute-start | bytes 393224 | tf_op jit(solution)/shard_map/ppermute | solution.py:152
  204.8 5.2 %collective-permute-start.13 = (f32[16,16,128]{2,1,0:T(8,128)S(1)}, f32[16,16,128]{2,1,0:T(8,128)S(1)}, u32[]{:S(2)}, u32[]{:S(2)}) collective-permute-start(f32[16,16,128]{2,1,0:T(8,128)S(1)} %multiply_multiply_fusion), channel_id=1, source_target_pairs={{0,256},{256,0},{512,768},{768,512},{1,257},{257,1},{513,769},{769... | collective-permute-start | bytes 393224 | tf_op jit(solution)/shard_map/ppermute | solution.py:154

commit v3 on v2

--- a/solution.py
+++ b/solution.py
@@ -84,13 +84,28 @@
     def framed_rows_of(field):
         return extended(field, (("row", 1),), radius_lat)
 
+    blocks = lax.axis_size("col")
+    pair = height // blocks
+    column_width = pair * across
+
     def to_columns(field):
-        return lax.all_to_all(field, "col", split_axis=3, concat_axis=1, tiled=True)
+        amount = field.shape[0]
+        chunks = field.reshape(amount, planes_local, blocks, pair, across)
+        chunks = chunks.transpose(2, 0, 1, 3, 4).reshape(blocks, amount * planes_local, column_width)
+        gathered = lax.all_to_all(chunks, "col", split_axis=0, concat_axis=0, tiled=True)
+        return gathered.reshape(blocks, amount, planes_local, column_width)
 
-    view_columns = to_columns(views)
-    column_shape = view_columns.shape
-    column_width = column_shape[2] * column_shape[3]
-    view_columns = view_columns.reshape(view_count, planes, column_width)
+    def to_slabs(columns):
+        amount = columns.shape[0]
+        chunks = columns.reshape(amount, blocks, planes_local, column_width).transpose(1, 0, 2, 3)
+        chunks = chunks.reshape(blocks, amount * planes_local, column_width)
+        spread = lax.all_to_all(chunks, "col", split_axis=0, concat_axis=0, tiled=True)
+        spread = spread.reshape(blocks, amount, planes_local, pair, across)
+        return spread.transpose(1, 2, 0, 3, 4).reshape(amount, planes_local, height, across)
+
+    view_columns = (
+        to_columns(views).transpose(1, 0, 2, 3).reshape(view_count, planes, column_width)
+    )
 
     def correct(coarse_framed, opening, amount):
         chosen = slice(opening, opening + amount)
@@ -106,18 +121,16 @@
         ).astype(jnp.bfloat16)
         columns = to_columns(lateral)
         blurred = jnp.einsum(
-            "vij,vjm->vim",
-            matrix_z,
-            columns.reshape(amount, planes, column_width),
+            "visz,svzm->vim",
+            matrix_z.reshape(amount, planes, blocks, planes_local),
+            columns,
             preferred_element_type=jnp.float32,
         )
         quotient = (view_columns[chosen] / blurred).astype(jnp.bfloat16)
         returned = jnp.einsum(
             "vij,vim->vjm", matrix_z, quotient, preferred_element_type=jnp.float32
         ).astype(jnp.bfloat16)
-        slab_back = lax.all_to_all(
-            returned.reshape(columns.shape), "col", split_axis=1, concat_axis=3, tiled=True
-        )
+        slab_back = to_slabs(returned)
         backward = jnp.einsum(
             "vij,vzjx->vzix", matrix_yback, framed(slab_back), preferred_element_type=jnp.float32
         ).astype(jnp.bfloat16)

time: 215 us -> 186 us (0.87)
  the two profiles are of different devices: /device:TPU:113 before, /device:TPU:9 now
where the time goes in v3:
time: 186 us
  starting transfers between devices  92.6 us (50%)
  waiting for transfers between devices  43.6 us (23%)
  blocking collectives  36.5 us (20%)
  local copies, waits for them, and re-layouts  6.45 us (3%)
  matrix products  3.34 us (2%)
  other arithmetic  2.51 us (1%)
    ppermute x4, starting transfers between devices, extended(): after = lax.ppermute(initial, axis, down)  25.9 us
    all_to_all x2, blocking collectives, to_slabs(): lax.all_to_all(chunks, 'col', split_axis=0, concat_axis=0, tiled=True)  23.8 us
    all_to_all x2, starting transfers between devices, to_columns(): lax.all_to_all(chunks, 'col', split_axis=0, concat_axis=0, tiled=True)  19.8 us
    ppermute x2, starting transfers between devices, on_device(): summed = paired + lax.ppermute(paired, 'view', to_far)  14.8 us
    ppermute x2, starting transfers between devices, on_device(): lax.ppermute(pick(accumulated, 1 - core_bit), 'view', to_core)  14.7 us
    all_to_all x2, waiting for transfers between devices, to_columns(): lax.all_to_all(chunks, 'col', split_axis=0, concat_axis=0, tiled=True)  13.9 us
    all_to_all x1, blocking collectives, to_columns(): lax.all_to_all(chunks, 'col', split_axis=0, concat_axis=0, tiled=True)  12.7 us
    ppermute x4, starting transfers between devices, extended(): before = lax.ppermute(last, axis, up)  12 us
  transfers between devices with their start and end apart: 16, of which 14 were waited for; matrix products, arithmetic and copies ran while one was open for 4% of the time, Pallas kernels for 0%

profile of v3, /device:TPU:9, one launch (start us, length us, event | category | flops | bytes accessed | tf_op | source)
XLA Modules:
  0.0 185.7 jit_solution(3231699504797211543)
XLA Ops:
  0.0 1.0 convert_element_type.82
  1.1 3.3 %collective-permute-start = (bf16[32,15,128]{2,1,0:T(8,128)(2,1)S(1)}, bf16[32,15,128]{2,1,0:T(8,128)(2,1)S(1)}, u32[]{:S(2)}, u32[]{:S(2)}) collective-permute-start(bf16[32,15,128]{2,1,0:T(8,128)(2,1)S(1)} %get-tuple-element.13), channel_id=1, source_target_pairs={{0,8},{8,16},{16,24},{24,32},{32,40},{40,48},{48,56},{56,64},{64,7... | collective-permute-start | bytes 368648 | tf_op jit(solution)/shard_map/ppermute | solution.py:16
  4.4 5.9 %collective-permute-start.1 = (bf16[32,15,128]{2,1,0:T(8,128)(2,1)S(1)}, bf16[32,15,128]{2,1,0:T(8,128)(2,1)S(1)}, u32[]{:S(2)}, u32[]{:S(2)}) collective-permute-start(bf16[32,15,128]{2,1,0:T(8,128)(2,1)S(1)} %get-tuple-element.14), channel_id=1, source_target_pairs={{8,0},{16,8},{24,16},{32,24},{40,32},{48,40},{56,48},{64,56},{72,6... | collective-permute-start | bytes 368648 | tf_op jit(solution)/shard_map/ppermute | solution.py:17
  10.3 0.2 copy.66
  10.6 0.9 reshape.98
  11.4 16.4 %all-to-all-start = ((bf16[8,64,256]{2,1,0:T(8,128)(2,1)}), bf16[8,64,256]{2,1,0:T(8,128)(2,1)S(1)}, u32[]{:S(2)}, u32[]{:S(2)}) async-start(bf16[8,64,256]{2,1,0:T(8,128)(2,1)} %reshape.98), calls=%async_computation | async-start | bytes 524288 | tf_op jit(solution)/shard_map/all_to_all | solution.py:95
  27.8 0.1 reduce_sum.29
  28.2 0.1 reduce_sum.28
  28.6 0.3 reshape.100
  29.1 0.3 reshape.99
  29.4 0.1 reduce_sum.27
  29.9 0.1 reshape.101
  30.1 0.1 reshape.102
  30.2 0.1 copy.55
  30.3 0.4 reshape.95
  30.8 0.1 copy.53
  30.9 0.7 fusion.5
  31.6 0.2 reshape.130
  31.8 0.8 copy.51
  32.6 5.4 %all-to-all-done = bf16[8,64,256]{2,1,0:T(8,128)(2,1)S(1)} async-done(((bf16[8,64,256]{2,1,0:T(8,128)(2,1)}), bf16[8,64,256]{2,1,0:T(8,128)(2,1)S(1)}, u32[]{:S(2)}, u32[]{:S(2)}) %all-to-all-start) | async-done | bytes 262176 | tf_op jit(solution)/shard_map/all_to_all | solution.py:95
  38.0 3.4 %all-to-all-start.1 = ((bf16[8,64,256]{2,1,0:T(8,128)(2,1)}), bf16[8,64,256]{2,1,0:T(8,128)(2,1)S(1)}, u32[]{:S(2)}, u32[]{:S(2)}) async-start(bf16[8,64,256]{2,1,0:T(8,128)(2,1)} %copy.51), calls=%async_computation.1 | async-start | bytes 524288 | tf_op jit(solution)/shard_map/all_to_all | solution.py:95
  41.5 0.1 copy.56
  41.6 0.4 reshape.96
  42.2 8.5 %all-to-all-done.1 = bf16[8,64,256]{2,1,0:T(8,128)(2,1)S(1)} async-done(((bf16[8,64,256]{2,1,0:T(8,128)(2,1)}), bf16[8,64,256]{2,1,0:T(8,128)(2,1)S(1)}, u32[]{:S(2)}, u32[]{:S(2)}) %all-to-all-start.1) | async-done | bytes 262176 | tf_op jit(solution)/shard_map/all_to_all | solution.py:95
  50.7 0.5 convolution_convert_fusion.5
  51.3 11.8 %all_to_all.25 = bf16[8,64,256]{2,1,0:T(8,128)(2,1)S(1)} all-to-all(bf16[8,64,256]{2,1,0:T(8,128)(2,1)S(1)} %bitcast.171), channel_id=1, replica_groups=mesh['view'=4,'row'=32,'col'=8] {'col'}, dimensions={0} | all-to-all | bytes 524288 | tf_op jit(solution)/shard_map/all_to_all | solution.py:102
  63.2 0.1 copy.35
  63.3 0.1 fusion.76
  63.4 1.9 %collective-permute-start.2 = (bf16[2,32,15,128]{3,2,0,1:T(8,128)(2,1)S(1)}, bf16[2,32,15,128]{3,2,0,1:T(8,128)(2,1)S(1)}, u32[]{:S(2)}, u32[]{:S(2)}) collective-permute-start(bf16[2,32,15,128]{3,2,0,1:T(8,128)(2,1)S(1)} %get-tuple-element.9), channel_id=1, source_target_pairs={{0,8},{8,16},{16,24},{24,32},{32,40},{40,48},{48,56},{56,64},{64,7... | collective-permute-start | bytes 737288 | tf_op jit(solution)/shard_map/ppermute | solution.py:16
  65.4 7.3 %collective-permute-start.3 = (bf16[2,32,15,128]{3,2,0,1:T(8,128)(2,1)S(1)}, bf16[2,32,15,128]{3,2,0,1:T(8,128)(2,1)S(1)}, u32[]{:S(2)}, u32[]{:S(2)}) collective-permute-start(bf16[2,32,15,128]{3,2,0,1:T(8,128)(2,1)S(1)} %get-tuple-element.10), channel_id=1, source_target_pairs={{8,0},{16,8},{24,16},{32,24},{40,32},{48,40},{56,48},{64,56},{72,6... | collective-permute-start | bytes 737288 | tf_op jit(solution)/shard_map/ppermute | solution.py:17
  72.8 0.1 reshape.110
  73.0 0.1 reshape.111
  73.1 1.5 collective-permute-done.2
  74.7 1.3 collective-permute-done.3
  76.0 0.5 fusion.8
  76.5 7.9 %collective-permute-start.4 = (f32[16,16,128]{2,1,0:T(8,128)S(1)}, f32[16,16,128]{2,1,0:T(8,128)S(1)}, u32[]{:S(2)}, u32[]{:S(2)}) collective-permute-start(f32[16,16,128]{2,1,0:T(8,128)S(1)} %constant_dynamic-slice_fusion.1), channel_id=1, source_target_pairs={{0,256},{256,0},{512,768},{768,512},{1,257},{257,1},{513,769},{769... | collective-permute-start | bytes 393224 | tf_op jit(solution)/shard_map/ppermute | solution.py:162
  84.4 1.0 collective-permute-done.4
  85.4 7.9 %collective-permute-start.5 = (f32[16,16,128]{2,1,0:T(8,128)S(1)}, f32[16,16,128]{2,1,0:T(8,128)S(1)}, u32[]{:S(2)}, u32[]{:S(2)}) collective-permute-start(f32[16,16,128]{2,1,0:T(8,128)S(1)} %dynamic-slice_add_fusion.1), channel_id=1, source_target_pairs={{0,512},{256,768},{512,0},{768,256},{1,513},{257,769},{513,1},{769... | collective-permute-start | bytes 393224 | tf_op jit(solution)/shard_map/ppermute | solution.py:165
  93.3 3.5 %collective-permute-done.5 = f32[16,16,128]{2,1,0:T(8,128)S(1)} collective-permute-done((f32[16,16,128]{2,1,0:T(8,128)S(1)}, f32[16,16,128]{2,1,0:T(8,128)S(1)}, u32[]{:S(2)}, u32[]{:S(2)}) %collective-permute-start.5) | collective-permute-done | bytes 131104 | tf_op jit(solution)/shard_map/ppermute | solution.py:165
  96.9 2.9 %collective-permute-start.6 = (bf16[16,16,128]{2,1,0:T(8,128)(2,1)S(1)}, bf16[16,16,128]{2,1,0:T(8,128)(2,1)S(1)}, u32[]{:S(2)}, u32[]{:S(2)}) collective-permute-start(bf16[16,16,128]{2,1,0:T(8,128)(2,1)S(1)} %get-tuple-element.5), channel_id=1, source_target_pairs={{0,256},{256,0},{512,768},{768,512},{1,257},{257,1},{513,769},{769... | collective-permute-start | bytes 196616 | tf_op jit(solution)/shard_map/ppermute | solution.py:160
  99.8 0.9 collective-permute-done.6
  100.8 4.7 %collective-permute-start.7 = (bf16[32,15,128]{2,1,0:T(8,128)(2,1)S(1)}, bf16[32,15,128]{2,1,0:T(8,128)(2,1)S(1)}, u32[]{:S(2)}, u32[]{:S(2)}) collective-permute-start(bf16[32,15,128]{2,1,0:T(8,128)(2,1)S(1)} %get-tuple-element.11), channel_id=1, source_target_pairs={{0,8},{8,16},{16,24},{24,32},{32,40},{40,48},{48,56},{56,64},{64,7... | collective-permute-start | bytes 368648 | tf_op jit(solution)/shard_map/ppermute | solution.py:16
  105.4 5.9 %collective-permute-start.8 = (bf16[32,15,128]{2,1,0:T(8,128)(2,1)S(1)}, bf16[32,15,128]{2,1,0:T(8,128)(2,1)S(1)}, u32[]{:S(2)}, u32[]{:S(2)}) collective-permute-start(bf16[32,15,128]{2,1,0:T(8,128)(2,1)S(1)} %get-tuple-element.12), channel_id=1, source_target_pairs={{8,0},{16,8},{24,16},{32,24},{40,32},{48,40},{56,48},{64,56},{72,6... | collective-permute-start | bytes 368648 | tf_op jit(solution)/shard_map/ppermute | solution.py:17
  111.3 1.6 collective-permute-done.7
  113.0 2.0 %collective-permute-done.8 = bf16[32,15,128]{2,1,0:T(8,128)(2,1)S(1)} collective-permute-done((bf16[32,15,128]{2,1,0:T(8,128)(2,1)S(1)}, bf16[32,15,128]{2,1,0:T(8,128)(2,1)S(1)}, u32[]{:S(2)}, u32[]{:S(2)}) %collective-permute-start.8) | collective-permute-done | bytes 122912 | tf_op jit(solution)/shard_map/ppermute | solution.py:17
  114.9 0.7 fusion.4
  115.7 0.2 reshape.131
  115.9 12.7 %all_to_all.26 = bf16[8,64,256]{2,1,0:T(8,128)(2,1)S(1)} all-to-all(bf16[8,64,256]{2,1,0:T(8,128)(2,1)S(1)} %copy.52), channel_id=1, replica_groups=mesh['view'=4,'row'=32,'col'=8] {'col'}, dimensions={0} | all-to-all | bytes 524288 | tf_op jit(solution)/shard_map/all_to_all | solution.py:95
  128.6 0.5 convolution_convert_fusion.3
  129.1 11.9 %all_to_all.27 = bf16[8,64,256]{2,1,0:T(8,128)(2,1)S(1)} all-to-all(bf16[8,64,256]{2,1,0:T(8,128)(2,1)S(1)} %bitcast.173), channel_id=1, replica_groups=mesh['view'=4,'row'=32,'col'=8] {'col'}, dimensions={0} | all-to-all | bytes 524288 | tf_op jit(solution)/shard_map/all_to_all | solution.py:102
  141.2 0.1 copy.42
  141.3 0.1 fusion.75
  141.4 6.9 %collective-permute-start.10 = (bf16[2,32,15,128]{3,2,0,1:T(8,128)(2,1)S(1)}, bf16[2,32,15,128]{3,2,0,1:T(8,128)(2,1)S(1)}, u32[]{:S(2)}, u32[]{:S(2)}) collective-permute-start(bf16[2,32,15,128]{3,2,0,1:T(8,128)(2,1)S(1)} %get-tuple-element.8), channel_id=1, source_target_pairs={{8,0},{16,8},{24,16},{32,24},{40,32},{48,40},{56,48},{64,56},{72,6... | collective-permute-start | bytes 737288 | tf_op jit(solution)/shard_map/ppermute | solution.py:17
  148.3 2.1 %collective-permute-start.9 = (bf16[2,32,15,128]{3,2,0,1:T(8,128)(2,1)S(1)}, bf16[2,32,15,128]{3,2,0,1:T(8,128)(2,1)S(1)}, u32[]{:S(2)}, u32[]{:S(2)}) collective-permute-start(bf16[2,32,15,128]{3,2,0,1:T(8,128)(2,1)S(1)} %get-tuple-element.7), channel_id=1, source_target_pairs={{0,8},{8,16},{16,24},{24,32},{32,40},{40,48},{48,56},{56,64},{64,7... | collective-permute-start | bytes 737288 | tf_op jit(solution)/shard_map/ppermute | solution.py:16
  150.4 3.1 %collective-permute-done.10 = bf16[2,32,15,128]{3,2,0,1:T(8,128)(2,1)S(1)} collective-permute-done((bf16[2,32,15,128]{3,2,0,1:T(8,128)(2,1)S(1)}, bf16[2,32,15,128]{3,2,0,1:T(8,128)(2,1)S(1)}, u32[]{:S(2)}, u32[]{:S(2)}) %collective-permute-start.10) | collective-permute-done | bytes 245792 | tf_op jit(solution)/shard_map/ppermute | solution.py:17
  153.5 5.8 %collective-permute-done.9 = bf16[2,32,15,128]{3,2,0,1:T(8,128)(2,1)S(1)} collective-permute-done((bf16[2,32,15,128]{3,2,0,1:T(8,128)(2,1)S(1)}, bf16[2,32,15,128]{3,2,0,1:T(8,128)(2,1)S(1)}, u32[]{:S(2)}, u32[]{:S(2)}) %collective-permute-start.9) | collective-permute-done | bytes 245792 | tf_op jit(solution)/shard_map/ppermute | solution.py:16
  159.3 0.5 fusion.11
  159.8 6.8 %collective-permute-start.11 = (f32[16,16,128]{2,1,0:T(8,128)S(1)}, f32[16,16,128]{2,1,0:T(8,128)S(1)}, u32[]{:S(2)}, u32[]{:S(2)}) collective-permute-start(f32[16,16,128]{2,1,0:T(8,128)S(1)} %constant_dynamic-slice_fusion), channel_id=1, source_target_pairs={{0,256},{256,0},{512,768},{768,512},{1,257},{257,1},{513,769},{769... | collective-permute-start | bytes 393224 | tf_op jit(solution)/shard_map/ppermute | solution.py:162
  166.7 1.0 collective-permute-done.11
  167.6 6.9 %collective-permute-start.12 = (f32[16,16,128]{2,1,0:T(8,128)S(1)}, f32[16,16,128]{2,1,0:T(8,128)S(1)}, u32[]{:S(2)}, u32[]{:S(2)}) collective-permute-start(f32[16,16,128]{2,1,0:T(8,128)S(1)} %dynamic-slice_add_fusion), channel_id=1, source_target_pairs={{0,512},{256,768},{512,0},{768,256},{1,513},{257,769},{513,1},{769... | collective-permute-start | bytes 393224 | tf_op jit(solution)/shard_map/ppermute | solution.py:165
  174.5 7.0 %collective-permute-done.12 = f32[16,16,128]{2,1,0:T(8,128)S(1)} collective-permute-done((f32[16,16,128]{2,1,0:T(8,128)S(1)}, f32[16,16,128]{2,1,0:T(8,128)S(1)}, u32[]{:S(2)}, u32[]{:S(2)}) %collective-permute-start.12) | collective-permute-done | bytes 131104 | tf_op jit(solution)/shard_map/ppermute | solution.py:165
  181.6 2.4 %collective-permute-start.13 = (f32[16,16,128]{2,1,0:T(8,128)S(1)}, f32[16,16,128]{2,1,0:T(8,128)S(1)}, u32[]{:S(2)}, u32[]{:S(2)}) collective-permute-start(f32[16,16,128]{2,1,0:T(8,128)S(1)} %multiply_multiply_fusion), channel_id=1, source_target_pairs={{0,256},{256,0},{512,768},{768,512},{1,257},{257,1},{513,769},{769... | collective-permute-start | bytes 393224 | tf_op jit(solution)/shard_map/ppermute | solution.py:167
  184.0 1.0 collective-permute-done.13
  184.9 0.7 maximum_select_fusion
  (68 shorter events, 2.0 us)
Async XLA Ops:
  0.0 10.3 %copy-start.1 = (bf16[2,32,16,128]{3,2,1,0:T(8,128)(2,1)S(1)}, bf16[2,32,16,128]{3,2,1,0:T(8,128)(2,1)}, u32[]{:S(2)}) copy-start(bf16[2,32,16,128]{3,2,1,0:T(8,128)(2,1)} %param.6) | copy-start | bytes 786436
  1.1 29.8 %collective-permute-start = (bf16[32,15,128]{2,1,0:T(8,128)(2,1)S(1)}, bf16[32,15,128]{2,1,0:T(8,128)(2,1)S(1)}, u32[]{:S(2)}, u32[]{:S(2)}) collective-permute-start(bf16[32,15,128]{2,1,0:T(8,128)(2,1)S(1)} %get-tuple-element.13), channel_id=1, source_target_pairs={{0,8},{8,16},{16,24},{24,32},{32,40},{40,48},{48,56},{56,64},{64,7... | collective-permute-start | bytes 368648 | tf_op jit(solution)/shard_map/ppermute | solution.py:16
  4.4 26.5 %collective-permute-start.1 = (bf16[32,15,128]{2,1,0:T(8,128)(2,1)S(1)}, bf16[32,15,128]{2,1,0:T(8,128)(2,1)S(1)}, u32[]{:S(2)}, u32[]{:S(2)}) collective-permute-start(bf16[32,15,128]{2,1,0:T(8,128)(2,1)S(1)} %get-tuple-element.14), channel_id=1, source_target_pairs={{8,0},{16,8},{24,16},{32,24},{40,32},{48,40},{56,48},{64,56},{72,6... | collective-permute-start | bytes 368648 | tf_op jit(solution)/shard_map/ppermute | solution.py:17
  10.5 17.3 %copy-start.2 = (f32[2,31]{1,0:T(2,128)S(1)}, f32[2,31]{1,0:T(2,128)}, u32[]{:S(2)}) copy-start(f32[2,31]{1,0:T(2,128)} %param.8) | copy-start | bytes 748
  10.5 17.7 %copy-start.3 = (f32[2,31]{1,0:T(2,128)S(1)}, f32[2,31]{1,0:T(2,128)}, u32[]{:S(2)}) copy-start(f32[2,31]{1,0:T(2,128)} %param.7) | copy-start | bytes 748
  11.4 26.6 %all-to-all-start = ((bf16[8,64,256]{2,1,0:T(8,128)(2,1)}), bf16[8,64,256]{2,1,0:T(8,128)(2,1)S(1)}, u32[]{:S(2)}, u32[]{:S(2)}) async-start(bf16[8,64,256]{2,1,0:T(8,128)(2,1)} %reshape.98), calls=%async_computation | async-start | bytes 524288 | tf_op jit(solution)/shard_map/all_to_all | solution.py:95
  27.8 1.6 copy-start.4
  28.6 1.2 copy-start.5
  38.0 12.7 %all-to-all-start.1 = ((bf16[8,64,256]{2,1,0:T(8,128)(2,1)}), bf16[8,64,256]{2,1,0:T(8,128)(2,1)S(1)}, u32[]{:S(2)}, u32[]{:S(2)}) async-start(bf16[8,64,256]{2,1,0:T(8,128)(2,1)} %copy.51), calls=%async_computation.1 | async-start | bytes 524288 | tf_op jit(solution)/shard_map/all_to_all | solution.py:95
  63.4 11.2 %collective-permute-start.2 = (bf16[2,32,15,128]{3,2,0,1:T(8,128)(2,1)S(1)}, bf16[2,32,15,128]{3,2,0,1:T(8,128)(2,1)S(1)}, u32[]{:S(2)}, u32[]{:S(2)}) collective-permute-start(bf16[2,32,15,128]{3,2,0,1:T(8,128)(2,1)S(1)} %get-tuple-element.9), channel_id=1, source_target_pairs={{0,8},{8,16},{16,24},{24,32},{32,40},{40,48},{48,56},{56,64},{64,7... | collective-permute-start | bytes 737288 | tf_op jit(solution)/shard_map/ppermute | solution.py:16
  65.4 10.6 %collective-permute-start.3 = (bf16[2,32,15,128]{3,2,0,1:T(8,128)(2,1)S(1)}, bf16[2,32,15,128]{3,2,0,1:T(8,128)(2,1)S(1)}, u32[]{:S(2)}, u32[]{:S(2)}) collective-permute-start(bf16[2,32,15,128]{3,2,0,1:T(8,128)(2,1)S(1)} %get-tuple-element.10), channel_id=1, source_target_pairs={{8,0},{16,8},{24,16},{32,24},{40,32},{48,40},{56,48},{64,56},{72,6... | collective-permute-start | bytes 737288 | tf_op jit(solution)/shard_map/ppermute | solution.py:17
  76.4 20.4 %copy-start = (f32[32,16,128]{2,1,0:T(8,128)S(1)}, f32[32,16,128]{2,1,0:T(8,128)}, u32[]{:S(2)}) copy-start(f32[32,16,128]{2,1,0:T(8,128)} %param.5) | copy-start | bytes 786436
  76.5 8.9 %collective-permute-start.4 = (f32[16,16,128]{2,1,0:T(8,128)S(1)}, f32[16,16,128]{2,1,0:T(8,128)S(1)}, u32[]{:S(2)}, u32[]{:S(2)}) collective-permute-start(f32[16,16,128]{2,1,0:T(8,128)S(1)} %constant_dynamic-slice_fusion.1), channel_id=1, source_target_pairs={{0,256},{256,0},{512,768},{768,512},{1,257},{257,1},{513,769},{769... | collective-permute-start | bytes 393224 | tf_op jit(solution)/shard_map/ppermute | solution.py:162
  85.4 11.5 %collective-permute-start.5 = (f32[16,16,128]{2,1,0:T(8,128)S(1)}, f32[16,16,128]{2,1,0:T(8,128)S(1)}, u32[]{:S(2)}, u32[]{:S(2)}) collective-permute-start(f32[16,16,128]{2,1,0:T(8,128)S(1)} %dynamic-slice_add_fusion.1), channel_id=1, source_target_pairs={{0,512},{256,768},{512,0},{768,256},{1,513},{257,769},{513,1},{769... | collective-permute-start | bytes 393224 | tf_op jit(solution)/shard_map/ppermute | solution.py:165
  96.9 3.8 %collective-permute-start.6 = (bf16[16,16,128]{2,1,0:T(8,128)(2,1)S(1)}, bf16[16,16,128]{2,1,0:T(8,128)(2,1)S(1)}, u32[]{:S(2)}, u32[]{:S(2)}) collective-permute-start(bf16[16,16,128]{2,1,0:T(8,128)(2,1)S(1)} %get-tuple-element.5), channel_id=1, source_target_pairs={{0,256},{256,0},{512,768},{768,512},{1,257},{257,1},{513,769},{769... | collective-permute-start | bytes 196616 | tf_op jit(solution)/shard_map/ppermute | solution.py:160
  100.8 12.2 %collective-permute-start.7 = (bf16[32,15,128]{2,1,0:T(8,128)(2,1)S(1)}, bf16[32,15,128]{2,1,0:T(8,128)(2,1)S(1)}, u32[]{:S(2)}, u32[]{:S(2)}) collective-permute-start(bf16[32,15,128]{2,1,0:T(8,128)(2,1)S(1)} %get-tuple-element.11), channel_id=1, source_target_pairs={{0,8},{8,16},{16,24},{24,32},{32,40},{40,48},{48,56},{56,64},{64,7... | collective-permute-start | bytes 368648 | tf_op jit(solution)/shard_map/ppermute | solution.py:16
  105.4 9.5 %collective-permute-start.8 = (bf16[32,15,128]{2,1,0:T(8,128)(2,1)S(1)}, bf16[32,15,128]{2,1,0:T(8,128)(2,1)S(1)}, u32[]{:S(2)}, u32[]{:S(2)}) collective-permute-start(bf16[32,15,128]{2,1,0:T(8,128)(2,1)S(1)} %get-tuple-element.12), channel_id=1, source_target_pairs={{8,0},{16,8},{24,16},{32,24},{40,32},{48,40},{56,48},{64,56},{72,6... | collective-permute-start | bytes 368648 | tf_op jit(solution)/shard_map/ppermute | solution.py:17
  141.4 12.1 %collective-permute-start.10 = (bf16[2,32,15,128]{3,2,0,1:T(8,128)(2,1)S(1)}, bf16[2,32,15,128]{3,2,0,1:T(8,128)(2,1)S(1)}, u32[]{:S(2)}, u32[]{:S(2)}) collective-permute-start(bf16[2,32,15,128]{3,2,0,1:T(8,128)(2,1)S(1)} %get-tuple-element.8), channel_id=1, source_target_pairs={{8,0},{16,8},{24,16},{32,24},{40,32},{48,40},{56,48},{64,56},{72,6... | collective-permute-start | bytes 737288 | tf_op jit(solution)/shard_map/ppermute | solution.py:17
  148.3 11.0 %collective-permute-start.9 = (bf16[2,32,15,128]{3,2,0,1:T(8,128)(2,1)S(1)}, bf16[2,32,15,128]{3,2,0,1:T(8,128)(2,1)S(1)}, u32[]{:S(2)}, u32[]{:S(2)}) collective-permute-start(bf16[2,32,15,128]{3,2,0,1:T(8,128)(2,1)S(1)} %get-tuple-element.7), channel_id=1, source_target_pairs={{0,8},{8,16},{16,24},{24,32},{32,40},{40,48},{48,56},{56,64},{64,7... | collective-permute-start | bytes 737288 | tf_op jit(solution)/shard_map/ppermute | solution.py:16
  159.8 7.8 %collective-permute-start.11 = (f32[16,16,128]{2,1,0:T(8,128)S(1)}, f32[16,16,128]{2,1,0:T(8,128)S(1)}, u32[]{:S(2)}, u32[]{:S(2)}) collective-permute-start(f32[16,16,128]{2,1,0:T(8,128)S(1)} %constant_dynamic-slice_fusion), channel_id=1, source_target_pairs={{0,256},{256,0},{512,768},{768,512},{1,257},{257,1},{513,769},{769... | collective-permute-start | bytes 393224 | tf_op jit(solution)/shard_map/ppermute | solution.py:162
  167.6 13.9 %collective-permute-start.12 = (f32[16,16,128]{2,1,0:T(8,128)S(1)}, f32[16,16,128]{2,1,0:T(8,128)S(1)}, u32[]{:S(2)}, u32[]{:S(2)}) collective-permute-start(f32[16,16,128]{2,1,0:T(8,128)S(1)} %dynamic-slice_add_fusion), channel_id=1, source_target_pairs={{0,512},{256,768},{512,0},{768,256},{1,513},{257,769},{513,1},{769... | collective-permute-start | bytes 393224 | tf_op jit(solution)/shard_map/ppermute | solution.py:165
  181.6 3.4 %collective-permute-start.13 = (f32[16,16,128]{2,1,0:T(8,128)S(1)}, f32[16,16,128]{2,1,0:T(8,128)S(1)}, u32[]{:S(2)}, u32[]{:S(2)}) collective-permute-start(f32[16,16,128]{2,1,0:T(8,128)S(1)} %multiply_multiply_fusion), channel_id=1, source_target_pairs={{0,256},{256,0},{512,768},{768,512},{1,257},{257,1},{513,769},{769... | collective-permute-start | bytes 393224 | tf_op jit(solution)/shard_map/ppermute | solution.py:167

commit v4 on v3

--- a/solution.py
+++ b/solution.py
@@ -103,11 +103,11 @@
         spread = spread.reshape(blocks, amount, planes_local, pair, across)
         return spread.transpose(1, 2, 0, 3, 4).reshape(amount, planes_local, height, across)
 
-    view_columns = (
-        to_columns(views).transpose(1, 0, 2, 3).reshape(view_count, planes, column_width)
-    )
+    def as_planes(columns):
+        amount = columns.shape[1]
+        return columns.transpose(1, 0, 2, 3).reshape(amount, planes, column_width)
 
-    def correct(coarse_framed, opening, amount):
+    def correct(coarse_framed, opening, amount, view_columns):
         chosen = slice(opening, opening + amount)
         matrix_x = bands_x[chosen]
         matrix_y = bands_y[chosen]
@@ -119,14 +119,18 @@
         lateral = jnp.einsum(
             "vij,vzjx->vzix", matrix_y, smeared, preferred_element_type=jnp.float32
         ).astype(jnp.bfloat16)
-        columns = to_columns(lateral)
+        if view_columns is None:
+            both = to_columns(jnp.concatenate([lateral, views[chosen]], axis=0))
+            columns, view_columns = both[:, :amount], as_planes(both[:, amount:])
+        else:
+            columns = to_columns(lateral)
         blurred = jnp.einsum(
             "visz,svzm->vim",
             matrix_z.reshape(amount, planes, blocks, planes_local),
             columns,
             preferred_element_type=jnp.float32,
         )
-        quotient = (view_columns[chosen] / blurred).astype(jnp.bfloat16)
+        quotient = (view_columns / blurred).astype(jnp.bfloat16)
         returned = jnp.einsum(
             "vij,vim->vjm", matrix_z, quotient, preferred_element_type=jnp.float32
         ).astype(jnp.bfloat16)
@@ -134,7 +138,10 @@
         backward = jnp.einsum(
             "vij,vzjx->vzix", matrix_yback, framed(slab_back), preferred_element_type=jnp.float32
         ).astype(jnp.bfloat16)
-        return jnp.einsum("vzyi,vij->zyj", backward, matrix_x, preferred_element_type=jnp.float32)
+        corrected = jnp.einsum(
+            "vzyi,vij->zyj", backward, matrix_x, preferred_element_type=jnp.float32
+        )
+        return corrected, view_columns
 
     half = planes_local // 2
     core_bit = lax.axis_index("view") % 2
@@ -154,11 +161,12 @@
 
     restored_mine = pick(estimate, core_bit)
     coarse = estimate.astype(jnp.bfloat16)
+    view_columns = None
     for iteration in range(ITERS):
         if iteration:
             coarse_mine = restored_mine.astype(jnp.bfloat16)
             coarse = joined(coarse_mine, lax.ppermute(coarse_mine, "view", to_core))
-        accumulated = correct(framed_rows_of(coarse), 0, view_count)
+        accumulated, view_columns = correct(framed_rows_of(coarse), 0, view_count, view_columns)
         paired = pick(accumulated, core_bit) + lax.ppermute(
             pick(accumulated, 1 - core_bit), "view", to_core
         )

time: 186 us -> 186 us (level)
  the two profiles are of different devices: /device:TPU:9 before, /device:TPU:113 now
where the time goes in v4:
time: 186 us; the launch traced here: 184 us
  starting transfers between devices  74 us (40%)
  waiting for transfers between devices  60.6 us (33%)
  blocking collectives  36.9 us (20%)
  local copies, waits for them, and re-layouts  5.86 us (3%)
  matrix products  3.35 us (2%)
  other arithmetic  2.55 us (1%)
    ppermute x4, starting transfers between devices, extended(): before = lax.ppermute(last, axis, up)  27.8 us
    all_to_all x2, blocking collectives, to_slabs(): lax.all_to_all(chunks, 'col', split_axis=0, concat_axis=0, tiled=True)  24.3 us
    ppermute x4, waiting for transfers between devices, extended(): after = lax.ppermute(initial, axis, down)  19.6 us
    ppermute x2, waiting for transfers between devices, on_device(): summed = paired + lax.ppermute(paired, 'view', to_far)  16.8 us
    all_to_all x1, starting transfers between devices, to_columns(): lax.all_to_all(chunks, 'col', split_axis=0, concat_axis=0, tiled=True)  16.4 us
    all_to_all x1, waiting for transfers between devices, to_columns(): lax.all_to_all(chunks, 'col', split_axis=0, concat_axis=0, tiled=True)  13.7 us
    all_to_all x1, blocking collectives, to_columns(): lax.all_to_all(chunks, 'col', split_axis=0, concat_axis=0, tiled=True)  12.6 us
    ppermute x2, starting transfers between devices, on_device(): lax.ppermute(pick(accumulated, 1 - core_bit), 'view', to_core)  11.7 us
  transfers between devices with their start and end apart: 15, of which 14 were waited for; matrix products, arithmetic and copies ran while one was open for 2% of the time, Pallas kernels for 0%

profile of v4, /device:TPU:113, one launch (start us, length us, event | category | flops | bytes accessed | tf_op | source)
XLA Modules:
  0.0 183.8 jit_solution(12052170312863590740)
XLA Ops:
  0.0 1.0 convert_element_type.75
  1.1 5.1 %collective-permute-start = (bf16[32,15,128]{2,1,0:T(8,128)(2,1)S(1)}, bf16[32,15,128]{2,1,0:T(8,128)(2,1)S(1)}, u32[]{:S(2)}, u32[]{:S(2)}) collective-permute-start(bf16[32,15,128]{2,1,0:T(8,128)(2,1)S(1)} %get-tuple-element.15), channel_id=1, source_target_pairs={{0,8},{8,16},{16,24},{24,32},{32,40},{40,48},{48,56},{56,64},{64,7... | collective-permute-start | bytes 368648 | tf_op jit(solution)/shard_map/ppermute | solution.py:16
  6.2 1.9 %collective-permute-start.1 = (bf16[32,15,128]{2,1,0:T(8,128)(2,1)S(1)}, bf16[32,15,128]{2,1,0:T(8,128)(2,1)S(1)}, u32[]{:S(2)}, u32[]{:S(2)}) collective-permute-start(bf16[32,15,128]{2,1,0:T(8,128)(2,1)S(1)} %get-tuple-element.16), channel_id=1, source_target_pairs={{8,0},{16,8},{24,16},{32,24},{40,32},{48,40},{56,48},{64,56},{72,6... | collective-permute-start | bytes 368648 | tf_op jit(solution)/shard_map/ppermute | solution.py:17
  8.1 0.1 reduce_sum.29
  8.4 0.1 rev.7
  8.7 0.1 reshape.90
  8.9 0.1 reshape.91
  9.0 0.1 reduce_sum.28
  9.4 0.3 reshape.89
  9.8 0.3 reshape.88
  10.1 0.1 reduce_sum.27
  10.3 4.3 %collective-permute-done.1 = bf16[32,15,128]{2,1,0:T(8,128)(2,1)S(1)} collective-permute-done((bf16[32,15,128]{2,1,0:T(8,128)(2,1)S(1)}, bf16[32,15,128]{2,1,0:T(8,128)(2,1)S(1)}, u32[]{:S(2)}, u32[]{:S(2)}) %collective-permute-start.1) | collective-permute-done | bytes 122912 | tf_op jit(solution)/shard_map/ppermute | solution.py:17
  14.6 0.7 fusion.12
  15.3 0.2 copy-done.1
  15.6 0.3 reshape.118
  16.0 0.9 copy.51
  16.9 16.4 %all-to-all-start = ((bf16[8,128,256]{2,1,0:T(8,128)(2,1)}), bf16[8,128,256]{2,1,0:T(8,128)(2,1)S(1)}, u32[]{:S(2)}, u32[]{:S(2)}) async-start(bf16[8,128,256]{2,1,0:T(8,128)(2,1)} %copy.51), calls=%async_computation | async-start | bytes 1048576 | tf_op jit(solution)/shard_map/all_to_all | solution.py:95
  33.5 0.1 copy.56
  33.6 0.4 reshape.86
  34.0 0.1 copy.53
  34.2 0.1 copy.57
  34.3 0.4 reshape.87
  34.8 0.1 copy.54
  34.9 13.7 %all-to-all-done = bf16[8,128,256]{2,1,0:T(8,128)(2,1)S(1)} async-done(((bf16[8,128,256]{2,1,0:T(8,128)(2,1)}), bf16[8,128,256]{2,1,0:T(8,128)(2,1)S(1)}, u32[]{:S(2)}, u32[]{:S(2)}) %all-to-all-start) | async-done | bytes 524320 | tf_op jit(solution)/shard_map/all_to_all | solution.py:95
  48.7 0.5 convolution_convert_fusion.5
  49.2 12.3 %all_to_all.20 = bf16[8,64,256]{2,1,0:T(8,128)(2,1)S(1)} all-to-all(bf16[8,64,256]{2,1,0:T(8,128)(2,1)S(1)} %bitcast.168), channel_id=1, replica_groups=mesh['view'=4,'row'=32,'col'=8] {'col'}, dimensions={0} | all-to-all | bytes 524288 | tf_op jit(solution)/shard_map/all_to_all | solution.py:102
  61.7 0.1 copy.35
  61.8 0.1 fusion.78
  61.9 8.3 %collective-permute-start.2 = (bf16[2,32,15,128]{3,2,0,1:T(8,128)(2,1)S(1)}, bf16[2,32,15,128]{3,2,0,1:T(8,128)(2,1)S(1)}, u32[]{:S(2)}, u32[]{:S(2)}) collective-permute-start(bf16[2,32,15,128]{3,2,0,1:T(8,128)(2,1)S(1)} %get-tuple-element.11), channel_id=1, source_target_pairs={{0,8},{8,16},{16,24},{24,32},{32,40},{40,48},{48,56},{56,64},{64,7... | collective-permute-start | bytes 737288 | tf_op jit(solution)/shard_map/ppermute | solution.py:16
  70.2 1.9 %collective-permute-start.3 = (bf16[2,32,15,128]{3,2,0,1:T(8,128)(2,1)S(1)}, bf16[2,32,15,128]{3,2,0,1:T(8,128)(2,1)S(1)}, u32[]{:S(2)}, u32[]{:S(2)}) collective-permute-start(bf16[2,32,15,128]{3,2,0,1:T(8,128)(2,1)S(1)} %get-tuple-element.12), channel_id=1, source_target_pairs={{8,0},{16,8},{24,16},{32,24},{40,32},{48,40},{56,48},{64,56},{72,6... | collective-permute-start | bytes 737288 | tf_op jit(solution)/shard_map/ppermute | solution.py:17
  72.2 0.1 reshape.100
  72.4 0.1 reshape.99
  72.6 2.2 %collective-permute-done.2 = bf16[2,32,15,128]{3,2,0,1:T(8,128)(2,1)S(1)} collective-permute-done((bf16[2,32,15,128]{3,2,0,1:T(8,128)(2,1)S(1)}, bf16[2,32,15,128]{3,2,0,1:T(8,128)(2,1)S(1)}, u32[]{:S(2)}, u32[]{:S(2)}) %collective-permute-start.2) | collective-permute-done | bytes 245792 | tf_op jit(solution)/shard_map/ppermute | solution.py:16
  74.8 6.5 %collective-permute-done.3 = bf16[2,32,15,128]{3,2,0,1:T(8,128)(2,1)S(1)} collective-permute-done((bf16[2,32,15,128]{3,2,0,1:T(8,128)(2,1)S(1)}, bf16[2,32,15,128]{3,2,0,1:T(8,128)(2,1)S(1)}, u32[]{:S(2)}, u32[]{:S(2)}) %collective-permute-start.3) | collective-permute-done | bytes 245792 | tf_op jit(solution)/shard_map/ppermute | solution.py:17
  81.3 0.5 fusion.8
  81.8 4.3 %collective-permute-start.4 = (f32[16,16,128]{2,1,0:T(8,128)S(1)}, f32[16,16,128]{2,1,0:T(8,128)S(1)}, u32[]{:S(2)}, u32[]{:S(2)}) collective-permute-start(f32[16,16,128]{2,1,0:T(8,128)S(1)} %constant_dynamic-slice_fusion.1), channel_id=1, source_target_pairs={{0,256},{256,0},{512,768},{768,512},{1,257},{257,1},{513,769},{769... | collective-permute-start | bytes 393224 | tf_op jit(solution)/shard_map/ppermute | solution.py:170
  86.2 1.0 collective-permute-done.4
  87.1 2.2 %collective-permute-start.5 = (f32[16,16,128]{2,1,0:T(8,128)S(1)}, f32[16,16,128]{2,1,0:T(8,128)S(1)}, u32[]{:S(2)}, u32[]{:S(2)}) collective-permute-start(f32[16,16,128]{2,1,0:T(8,128)S(1)} %dynamic-slice_add_fusion.1), channel_id=1, source_target_pairs={{0,512},{256,768},{512,0},{768,256},{1,513},{257,769},{513,1},{769... | collective-permute-start | bytes 393224 | tf_op jit(solution)/shard_map/ppermute | solution.py:173
  89.4 8.3 %collective-permute-done.5 = f32[16,16,128]{2,1,0:T(8,128)S(1)} collective-permute-done((f32[16,16,128]{2,1,0:T(8,128)S(1)}, f32[16,16,128]{2,1,0:T(8,128)S(1)}, u32[]{:S(2)}, u32[]{:S(2)}) %collective-permute-start.5) | collective-permute-done | bytes 131104 | tf_op jit(solution)/shard_map/ppermute | solution.py:173
  97.7 3.1 %collective-permute-start.6 = (bf16[16,16,128]{2,1,0:T(8,128)(2,1)S(1)}, bf16[16,16,128]{2,1,0:T(8,128)(2,1)S(1)}, u32[]{:S(2)}, u32[]{:S(2)}) collective-permute-start(bf16[16,16,128]{2,1,0:T(8,128)(2,1)S(1)} %get-tuple-element.5), channel_id=1, source_target_pairs={{0,256},{256,0},{512,768},{768,512},{1,257},{257,1},{513,769},{769... | collective-permute-start | bytes 196616 | tf_op jit(solution)/shard_map/ppermute | solution.py:168
  100.8 0.9 collective-permute-done.6
  101.7 6.9 %collective-permute-start.7 = (bf16[32,15,128]{2,1,0:T(8,128)(2,1)S(1)}, bf16[32,15,128]{2,1,0:T(8,128)(2,1)S(1)}, u32[]{:S(2)}, u32[]{:S(2)}) collective-permute-start(bf16[32,15,128]{2,1,0:T(8,128)(2,1)S(1)} %get-tuple-element.13), channel_id=1, source_target_pairs={{0,8},{8,16},{16,24},{24,32},{32,40},{40,48},{48,56},{56,64},{64,7... | collective-permute-start | bytes 368648 | tf_op jit(solution)/shard_map/ppermute | solution.py:16
  108.7 1.9 %collective-permute-start.8 = (bf16[32,15,128]{2,1,0:T(8,128)(2,1)S(1)}, bf16[32,15,128]{2,1,0:T(8,128)(2,1)S(1)}, u32[]{:S(2)}, u32[]{:S(2)}) collective-permute-start(bf16[32,15,128]{2,1,0:T(8,128)(2,1)S(1)} %get-tuple-element.14), channel_id=1, source_target_pairs={{8,0},{16,8},{24,16},{32,24},{40,32},{48,40},{56,48},{64,56},{72,6... | collective-permute-start | bytes 368648 | tf_op jit(solution)/shard_map/ppermute | solution.py:17
  110.6 0.5 collective-permute-done.7
  111.1 6.5 %collective-permute-done.8 = bf16[32,15,128]{2,1,0:T(8,128)(2,1)S(1)} collective-permute-done((bf16[32,15,128]{2,1,0:T(8,128)(2,1)S(1)}, bf16[32,15,128]{2,1,0:T(8,128)(2,1)S(1)}, u32[]{:S(2)}, u32[]{:S(2)}) %collective-permute-start.8) | collective-permute-done | bytes 122912 | tf_op jit(solution)/shard_map/ppermute | solution.py:17
  117.7 0.7 fusion.4
  118.4 0.2 reshape.119
  118.6 12.6 %all_to_all.21 = bf16[8,64,256]{2,1,0:T(8,128)(2,1)S(1)} all-to-all(bf16[8,64,256]{2,1,0:T(8,128)(2,1)S(1)} %copy.52), channel_id=1, replica_groups=mesh['view'=4,'row'=32,'col'=8] {'col'}, dimensions={0} | all-to-all | bytes 524288 | tf_op jit(solution)/shard_map/all_to_all | solution.py:95
  131.3 0.5 convolution_convert_fusion.3
  131.8 12.0 %all_to_all.22 = bf16[8,64,256]{2,1,0:T(8,128)(2,1)S(1)} all-to-all(bf16[8,64,256]{2,1,0:T(8,128)(2,1)S(1)} %bitcast.170), channel_id=1, replica_groups=mesh['view'=4,'row'=32,'col'=8] {'col'}, dimensions={0} | all-to-all | bytes 524288 | tf_op jit(solution)/shard_map/all_to_all | solution.py:102
  143.9 0.1 copy.42
  144.0 0.1 fusion.77
  144.1 1.9 %collective-permute-start.10 = (bf16[2,32,15,128]{3,2,0,1:T(8,128)(2,1)S(1)}, bf16[2,32,15,128]{3,2,0,1:T(8,128)(2,1)S(1)}, u32[]{:S(2)}, u32[]{:S(2)}) collective-permute-start(bf16[2,32,15,128]{3,2,0,1:T(8,128)(2,1)S(1)} %get-tuple-element.10), channel_id=1, source_target_pairs={{8,0},{16,8},{24,16},{32,24},{40,32},{48,40},{56,48},{64,56},{72,6... | collective-permute-start | bytes 737288 | tf_op jit(solution)/shard_map/ppermute | solution.py:17
  146.0 7.4 %collective-permute-start.9 = (bf16[2,32,15,128]{3,2,0,1:T(8,128)(2,1)S(1)}, bf16[2,32,15,128]{3,2,0,1:T(8,128)(2,1)S(1)}, u32[]{:S(2)}, u32[]{:S(2)}) collective-permute-start(bf16[2,32,15,128]{3,2,0,1:T(8,128)(2,1)S(1)} %get-tuple-element.9), channel_id=1, source_target_pairs={{0,8},{8,16},{16,24},{24,32},{32,40},{40,48},{48,56},{56,64},{64,7... | collective-permute-start | bytes 737288 | tf_op jit(solution)/shard_map/ppermute | solution.py:16
  153.4 2.3 %collective-permute-done.10 = bf16[2,32,15,128]{3,2,0,1:T(8,128)(2,1)S(1)} collective-permute-done((bf16[2,32,15,128]{3,2,0,1:T(8,128)(2,1)S(1)}, bf16[2,32,15,128]{3,2,0,1:T(8,128)(2,1)S(1)}, u32[]{:S(2)}, u32[]{:S(2)}) %collective-permute-start.10) | collective-permute-done | bytes 245792 | tf_op jit(solution)/shard_map/ppermute | solution.py:17
  155.7 3.9 %collective-permute-done.9 = bf16[2,32,15,128]{3,2,0,1:T(8,128)(2,1)S(1)} collective-permute-done((bf16[2,32,15,128]{3,2,0,1:T(8,128)(2,1)S(1)}, bf16[2,32,15,128]{3,2,0,1:T(8,128)(2,1)S(1)}, u32[]{:S(2)}, u32[]{:S(2)}) %collective-permute-start.9) | collective-permute-done | bytes 245792 | tf_op jit(solution)/shard_map/ppermute | solution.py:16
  159.6 0.5 fusion.11
  160.1 7.4 %collective-permute-start.11 = (f32[16,16,128]{2,1,0:T(8,128)S(1)}, f32[16,16,128]{2,1,0:T(8,128)S(1)}, u32[]{:S(2)}, u32[]{:S(2)}) collective-permute-start(f32[16,16,128]{2,1,0:T(8,128)S(1)} %constant_dynamic-slice_fusion), channel_id=1, source_target_pairs={{0,256},{256,0},{512,768},{768,512},{1,257},{257,1},{513,769},{769... | collective-permute-start | bytes 393224 | tf_op jit(solution)/shard_map/ppermute | solution.py:170
  167.5 1.0 collective-permute-done.11
  168.4 1.9 %collective-permute-start.12 = (f32[16,16,128]{2,1,0:T(8,128)S(1)}, f32[16,16,128]{2,1,0:T(8,128)S(1)}, u32[]{:S(2)}, u32[]{:S(2)}) collective-permute-start(f32[16,16,128]{2,1,0:T(8,128)S(1)} %dynamic-slice_add_fusion), channel_id=1, source_target_pairs={{0,512},{256,768},{512,0},{768,256},{1,513},{257,769},{513,1},{769... | collective-permute-start | bytes 393224 | tf_op jit(solution)/shard_map/ppermute | solution.py:173
  170.4 8.6 %collective-permute-done.12 = f32[16,16,128]{2,1,0:T(8,128)S(1)} collective-permute-done((f32[16,16,128]{2,1,0:T(8,128)S(1)}, f32[16,16,128]{2,1,0:T(8,128)S(1)}, u32[]{:S(2)}, u32[]{:S(2)}) %collective-permute-start.12) | collective-permute-done | bytes 131104 | tf_op jit(solution)/shard_map/ppermute | solution.py:173
  179.0 3.1 %collective-permute-start.13 = (f32[16,16,128]{2,1,0:T(8,128)S(1)}, f32[16,16,128]{2,1,0:T(8,128)S(1)}, u32[]{:S(2)}, u32[]{:S(2)}) collective-permute-start(f32[16,16,128]{2,1,0:T(8,128)S(1)} %multiply_multiply_fusion), channel_id=1, source_target_pairs={{0,256},{256,0},{512,768},{768,512},{1,257},{257,1},{513,769},{769... | collective-permute-start | bytes 393224 | tf_op jit(solution)/shard_map/ppermute | solution.py:175
  182.1 1.0 collective-permute-done.13
  183.1 0.7 maximum_select_fusion
  (65 shorter events, 1.9 us)
Async XLA Ops:
  0.0 8.5 %copy-start.5 = (pred[62]{0:T(512)(128)(4,1)S(1)}, pred[62]{0:T(512)(128)(4,1)}, u32[]{:S(2)}) copy-start(pred[62]{0:T(512)(128)(4,1)} %constant.39.clone.1) | copy-start | bytes 190
  0.0 8.1 %copy-start.2 = (f32[2,31]{1,0:T(2,128)S(1)}, f32[2,31]{1,0:T(2,128)}, u32[]{:S(2)}) copy-start(f32[2,31]{1,0:T(2,128)} %param.8) | copy-start | bytes 748
  0.0 9.0 %copy-start.3 = (f32[2,31]{1,0:T(2,128)S(1)}, f32[2,31]{1,0:T(2,128)}, u32[]{:S(2)}) copy-start(f32[2,31]{1,0:T(2,128)} %param.7) | copy-start | bytes 748
  1.1 9.1 %copy-start.4 = (f32[2,121]{1,0:T(2,128)S(1)}, f32[2,121]{1,0:T(2,128)}, u32[]{:S(2)}) copy-start(f32[2,121]{1,0:T(2,128)} %param.9) | copy-start | bytes 2908
  1.1 9.3 %collective-permute-start = (bf16[32,15,128]{2,1,0:T(8,128)(2,1)S(1)}, bf16[32,15,128]{2,1,0:T(8,128)(2,1)S(1)}, u32[]{:S(2)}, u32[]{:S(2)}) collective-permute-start(bf16[32,15,128]{2,1,0:T(8,128)(2,1)S(1)} %get-tuple-element.15), channel_id=1, source_target_pairs={{0,8},{8,16},{16,24},{24,32},{32,40},{40,48},{48,56},{56,64},{64,7... | collective-permute-start | bytes 368648 | tf_op jit(solution)/shard_map/ppermute | solution.py:16
  6.2 8.4 %collective-permute-start.1 = (bf16[32,15,128]{2,1,0:T(8,128)(2,1)S(1)}, bf16[32,15,128]{2,1,0:T(8,128)(2,1)S(1)}, u32[]{:S(2)}, u32[]{:S(2)}) collective-permute-start(bf16[32,15,128]{2,1,0:T(8,128)(2,1)S(1)} %get-tuple-element.16), channel_id=1, source_target_pairs={{8,0},{16,8},{24,16},{32,24},{40,32},{48,40},{56,48},{64,56},{72,6... | collective-permute-start | bytes 368648 | tf_op jit(solution)/shard_map/ppermute | solution.py:17
  14.6 1.0 copy-start.1
  16.9 31.7 %all-to-all-start = ((bf16[8,128,256]{2,1,0:T(8,128)(2,1)}), bf16[8,128,256]{2,1,0:T(8,128)(2,1)S(1)}, u32[]{:S(2)}, u32[]{:S(2)}) async-start(bf16[8,128,256]{2,1,0:T(8,128)(2,1)} %copy.51), calls=%async_computation | async-start | bytes 1048576 | tf_op jit(solution)/shard_map/all_to_all | solution.py:95
  61.9 12.9 %collective-permute-start.2 = (bf16[2,32,15,128]{3,2,0,1:T(8,128)(2,1)S(1)}, bf16[2,32,15,128]{3,2,0,1:T(8,128)(2,1)S(1)}, u32[]{:S(2)}, u32[]{:S(2)}) collective-permute-start(bf16[2,32,15,128]{3,2,0,1:T(8,128)(2,1)S(1)} %get-tuple-element.11), channel_id=1, source_target_pairs={{0,8},{8,16},{16,24},{24,32},{32,40},{40,48},{48,56},{56,64},{64,7... | collective-permute-start | bytes 737288 | tf_op jit(solution)/shard_map/ppermute | solution.py:16
  70.2 11.1 %collective-permute-start.3 = (bf16[2,32,15,128]{3,2,0,1:T(8,128)(2,1)S(1)}, bf16[2,32,15,128]{3,2,0,1:T(8,128)(2,1)S(1)}, u32[]{:S(2)}, u32[]{:S(2)}) collective-permute-start(bf16[2,32,15,128]{3,2,0,1:T(8,128)(2,1)S(1)} %get-tuple-element.12), channel_id=1, source_target_pairs={{8,0},{16,8},{24,16},{32,24},{40,32},{48,40},{56,48},{64,56},{72,6... | collective-permute-start | bytes 737288 | tf_op jit(solution)/shard_map/ppermute | solution.py:17
  81.8 15.9 %copy-start = (f32[32,16,128]{2,1,0:T(8,128)S(1)}, f32[32,16,128]{2,1,0:T(8,128)}, u32[]{:S(2)}) copy-start(f32[32,16,128]{2,1,0:T(8,128)} %param.5) | copy-start | bytes 786436
  81.8 5.3 %collective-permute-start.4 = (f32[16,16,128]{2,1,0:T(8,128)S(1)}, f32[16,16,128]{2,1,0:T(8,128)S(1)}, u32[]{:S(2)}, u32[]{:S(2)}) collective-permute-start(f32[16,16,128]{2,1,0:T(8,128)S(1)} %constant_dynamic-slice_fusion.1), channel_id=1, source_target_pairs={{0,256},{256,0},{512,768},{768,512},{1,257},{257,1},{513,769},{769... | collective-permute-start | bytes 393224 | tf_op jit(solution)/shard_map/ppermute | solution.py:170
  87.1 10.5 %collective-permute-start.5 = (f32[16,16,128]{2,1,0:T(8,128)S(1)}, f32[16,16,128]{2,1,0:T(8,128)S(1)}, u32[]{:S(2)}, u32[]{:S(2)}) collective-permute-start(f32[16,16,128]{2,1,0:T(8,128)S(1)} %dynamic-slice_add_fusion.1), channel_id=1, source_target_pairs={{0,512},{256,768},{512,0},{768,256},{1,513},{257,769},{513,1},{769... | collective-permute-start | bytes 393224 | tf_op jit(solution)/shard_map/ppermute | solution.py:173
  97.7 4.0 %collective-permute-start.6 = (bf16[16,16,128]{2,1,0:T(8,128)(2,1)S(1)}, bf16[16,16,128]{2,1,0:T(8,128)(2,1)S(1)}, u32[]{:S(2)}, u32[]{:S(2)}) collective-permute-start(bf16[16,16,128]{2,1,0:T(8,128)(2,1)S(1)} %get-tuple-element.5), channel_id=1, source_target_pairs={{0,256},{256,0},{512,768},{768,512},{1,257},{257,1},{513,769},{769... | collective-permute-start | bytes 196616 | tf_op jit(solution)/shard_map/ppermute | solution.py:168
  101.7 9.4 %collective-permute-start.7 = (bf16[32,15,128]{2,1,0:T(8,128)(2,1)S(1)}, bf16[32,15,128]{2,1,0:T(8,128)(2,1)S(1)}, u32[]{:S(2)}, u32[]{:S(2)}) collective-permute-start(bf16[32,15,128]{2,1,0:T(8,128)(2,1)S(1)} %get-tuple-element.13), channel_id=1, source_target_pairs={{0,8},{8,16},{16,24},{24,32},{32,40},{40,48},{48,56},{56,64},{64,7... | collective-permute-start | bytes 368648 | tf_op jit(solution)/shard_map/ppermute | solution.py:16
  108.7 9.0 %collective-permute-start.8 = (bf16[32,15,128]{2,1,0:T(8,128)(2,1)S(1)}, bf16[32,15,128]{2,1,0:T(8,128)(2,1)S(1)}, u32[]{:S(2)}, u32[]{:S(2)}) collective-permute-start(bf16[32,15,128]{2,1,0:T(8,128)(2,1)S(1)} %get-tuple-element.14), channel_id=1, source_target_pairs={{8,0},{16,8},{24,16},{32,24},{40,32},{48,40},{56,48},{64,56},{72,6... | collective-permute-start | bytes 368648 | tf_op jit(solution)/shard_map/ppermute | solution.py:17
  144.1 11.7 %collective-permute-start.10 = (bf16[2,32,15,128]{3,2,0,1:T(8,128)(2,1)S(1)}, bf16[2,32,15,128]{3,2,0,1:T(8,128)(2,1)S(1)}, u32[]{:S(2)}, u32[]{:S(2)}) collective-permute-start(bf16[2,32,15,128]{3,2,0,1:T(8,128)(2,1)S(1)} %get-tuple-element.10), channel_id=1, source_target_pairs={{8,0},{16,8},{24,16},{32,24},{40,32},{48,40},{56,48},{64,56},{72,6... | collective-permute-start | bytes 737288 | tf_op jit(solution)/shard_map/ppermute | solution.py:17
  146.0 13.6 %collective-permute-start.9 = (bf16[2,32,15,128]{3,2,0,1:T(8,128)(2,1)S(1)}, bf16[2,32,15,128]{3,2,0,1:T(8,128)(2,1)S(1)}, u32[]{:S(2)}, u32[]{:S(2)}) collective-permute-start(bf16[2,32,15,128]{3,2,0,1:T(8,128)(2,1)S(1)} %get-tuple-element.9), channel_id=1, source_target_pairs={{0,8},{8,16},{16,24},{24,32},{32,40},{40,48},{48,56},{56,64},{64,7... | collective-permute-start | bytes 737288 | tf_op jit(solution)/shard_map/ppermute | solution.py:16
  160.1 8.3 %collective-permute-start.11 = (f32[16,16,128]{2,1,0:T(8,128)S(1)}, f32[16,16,128]{2,1,0:T(8,128)S(1)}, u32[]{:S(2)}, u32[]{:S(2)}) collective-permute-start(f32[16,16,128]{2,1,0:T(8,128)S(1)} %constant_dynamic-slice_fusion), channel_id=1, source_target_pairs={{0,256},{256,0},{512,768},{768,512},{1,257},{257,1},{513,769},{769... | collective-permute-start | bytes 393224 | tf_op jit(solution)/shard_map/ppermute | solution.py:170
  168.4 10.5 %collective-permute-start.12 = (f32[16,16,128]{2,1,0:T(8,128)S(1)}, f32[16,16,128]{2,1,0:T(8,128)S(1)}, u32[]{:S(2)}, u32[]{:S(2)}) collective-permute-start(f32[16,16,128]{2,1,0:T(8,128)S(1)} %dynamic-slice_add_fusion), channel_id=1, source_target_pairs={{0,512},{256,768},{512,0},{768,256},{1,513},{257,769},{513,1},{769... | collective-permute-start | bytes 393224 | tf_op jit(solution)/shard_map/ppermute | solution.py:173
  179.0 4.1 %collective-permute-start.13 = (f32[16,16,128]{2,1,0:T(8,128)S(1)}, f32[16,16,128]{2,1,0:T(8,128)S(1)}, u32[]{:S(2)}, u32[]{:S(2)}) collective-permute-start(f32[16,16,128]{2,1,0:T(8,128)S(1)} %multiply_multiply_fusion), channel_id=1, source_target_pairs={{0,256},{256,0},{512,768},{768,512},{1,257},{257,1},{513,769},{769... | collective-permute-start | bytes 393224 | tf_op jit(solution)/shard_map/ppermute | solution.py:175

commit v5 on v0

v5 whole, which is shorter than its diff:
```python
import jax
import jax.numpy as jnp
from jax import lax
from jax.sharding import PartitionSpec as P

ITERS = 2


def extended(shard, sides, width):
    for axis, dim in sides:
        count, length = (lax.axis_size(axis), shard.shape[dim])
        up = [(i, (i + 1) % count) for i in range(count - 1)]
        down = [(j, i) for i, j in up]
        last = lax.slice_in_dim(shard, length - width, length, axis=dim)
        initial = lax.slice_in_dim(shard, 0, width, axis=dim)
        before = lax.ppermute(last, axis, up)
        after = lax.ppermute(initial, axis, down)
        shard = jnp.concatenate([before, shard, after], axis=dim)
    return shard


def toeplitz_band(kernel, height, breadth, offset):
    extent = height + breadth
    zeros_pad = jnp.zeros((extent,), kernel.dtype)
    padded = jnp.concatenate([zeros_pad, kernel, zeros_pad])
    leading = lax.slice_in_dim(padded, extent + offset, extent + offset + breadth)
    trailing = lax.slice_in_dim(padded, extent + offset - height, extent + offset)
    ribbon = jnp.concatenate([leading, trailing])
    tiled = jnp.tile(ribbon, height)[: height * (extent - 1)]
    return tiled.reshape(height, extent - 1)[:, :breadth]


def normalized(kernel):
    return (kernel / jnp.sum(kernel, axis=1, keepdims=True)).astype(jnp.bfloat16)


def on_device(estimate, views, kernel_xdir, kernel_ydir, kernel_axial):
    planes_local, height, across = estimate.shape
    blocks = lax.axis_size("col")
    planes = planes_local * blocks
    view_size = lax.axis_size("view")
    view_count = views.shape[0]
    total_views = view_count * view_size
    radius_lat = kernel_xdir.shape[1] // 2
    radius_ax = kernel_axial.shape[1] // 2
    framed_rows = height + 2 * radius_lat
    half = planes_local // 2
    pair = height // blocks
    column_width = pair * across
    core_bit = lax.axis_index("view") % 2
    to_core = [(i, i ^ 1) for i in range(view_size)]
    to_far = [(i, i ^ 2) for i in range(view_size)]
    group = 2 * blocks
    groups = [list(range(g * group, (g + 1) * group)) for g in range(view_size // 2)]

    def joined(mine, theirs):
        return jnp.where(
            core_bit == 0,
            jnp.concatenate([mine, theirs], axis=0),
            jnp.concatenate([theirs, mine], axis=0),
        )

    def chip_taps(kernel):
        return normalized(joined(kernel, lax.ppermute(kernel, "view", to_core)))

    chip_x = chip_taps(kernel_xdir)
    chip_y = chip_taps(kernel_ydir)
    taps_axial = normalized(kernel_axial)
    chip_count = chip_x.shape[0]
    bands_x = jnp.stack(
        [toeplitz_band(chip_x[member], across, across, radius_lat) for member in range(chip_count)]
    )
    bands_y = jnp.stack(
        [toeplitz_band(chip_y[member], height, framed_rows, 0) for member in range(chip_count)]
    )
    bands_yback = jnp.stack(
        [
            toeplitz_band(chip_y[member][::-1], height, framed_rows, 0)
            for member in range(chip_count)
        ]
    )
    bands_z = jnp.stack(
        [
            toeplitz_band(taps_axial[member], planes, planes, radius_ax)
            for member in range(view_count)
        ]
    )
    bands_z = bands_z.reshape(view_count, planes, blocks, 2, half)

    def framed(field):
        return extended(field, (("row", 2),), radius_lat)

    def chip_exchange(chunks):
        return lax.all_to_all(
            chunks, ("view", "col"), 0, 0, axis_index_groups=groups, tiled=True
        )

    def to_columns(field):
        chunks = field.reshape(2, view_count, half, blocks, pair, across)
        chunks = chunks.transpose(0, 3, 1, 2, 4, 5).reshape(group, view_count * half, column_width)
        gathered = chip_exchange(chunks)
        return gathered.reshape(2, blocks, view_count, half, column_width)

    def to_slabs(columns):
        chunks = columns.reshape(view_count, blocks, 2, half, column_width)
        chunks = chunks.transpose(2, 1, 0, 3, 4).reshape(group, view_count * half, column_width)
        spread = chip_exchange(chunks)
        spread = spread.reshape(2, blocks, view_count, half, pair, across)
        spread = spread.transpose(0, 2, 3, 1, 4, 5)
        return spread.reshape(chip_count, half, height, across)

    own = lax.all_to_all(
        views.reshape(view_count, planes_local, blocks, column_width).transpose(2, 0, 1, 3),
        "col",
        0,
        0,
        tiled=True,
    )
    view_columns = own.transpose(1, 0, 2, 3).reshape(view_count, planes, column_width)

    def correct(coarse_framed):
        smeared = jnp.einsum(
            "zyj,vij->vzyi", coarse_framed, bands_x, preferred_element_type=jnp.float32
        ).astype(jnp.bfloat16)
        lateral = jnp.einsum(
            "vij,vzjx->vzix", bands_y, smeared, preferred_element_type=jnp.float32
        ).astype(jnp.bfloat16)
        columns = to_columns(lateral)
        blurred = jnp.einsum(
            "vicbz,bcvzm->vim", bands_z, columns, preferred_element_type=jnp.float32
        )
        quotient = (view_columns / blurred).astype(jnp.bfloat16)
        returned = jnp.einsum(
            "vicbz,vim->vcbzm", bands_z, quotient, preferred_element_type=jnp.float32
        ).astype(jnp.bfloat16)
        backward = jnp.einsum(
            "vij,vzjx->vzix", bands_yback, framed(to_slabs(returned)),
            preferred_element_type=jnp.float32,
        ).astype(jnp.bfloat16)
        return jnp.einsum("vzyi,vij->zyj", backward, bands_x, preferred_element_type=jnp.float32)

    restored_mine = lax.dynamic_slice_in_dim(estimate, core_bit * half, half, axis=0)
    for iteration in range(ITERS):
        coarse_mine = restored_mine.astype(jnp.bfloat16)
        accumulated = correct(extended(coarse_mine, (("row", 1),), radius_lat))
        summed = accumulated + lax.ppermute(accumulated, "view", to_far)
        restored_mine = restored_mine * summed / total_views
    return joined(restored_mine, lax.ppermute(restored_mine, "view", to_core))


def solution(mesh):
    placed = (
        P("col", "row", None),
        P("view", "col", "row", None),
        P("view", None),
        P("view", None),
        P("view", None),
    )
    return jax.shard_map(
        on_device, mesh=mesh, in_specs=placed, out_specs=P("col", "row", None), check_vma=False
    )
```

time: 382 us -> 188 us (0.49)
  the two profiles are of different devices: /device:TPU:1 before, /device:TPU:113 now
where the time goes in v5:
time: 188 us; the launch traced here: 186 us
  starting transfers between devices  69.7 us (37%)
  waiting for transfers between devices  65.7 us (35%)
  blocking collectives  34.9 us (19%)
  local copies, waits for them, and re-layouts  10.1 us (5%)
  matrix products  3.06 us (2%)
    all_to_all x2, blocking collectives, chip_exchange(): lax.all_to_all(chunks, ('view', 'col'), 0, 0, axis_index_groups=groups, t...  34.9 us
    ppermute x4, starting transfers between devices, extended(): before = lax.ppermute(last, axis, up)  22.8 us
    all_to_all x2, waiting for transfers between devices, chip_exchange(): lax.all_to_all(chunks, ('view', 'col'), 0, 0, axis_index_groups=groups, t...  17.6 us
    all_to_all x1, starting transfers between devices, on_device(): lax.all_to_all(views.reshape(view_count, planes_local, blocks, column_wid...  16.4 us
    ppermute x2, waiting for transfers between devices, on_device(): summed = accumulated + lax.ppermute(accumulated, 'view', to_far)  16.1 us
    ppermute x4, waiting for transfers between devices, extended(): after = lax.ppermute(initial, axis, down)  16 us
    ppermute x4, waiting for transfers between devices, extended(): before = lax.ppermute(last, axis, up)  11.1 us
    all_to_all x2, starting transfers between devices, chip_exchange(): lax.all_to_all(chunks, ('view', 'col'), 0, 0, axis_index_groups=groups, t...  11.1 us
  transfers between devices with their start and end apart: 16, of which 11 were waited for; matrix products, arithmetic and copies ran while one was open for 5% of the time, Pallas kernels for 0%

profile of v5, /device:TPU:113, one launch (start us, length us, event | category | flops | bytes accessed | tf_op | source)
XLA Modules:
  0.0 185.6 jit_solution(2508591770669724023)
XLA Ops:
  0.0 2.7 %collective-permute-start.3 = (f32[2,31]{1,0:T(2,128)}, f32[2,31]{1,0:T(2,128)S(1)}, u32[]{:S(2)}, u32[]{:S(2)}) collective-permute-start(f32[2,31]{1,0:T(2,128)} %param.8), channel_id=1, source_target_pairs={{0,256},{256,0},{512,768},{768,512},{1,257},{257,1},{513,769},{769... | collective-permute-start | bytes 752 | tf_op jit(solution)/shard_map/ppermute | solution.py:64
  2.7 1.9 %collective-permute-start = (f32[2,31]{1,0:T(2,128)}, f32[2,31]{1,0:T(2,128)S(1)}, u32[]{:S(2)}, u32[]{:S(2)}) collective-permute-start(f32[2,31]{1,0:T(2,128)} %param.7), channel_id=1, source_target_pairs={{0,256},{256,0},{512,768},{768,512},{1,257},{257,1},{513,769},{769... | collective-permute-start | bytes 752 | tf_op jit(solution)/shard_map/ppermute | solution.py:64
  4.7 0.9 dynamic-slice_convert_fusion
  5.6 5.1 %collective-permute-start.1 = (bf16[16,15,128]{2,1,0:T(8,128)(2,1)S(1)}, bf16[16,15,128]{2,1,0:T(8,128)(2,1)S(1)}, u32[]{:S(2)}, u32[]{:S(2)}) collective-permute-start(bf16[16,15,128]{2,1,0:T(8,128)(2,1)S(1)} %get-tuple-element.13), channel_id=1, source_target_pairs={{0,8},{8,16},{16,24},{24,32},{32,40},{40,48},{48,56},{56,64},{64,7... | collective-permute-start | bytes 184328 | tf_op jit(solution)/shard_map/ppermute | solution.py:16
  10.8 1.9 %collective-permute-start.2 = (bf16[16,15,128]{2,1,0:T(8,128)(2,1)S(1)}, bf16[16,15,128]{2,1,0:T(8,128)(2,1)S(1)}, u32[]{:S(2)}, u32[]{:S(2)}) collective-permute-start(bf16[16,15,128]{2,1,0:T(8,128)(2,1)S(1)} %get-tuple-element.14), channel_id=1, source_target_pairs={{8,0},{16,8},{24,16},{32,24},{40,32},{48,40},{56,48},{64,56},{72,6... | collective-permute-start | bytes 184328 | tf_op jit(solution)/shard_map/ppermute | solution.py:17
  12.8 0.8 copy.35
  13.6 16.4 %all-to-all-start = ((bf16[8,2,32,256]{3,2,1,0:T(8,128)(2,1)}), bf16[8,2,32,256]{3,2,1,0:T(8,128)(2,1)S(1)}, u32[]{:S(2)}, u32[]{:S(2)}) async-start(bf16[8,2,32,256]{3,2,1,0:T(8,128)(2,1)} %copy.35), calls=%async_computation | async-start | bytes 524288 | tf_op jit(solution)/shard_map/all_to_all | solution.py:112
  30.0 0.1 reduce_sum.27
  30.3 0.1 copy.61
  30.5 0.4 reshape.106
  31.1 0.1 fusion.68
  31.3 0.1 fusion.69
  32.0 0.1 reshape.114
  32.2 0.1 reshape.113
  32.4 0.1 reshape.116
  32.6 0.1 reshape.115
  32.9 0.3 reshape.112
  33.4 0.3 reshape.111
  33.9 0.3 reshape.110
  34.4 0.3 reshape.109
  34.7 0.6 fusion.5
  35.3 0.2 copy.80
  35.6 0.9 reshape.118
  36.4 3.9 %all-to-all-done = bf16[8,2,32,256]{3,2,1,0:T(8,128)(2,1)S(1)} async-done(((bf16[8,2,32,256]{3,2,1,0:T(8,128)(2,1)}), bf16[8,2,32,256]{3,2,1,0:T(8,128)(2,1)S(1)}, u32[]{:S(2)}, u32[]{:S(2)}) %all-to-all-start) | async-done | bytes 262176 | tf_op jit(solution)/shard_map/all_to_all | solution.py:112
  40.3 5.9 %all-to-all-start.1 = ((bf16[16,32,256]{2,1,0:T(8,128)(2,1)}), bf16[16,32,256]{2,1,0:T(8,128)(2,1)S(1)}, u32[]{:S(2)}, u32[]{:S(2)}) async-start(bf16[16,32,256]{2,1,0:T(8,128)(2,1)} %reshape.118), calls=%async_computation.1 | async-start | bytes 524288 | tf_op jit(solution)/shard_map/all_to_all | solution.py:94
  46.2 0.1 copy.62
  46.3 0.4 reshape.107
  47.0 8.5 %all-to-all-done.1 = bf16[16,32,256]{2,1,0:T(8,128)(2,1)S(1)} async-done(((bf16[16,32,256]{2,1,0:T(8,128)(2,1)}), bf16[16,32,256]{2,1,0:T(8,128)(2,1)S(1)}, u32[]{:S(2)}, u32[]{:S(2)}) %all-to-all-start.1) | async-done | bytes 262176 | tf_op jit(solution)/shard_map/all_to_all | solution.py:94
  55.6 0.5 fusion.12
  56.0 0.7 copy.40
  56.8 5.2 %all-to-all-start.2 = ((bf16[16,32,256]{2,1,0:T(8,128)(2,1)}), bf16[16,32,256]{2,1,0:T(8,128)(2,1)S(1)}, u32[]{:S(2)}, u32[]{:S(2)}) async-start(bf16[16,32,256]{2,1,0:T(8,128)(2,1)} %bitcast.38), calls=%async_computation.2 | async-start | bytes 524288 | tf_op jit(solution)/shard_map/all_to_all | solution.py:94
  62.1 0.1 reshape.126
  62.3 0.1 reshape.125
  62.5 0.1 reshape.124
  62.6 9.0 %all-to-all-done.2 = bf16[16,32,256]{2,1,0:T(8,128)(2,1)S(1)} async-done(((bf16[16,32,256]{2,1,0:T(8,128)(2,1)}), bf16[16,32,256]{2,1,0:T(8,128)(2,1)S(1)}, u32[]{:S(2)}, u32[]{:S(2)}) %all-to-all-start.2) | async-done | bytes 262176 | tf_op jit(solution)/shard_map/all_to_all | solution.py:94
  71.8 0.1 fusion.80
  72.0 6.1 %collective-permute-start.4 = (bf16[4,16,15,128]{3,2,0,1:T(8,128)(2,1)S(1)}, bf16[4,16,15,128]{3,2,0,1:T(8,128)(2,1)S(1)}, u32[]{:S(2)}, u32[]{:S(2)}) collective-permute-start(bf16[4,16,15,128]{3,2,0,1:T(8,128)(2,1)S(1)} %get-tuple-element.9), channel_id=1, source_target_pairs={{0,8},{8,16},{16,24},{24,32},{32,40},{40,48},{48,56},{56,64},{64,7... | collective-permute-start | bytes 737288 | tf_op jit(solution)/shard_map/ppermute | solution.py:16
  78.0 1.9 %collective-permute-start.5 = (bf16[4,16,15,128]{3,2,0,1:T(8,128)(2,1)S(1)}, bf16[4,16,15,128]{3,2,0,1:T(8,128)(2,1)S(1)}, u32[]{:S(2)}, u32[]{:S(2)}) collective-permute-start(bf16[4,16,15,128]{3,2,0,1:T(8,128)(2,1)S(1)} %get-tuple-element.10), channel_id=1, source_target_pairs={{8,0},{16,8},{24,16},{32,24},{40,32},{48,40},{56,48},{64,56},{72,6... | collective-permute-start | bytes 737288 | tf_op jit(solution)/shard_map/ppermute | solution.py:17
  80.1 0.1 reshape.123
  80.2 2.7 %collective-permute-done.4 = bf16[4,16,15,128]{3,2,0,1:T(8,128)(2,1)S(1)} collective-permute-done((bf16[4,16,15,128]{3,2,0,1:T(8,128)(2,1)S(1)}, bf16[4,16,15,128]{3,2,0,1:T(8,128)(2,1)S(1)}, u32[]{:S(2)}, u32[]{:S(2)}) %collective-permute-start.4) | collective-permute-done | bytes 245792 | tf_op jit(solution)/shard_map/ppermute | solution.py:16
  82.9 6.5 %collective-permute-done.5 = bf16[4,16,15,128]{3,2,0,1:T(8,128)(2,1)S(1)} collective-permute-done((bf16[4,16,15,128]{3,2,0,1:T(8,128)(2,1)S(1)}, bf16[4,16,15,128]{3,2,0,1:T(8,128)(2,1)S(1)}, u32[]{:S(2)}, u32[]{:S(2)}) %collective-permute-start.5) | collective-permute-done | bytes 245792 | tf_op jit(solution)/shard_map/ppermute | solution.py:17
  89.4 0.5 fusion.19
  89.9 1.9 %collective-permute-start.6 = (f32[16,16,128]{2,1,0:T(8,128)S(1)}, f32[16,16,128]{2,1,0:T(8,128)S(1)}, u32[]{:S(2)}, u32[]{:S(2)}) collective-permute-start(f32[16,16,128]{2,1,0:T(8,128)S(1)} %fusion.19), channel_id=1, source_target_pairs={{0,512},{256,768},{512,0},{768,256},{1,513},{257,769},{513,1},{769... | collective-permute-start | bytes 393224 | tf_op jit(solution)/shard_map/ppermute | solution.py:146
  91.8 7.7 %collective-permute-done.6 = f32[16,16,128]{2,1,0:T(8,128)S(1)} collective-permute-done((f32[16,16,128]{2,1,0:T(8,128)S(1)}, f32[16,16,128]{2,1,0:T(8,128)S(1)}, u32[]{:S(2)}, u32[]{:S(2)}) %collective-permute-start.6) | collective-permute-done | bytes 131104 | tf_op jit(solution)/shard_map/ppermute | solution.py:146
  99.6 5.6 %collective-permute-start.7 = (bf16[16,15,128]{2,1,0:T(8,128)(2,1)S(1)}, bf16[16,15,128]{2,1,0:T(8,128)(2,1)S(1)}, u32[]{:S(2)}, u32[]{:S(2)}) collective-permute-start(bf16[16,15,128]{2,1,0:T(8,128)(2,1)S(1)} %get-tuple-element.11), channel_id=1, source_target_pairs={{0,8},{8,16},{16,24},{24,32},{32,40},{40,48},{48,56},{56,64},{64,7... | collective-permute-start | bytes 184328 | tf_op jit(solution)/shard_map/ppermute | solution.py:16
  105.2 1.9 %collective-permute-start.8 = (bf16[16,15,128]{2,1,0:T(8,128)(2,1)S(1)}, bf16[16,15,128]{2,1,0:T(8,128)(2,1)S(1)}, u32[]{:S(2)}, u32[]{:S(2)}) collective-permute-start(bf16[16,15,128]{2,1,0:T(8,128)(2,1)S(1)} %get-tuple-element.12), channel_id=1, source_target_pairs={{8,0},{16,8},{24,16},{32,24},{40,32},{48,40},{56,48},{64,56},{72,6... | collective-permute-start | bytes 184328 | tf_op jit(solution)/shard_map/ppermute | solution.py:17
  107.1 5.8 %collective-permute-done.8 = bf16[16,15,128]{2,1,0:T(8,128)(2,1)S(1)} collective-permute-done((bf16[16,15,128]{2,1,0:T(8,128)(2,1)S(1)}, bf16[16,15,128]{2,1,0:T(8,128)(2,1)S(1)}, u32[]{:S(2)}, u32[]{:S(2)}) %collective-permute-start.8) | collective-permute-done | bytes 61472 | tf_op jit(solution)/shard_map/ppermute | solution.py:17
  112.9 0.6 fusion.4
  113.5 0.2 copy.79
  113.7 0.2 reshape.128
  113.9 20.5 %all_to_all.25 = bf16[16,32,256]{2,1,0:T(8,128)(2,1)S(1)} all-to-all(bf16[16,32,256]{2,1,0:T(8,128)(2,1)S(1)} %reshape.128), channel_id=1, replica_groups={{0,1,2,3,4,5,6,7,256,257,258,259,260,261,262,263},{512,513,514,515,516,..., dimensions={0} | all-to-all | bytes 524288 | tf_op jit(solution)/shard_map/all_to_all | solution.py:94
  134.4 0.5 fusion.15
  134.9 14.4 %all_to_all.26 = bf16[16,32,256]{2,1,0:T(8,128)(2,1)S(1)} all-to-all(bf16[16,32,256]{2,1,0:T(8,128)(2,1)S(1)} %bitcast.216), channel_id=1, replica_groups={{0,1,2,3,4,5,6,7,256,257,258,259,260,261,262,263},{512,513,514,515,516,..., dimensions={0} | all-to-all | bytes 524288 | tf_op jit(solution)/shard_map/all_to_all | solution.py:94
  149.5 0.1 fusion.79
  149.6 1.9 %collective-permute-start.10 = (bf16[4,16,15,128]{3,2,0,1:T(8,128)(2,1)S(1)}, bf16[4,16,15,128]{3,2,0,1:T(8,128)(2,1)S(1)}, u32[]{:S(2)}, u32[]{:S(2)}) collective-permute-start(bf16[4,16,15,128]{3,2,0,1:T(8,128)(2,1)S(1)} %get-tuple-element.8), channel_id=1, source_target_pairs={{8,0},{16,8},{24,16},{32,24},{40,32},{48,40},{56,48},{64,56},{72,6... | collective-permute-start | bytes 737288 | tf_op jit(solution)/shard_map/ppermute | solution.py:17
  151.5 6.1 %collective-permute-start.9 = (bf16[4,16,15,128]{3,2,0,1:T(8,128)(2,1)S(1)}, bf16[4,16,15,128]{3,2,0,1:T(8,128)(2,1)S(1)}, u32[]{:S(2)}, u32[]{:S(2)}) collective-permute-start(bf16[4,16,15,128]{3,2,0,1:T(8,128)(2,1)S(1)} %get-tuple-element.7), channel_id=1, source_target_pairs={{0,8},{8,16},{16,24},{24,32},{32,40},{40,48},{48,56},{56,64},{64,7... | collective-permute-start | bytes 737288 | tf_op jit(solution)/shard_map/ppermute | solution.py:16
  157.6 3.8 %collective-permute-done.10 = bf16[4,16,15,128]{3,2,0,1:T(8,128)(2,1)S(1)} collective-permute-done((bf16[4,16,15,128]{3,2,0,1:T(8,128)(2,1)S(1)}, bf16[4,16,15,128]{3,2,0,1:T(8,128)(2,1)S(1)}, u32[]{:S(2)}, u32[]{:S(2)}) %collective-permute-start.10) | collective-permute-done | bytes 245792 | tf_op jit(solution)/shard_map/ppermute | solution.py:17
  161.4 8.4 %collective-permute-done.9 = bf16[4,16,15,128]{3,2,0,1:T(8,128)(2,1)S(1)} collective-permute-done((bf16[4,16,15,128]{3,2,0,1:T(8,128)(2,1)S(1)}, bf16[4,16,15,128]{3,2,0,1:T(8,128)(2,1)S(1)}, u32[]{:S(2)}, u32[]{:S(2)}) %collective-permute-start.9) | collective-permute-done | bytes 245792 | tf_op jit(solution)/shard_map/ppermute | solution.py:16
  169.7 0.5 fusion.18
  170.2 1.9 %collective-permute-start.11 = (f32[16,16,128]{2,1,0:T(8,128)S(1)}, f32[16,16,128]{2,1,0:T(8,128)S(1)}, u32[]{:S(2)}, u32[]{:S(2)}) collective-permute-start(f32[16,16,128]{2,1,0:T(8,128)S(1)} %fusion.18), channel_id=1, source_target_pairs={{0,512},{256,768},{512,0},{768,256},{1,513},{257,769},{513,1},{769... | collective-permute-start | bytes 393224 | tf_op jit(solution)/shard_map/ppermute | solution.py:146
  172.1 8.4 %collective-permute-done.11 = f32[16,16,128]{2,1,0:T(8,128)S(1)} collective-permute-done((f32[16,16,128]{2,1,0:T(8,128)S(1)}, f32[16,16,128]{2,1,0:T(8,128)S(1)}, u32[]{:S(2)}, u32[]{:S(2)}) %collective-permute-start.11) | collective-permute-done | bytes 131104 | tf_op jit(solution)/shard_map/ppermute | solution.py:146
  180.6 3.3 %collective-permute-start.12 = (f32[16,16,128]{2,1,0:T(8,128)S(1)}, f32[16,16,128]{2,1,0:T(8,128)S(1)}, u32[]{:S(2)}, u32[]{:S(2)}) collective-permute-start(f32[16,16,128]{2,1,0:T(8,128)S(1)} %multiply_multiply_fusion), channel_id=1, source_target_pairs={{0,256},{256,0},{512,768},{768,512},{1,257},{257,1},{513,769},{769... | collective-permute-start | bytes 393224 | tf_op jit(solution)/shard_map/ppermute | solution.py:148
  183.9 1.0 collective-permute-done.12
  184.8 0.7 maximum_select_fusion
  (95 shorter events, 3.2 us)
Async XLA Ops:
  0.0 12.7 %copy-start = (bf16[2,32,16,128]{3,2,1,0:T(8,128)(2,1)S(1)}, bf16[2,32,16,128]{3,2,1,0:T(8,128)(2,1)}, u32[]{:S(2)}) copy-start(bf16[2,32,16,128]{3,2,1,0:T(8,128)(2,1)} %param.6) | copy-start | bytes 786436
  0.0 31.1 %collective-permute-start.3 = (f32[2,31]{1,0:T(2,128)}, f32[2,31]{1,0:T(2,128)S(1)}, u32[]{:S(2)}, u32[]{:S(2)}) collective-permute-start(f32[2,31]{1,0:T(2,128)} %param.8), channel_id=1, source_target_pairs={{0,256},{256,0},{512,768},{768,512},{1,257},{257,1},{513,769},{769... | collective-permute-start | bytes 752 | tf_op jit(solution)/shard_map/ppermute | solution.py:64
  2.7 28.5 %collective-permute-start = (f32[2,31]{1,0:T(2,128)}, f32[2,31]{1,0:T(2,128)S(1)}, u32[]{:S(2)}, u32[]{:S(2)}) collective-permute-start(f32[2,31]{1,0:T(2,128)} %param.7), channel_id=1, source_target_pairs={{0,256},{256,0},{512,768},{768,512},{1,257},{257,1},{513,769},{769... | collective-permute-start | bytes 752 | tf_op jit(solution)/shard_map/ppermute | solution.py:64
  5.6 29.1 %collective-permute-start.1 = (bf16[16,15,128]{2,1,0:T(8,128)(2,1)S(1)}, bf16[16,15,128]{2,1,0:T(8,128)(2,1)S(1)}, u32[]{:S(2)}, u32[]{:S(2)}) collective-permute-start(bf16[16,15,128]{2,1,0:T(8,128)(2,1)S(1)} %get-tuple-element.13), channel_id=1, source_target_pairs={{0,8},{8,16},{16,24},{24,32},{32,40},{40,48},{48,56},{56,64},{64,7... | collective-permute-start | bytes 184328 | tf_op jit(solution)/shard_map/ppermute | solution.py:16
  10.8 24.0 %collective-permute-start.2 = (bf16[16,15,128]{2,1,0:T(8,128)(2,1)S(1)}, bf16[16,15,128]{2,1,0:T(8,128)(2,1)S(1)}, u32[]{:S(2)}, u32[]{:S(2)}) collective-permute-start(bf16[16,15,128]{2,1,0:T(8,128)(2,1)S(1)} %get-tuple-element.14), channel_id=1, source_target_pairs={{8,0},{16,8},{24,16},{32,24},{40,32},{48,40},{56,48},{64,56},{72,6... | collective-permute-start | bytes 184328 | tf_op jit(solution)/shard_map/ppermute | solution.py:17
  12.8 17.2 %copy-start.4 = (f32[2,121]{1,0:T(2,128)S(1)}, f32[2,121]{1,0:T(2,128)}, u32[]{:S(2)}) copy-start(f32[2,121]{1,0:T(2,128)} %param.9) | copy-start | bytes 2908
  13.6 26.7 %all-to-all-start = ((bf16[8,2,32,256]{3,2,1,0:T(8,128)(2,1)}), bf16[8,2,32,256]{3,2,1,0:T(8,128)(2,1)S(1)}, u32[]{:S(2)}, u32[]{:S(2)}) async-start(bf16[8,2,32,256]{3,2,1,0:T(8,128)(2,1)} %copy.35), calls=%async_computation | async-start | bytes 524288 | tf_op jit(solution)/shard_map/all_to_all | solution.py:112
  30.4 0.7 copy-start.2
  30.5 0.8 copy-start.3
  30.5 1.4 copy-start.5
  40.3 15.2 %all-to-all-start.1 = ((bf16[16,32,256]{2,1,0:T(8,128)(2,1)}), bf16[16,32,256]{2,1,0:T(8,128)(2,1)S(1)}, u32[]{:S(2)}, u32[]{:S(2)}) async-start(bf16[16,32,256]{2,1,0:T(8,128)(2,1)} %reshape.118), calls=%async_computation.1 | async-start | bytes 524288 | tf_op jit(solution)/shard_map/all_to_all | solution.py:94
  56.8 14.9 %all-to-all-start.2 = ((bf16[16,32,256]{2,1,0:T(8,128)(2,1)}), bf16[16,32,256]{2,1,0:T(8,128)(2,1)S(1)}, u32[]{:S(2)}, u32[]{:S(2)}) async-start(bf16[16,32,256]{2,1,0:T(8,128)(2,1)} %bitcast.38), calls=%async_computation.2 | async-start | bytes 524288 | tf_op jit(solution)/shard_map/all_to_all | solution.py:94
  72.0 11.0 %collective-permute-start.4 = (bf16[4,16,15,128]{3,2,0,1:T(8,128)(2,1)S(1)}, bf16[4,16,15,128]{3,2,0,1:T(8,128)(2,1)S(1)}, u32[]{:S(2)}, u32[]{:S(2)}) collective-permute-start(bf16[4,16,15,128]{3,2,0,1:T(8,128)(2,1)S(1)} %get-tuple-element.9), channel_id=1, source_target_pairs={{0,8},{8,16},{16,24},{24,32},{32,40},{40,48},{48,56},{56,64},{64,7... | collective-permute-start | bytes 737288 | tf_op jit(solution)/shard_map/ppermute | solution.py:16
  78.0 11.4 %collective-permute-start.5 = (bf16[4,16,15,128]{3,2,0,1:T(8,128)(2,1)S(1)}, bf16[4,16,15,128]{3,2,0,1:T(8,128)(2,1)S(1)}, u32[]{:S(2)}, u32[]{:S(2)}) collective-permute-start(bf16[4,16,15,128]{3,2,0,1:T(8,128)(2,1)S(1)} %get-tuple-element.10), channel_id=1, source_target_pairs={{8,0},{16,8},{24,16},{32,24},{40,32},{48,40},{56,48},{64,56},{72,6... | collective-permute-start | bytes 737288 | tf_op jit(solution)/shard_map/ppermute | solution.py:17
  80.2 19.3 %copy-start.1 = (f32[32,16,128]{2,1,0:T(8,128)S(1)}, f32[32,16,128]{2,1,0:T(8,128)}, u32[]{:S(2)}) copy-start(f32[32,16,128]{2,1,0:T(8,128)} %param.5) | copy-start | bytes 786436
  89.9 9.6 %collective-permute-start.6 = (f32[16,16,128]{2,1,0:T(8,128)S(1)}, f32[16,16,128]{2,1,0:T(8,128)S(1)}, u32[]{:S(2)}, u32[]{:S(2)}) collective-permute-start(f32[16,16,128]{2,1,0:T(8,128)S(1)} %fusion.19), channel_id=1, source_target_pairs={{0,512},{256,768},{512,0},{768,256},{1,513},{257,769},{513,1},{769... | collective-permute-start | bytes 393224 | tf_op jit(solution)/shard_map/ppermute | solution.py:146
  99.6 7.5 %collective-permute-start.7 = (bf16[16,15,128]{2,1,0:T(8,128)(2,1)S(1)}, bf16[16,15,128]{2,1,0:T(8,128)(2,1)S(1)}, u32[]{:S(2)}, u32[]{:S(2)}) collective-permute-start(bf16[16,15,128]{2,1,0:T(8,128)(2,1)S(1)} %get-tuple-element.11), channel_id=1, source_target_pairs={{0,8},{8,16},{16,24},{24,32},{32,40},{40,48},{48,56},{56,64},{64,7... | collective-permute-start | bytes 184328 | tf_op jit(solution)/shard_map/ppermute | solution.py:16
  105.2 7.7 %collective-permute-start.8 = (bf16[16,15,128]{2,1,0:T(8,128)(2,1)S(1)}, bf16[16,15,128]{2,1,0:T(8,128)(2,1)S(1)}, u32[]{:S(2)}, u32[]{:S(2)}) collective-permute-start(bf16[16,15,128]{2,1,0:T(8,128)(2,1)S(1)} %get-tuple-element.12), channel_id=1, source_target_pairs={{8,0},{16,8},{24,16},{32,24},{40,32},{48,40},{56,48},{64,56},{72,6... | collective-permute-start | bytes 184328 | tf_op jit(solution)/shard_map/ppermute | solution.py:17
  149.6 11.8 %collective-permute-start.10 = (bf16[4,16,15,128]{3,2,0,1:T(8,128)(2,1)S(1)}, bf16[4,16,15,128]{3,2,0,1:T(8,128)(2,1)S(1)}, u32[]{:S(2)}, u32[]{:S(2)}) collective-permute-start(bf16[4,16,15,128]{3,2,0,1:T(8,128)(2,1)S(1)} %get-tuple-element.8), channel_id=1, source_target_pairs={{8,0},{16,8},{24,16},{32,24},{40,32},{48,40},{56,48},{64,56},{72,6... | collective-permute-start | bytes 737288 | tf_op jit(solution)/shard_map/ppermute | solution.py:17
  151.5 18.2 %collective-permute-start.9 = (bf16[4,16,15,128]{3,2,0,1:T(8,128)(2,1)S(1)}, bf16[4,16,15,128]{3,2,0,1:T(8,128)(2,1)S(1)}, u32[]{:S(2)}, u32[]{:S(2)}) collective-permute-start(bf16[4,16,15,128]{3,2,0,1:T(8,128)(2,1)S(1)} %get-tuple-element.7), channel_id=1, source_target_pairs={{0,8},{8,16},{16,24},{24,32},{32,40},{40,48},{48,56},{56,64},{64,7... | collective-permute-start | bytes 737288 | tf_op jit(solution)/shard_map/ppermute | solution.py:16
  170.2 10.4 %collective-permute-start.11 = (f32[16,16,128]{2,1,0:T(8,128)S(1)}, f32[16,16,128]{2,1,0:T(8,128)S(1)}, u32[]{:S(2)}, u32[]{:S(2)}) collective-permute-start(f32[16,16,128]{2,1,0:T(8,128)S(1)} %fusion.18), channel_id=1, source_target_pairs={{0,512},{256,768},{512,0},{768,256},{1,513},{257,769},{513,1},{769... | collective-permute-start | bytes 393224 | tf_op jit(solution)/shard_map/ppermute | solution.py:146
  180.6 4.2 %collective-permute-start.12 = (f32[16,16,128]{2,1,0:T(8,128)S(1)}, f32[16,16,128]{2,1,0:T(8,128)S(1)}, u32[]{:S(2)}, u32[]{:S(2)}) collective-permute-start(f32[16,16,128]{2,1,0:T(8,128)S(1)} %multiply_multiply_fusion), channel_id=1, source_target_pairs={{0,256},{256,0},{512,768},{768,512},{1,257},{257,1},{513,769},{769... | collective-permute-start | bytes 393224 | tf_op jit(solution)/shard_map/ppermute | solution.py:148

commit v6 on v5

--- a/solution.py
+++ b/solution.py
@@ -45,8 +45,6 @@
     radius_ax = kernel_axial.shape[1] // 2
     framed_rows = height + 2 * radius_lat
     half = planes_local // 2
-    pair = height // blocks
-    column_width = pair * across
     core_bit = lax.axis_index("view") % 2
     to_core = [(i, i ^ 1) for i in range(view_size)]
     to_far = [(i, i ^ 2) for i in range(view_size)]
@@ -65,7 +63,7 @@
 
     chip_x = chip_taps(kernel_xdir)
     chip_y = chip_taps(kernel_ydir)
-    taps_axial = normalized(kernel_axial)
+    chip_z = chip_taps(kernel_axial)
     chip_count = chip_x.shape[0]
     bands_x = jnp.stack(
         [toeplitz_band(chip_x[member], across, across, radius_lat) for member in range(chip_count)]
@@ -81,11 +79,11 @@
     )
     bands_z = jnp.stack(
         [
-            toeplitz_band(taps_axial[member], planes, planes, radius_ax)
-            for member in range(view_count)
+            toeplitz_band(chip_z[member], planes, planes, radius_ax)
+            for member in range(chip_count)
         ]
     )
-    bands_z = bands_z.reshape(view_count, planes, blocks, 2, half)
+    bands_z = bands_z.reshape(chip_count, planes, blocks, 2, half)
 
     def framed(field):
         return extended(field, (("row", 2),), radius_lat)
@@ -95,54 +93,63 @@
             chunks, ("view", "col"), 0, 0, axis_index_groups=groups, tiled=True
         )
 
-    def to_columns(field):
-        chunks = field.reshape(2, view_count, half, blocks, pair, across)
-        chunks = chunks.transpose(0, 3, 1, 2, 4, 5).reshape(group, view_count * half, column_width)
+    def by_row(field):
+        lead, depth = field.shape[0], field.shape[1]
+        chunks = field.reshape(lead, depth, blocks, 2, across).transpose(3, 2, 0, 1, 4)
+        return chunks.reshape(group, lead * depth, across)
+
+    def to_columns(lateral, own_views):
+        chunks = by_row(lateral)
+        width = chunks.shape[1]
+        if own_views is not None:
+            chunks = jnp.concatenate([chunks, by_row(own_views)], axis=1)
         gathered = chip_exchange(chunks)
-        return gathered.reshape(2, blocks, view_count, half, column_width)
+        columns = gathered[:, :width].reshape(2, blocks, chip_count, half, across)
+        if own_views is None:
+            return columns, None
+        placed = gathered[:, width:].reshape(2, blocks, view_count, planes_local, across)
+        placed = placed.transpose(0, 2, 1, 3, 4).reshape(chip_count, planes, across)
+        return columns, placed
 
-    def to_slabs(columns):
-        chunks = columns.reshape(view_count, blocks, 2, half, column_width)
-        chunks = chunks.transpose(2, 1, 0, 3, 4).reshape(group, view_count * half, column_width)
-        spread = chip_exchange(chunks)
-        spread = spread.reshape(2, blocks, view_count, half, pair, across)
-        spread = spread.transpose(0, 2, 3, 1, 4, 5)
+    def to_slabs(returned):
+        spread = chip_exchange(returned.reshape(group, chip_count * half, across))
+        spread = spread.reshape(2, blocks, chip_count, half, across).transpose(2, 3, 1, 0, 4)
         return spread.reshape(chip_count, half, height, across)
 
-    own = lax.all_to_all(
-        views.reshape(view_count, planes_local, blocks, column_width).transpose(2, 0, 1, 3),
-        "col",
-        0,
-        0,
-        tiled=True,
-    )
-    view_columns = own.transpose(1, 0, 2, 3).reshape(view_count, planes, column_width)
-
-    def correct(coarse_framed):
+    def correct(coarse_framed, view_columns):
         smeared = jnp.einsum(
             "zyj,vij->vzyi", coarse_framed, bands_x, preferred_element_type=jnp.float32
         ).astype(jnp.bfloat16)
         lateral = jnp.einsum(
             "vij,vzjx->vzix", bands_y, smeared, preferred_element_type=jnp.float32
         ).astype(jnp.bfloat16)
-        columns = to_columns(lateral)
+        if view_columns is None:
+            columns, view_columns = to_columns(lateral, views)
+        else:
+            columns, _ = to_columns(lateral, None)
         blurred = jnp.einsum(
             "vicbz,bcvzm->vim", bands_z, columns, preferred_element_type=jnp.float32
         )
         quotient = (view_columns / blurred).astype(jnp.bfloat16)
         returned = jnp.einsum(
-            "vicbz,vim->vcbzm", bands_z, quotient, preferred_element_type=jnp.float32
+            "vicbz,vim->bcvzm", bands_z, quotient, preferred_element_type=jnp.float32
         ).astype(jnp.bfloat16)
         backward = jnp.einsum(
             "vij,vzjx->vzix", bands_yback, framed(to_slabs(returned)),
             preferred_element_type=jnp.float32,
         ).astype(jnp.bfloat16)
-        return jnp.einsum("vzyi,vij->zyj", backward, bands_x, preferred_element_type=jnp.float32)
+        corrected = jnp.einsum(
+            "vzyi,vij->zyj", backward, bands_x, preferred_element_type=jnp.float32
+        )
+        return corrected, view_columns
 
     restored_mine = lax.dynamic_slice_in_dim(estimate, core_bit * half, half, axis=0)
+    view_columns = None
     for iteration in range(ITERS):
         coarse_mine = restored_mine.astype(jnp.bfloat16)
-        accumulated = correct(extended(coarse_mine, (("row", 1),), radius_lat))
+        accumulated, view_columns = correct(
+            extended(coarse_mine, (("row", 1),), radius_lat), view_columns
+        )
         summed = accumulated + lax.ppermute(accumulated, "view", to_far)
         restored_mine = restored_mine * summed / total_views
     return joined(restored_mine, lax.ppermute(restored_mine, "view", to_core))

time: 188 us -> 183 us (0.973); the launches traced: 186 us -> 182 us
  waiting for transfers between devices: 65.7 us -> 60.3 us
    all_to_all x1 -> x0, starting transfers between devices: 16.4 us -> none  [on_device(): lax.all_to_all(views.reshape(view_count, planes_local, blocks, column_wid...]
    all_to_all x2, starting transfers between devices: 11.1 us -> 22.4 us  [chip_exchange(): lax.all_to_all(chunks, ('view', 'col'), 0, 0, axis_index_groups=groups, t...]
    ppermute x1, starting transfers between devices: 3.26 us -> 9.43 us  [on_device(): return joined(restored_mine, lax.ppermute(restored_mine, 'view', to_core))]
    ppermute x4, waiting for transfers between devices: 11.1 us -> 6.38 us  [extended(): before = lax.ppermute(last, axis, up)]
    ppermute x4, starting transfers between devices: 22.8 us -> 18.8 us  [extended(): before = lax.ppermute(last, axis, up)]
    all_to_all x1 -> x0, waiting for transfers between devices: 3.87 us -> none  [on_device(): lax.all_to_all(views.reshape(view_count, planes_local, blocks, column_wid...]
    all_to_all x2, waiting for transfers between devices: 17.6 us -> 20.7 us  [chip_exchange(): lax.all_to_all(chunks, ('view', 'col'), 0, 0, axis_index_groups=groups, t...]
    ppermute x2 -> x3, starting transfers between devices: 4.63 us -> 7.32 us  [chip_taps(): return normalized(joined(kernel, lax.ppermute(kernel, 'view', to_core)))]
  transfers between devices with their start and end apart: 16 -> 16, of which waited for: 11 -> 10; matrix products, arithmetic and copies ran while one was open for 5% -> 5% of each run, Pallas kernels for 0% -> 0%
where the time goes in v6:
time: 183 us; the launch traced here: 182 us
  starting transfers between devices  70.9 us (39%)
  waiting for transfers between devices  60.3 us (33%)
  blocking collectives  34.9 us (19%)
  local copies, waits for them, and re-layouts  9.83 us (5%)
  matrix products  3.25 us (2%)
  other arithmetic  2.43 us (1%)
    all_to_all x2, blocking collectives, chip_exchange(): lax.all_to_all(chunks, ('view', 'col'), 0, 0, axis_index_groups=groups, t...  34.9 us
    all_to_all x2, starting transfers between devices, chip_exchange(): lax.all_to_all(chunks, ('view', 'col'), 0, 0, axis_index_groups=groups, t...  22.4 us
    all_to_all x2, waiting for transfers between devices, chip_exchange(): lax.all_to_all(chunks, ('view', 'col'), 0, 0, axis_index_groups=groups, t...  20.7 us
    ppermute x4, starting transfers between devices, extended(): before = lax.ppermute(last, axis, up)  18.8 us
    ppermute x4, waiting for transfers between devices, extended(): after = lax.ppermute(initial, axis, down)  16.9 us
    ppermute x2, waiting for transfers between devices, on_device(): summed = accumulated + lax.ppermute(accumulated, 'view', to_far)  15.4 us
    ppermute x1, starting transfers between devices, on_device(): return joined(restored_mine, lax.ppermute(restored_mine, 'view', to_core))  9.43 us
    ppermute x4, starting transfers between devices, extended(): after = lax.ppermute(initial, axis, down)  9.12 us
  transfers between devices with their start and end apart: 16, of which 10 were waited for; matrix products, arithmetic and copies ran while one was open for 5% of the time, Pallas kernels for 0%

profile of v6, /device:TPU:113, one launch (start us, length us, event | category | flops | bytes accessed | tf_op | source)
XLA Modules:
  0.0 182.4 jit_solution(11924846813988624150)
XLA Ops:
  0.0 2.7 %collective-permute-start.3 = (f32[2,31]{1,0:T(2,128)}, f32[2,31]{1,0:T(2,128)S(1)}, u32[]{:S(2)}, u32[]{:S(2)}) collective-permute-start(f32[2,31]{1,0:T(2,128)} %param.8), channel_id=1, source_target_pairs={{0,256},{256,0},{512,768},{768,512},{1,257},{257,1},{513,769},{769... | collective-permute-start | bytes 752 | tf_op jit(solution)/shard_map/ppermute | solution.py:62
  2.7 1.9 %collective-permute-start = (f32[2,31]{1,0:T(2,128)}, f32[2,31]{1,0:T(2,128)S(1)}, u32[]{:S(2)}, u32[]{:S(2)}) collective-permute-start(f32[2,31]{1,0:T(2,128)} %param.7), channel_id=1, source_target_pairs={{0,256},{256,0},{512,768},{768,512},{1,257},{257,1},{513,769},{769... | collective-permute-start | bytes 752 | tf_op jit(solution)/shard_map/ppermute | solution.py:62
  4.7 0.9 dynamic-slice_convert_fusion
  5.6 5.1 %collective-permute-start.1 = (bf16[16,15,128]{2,1,0:T(8,128)(2,1)S(1)}, bf16[16,15,128]{2,1,0:T(8,128)(2,1)S(1)}, u32[]{:S(2)}, u32[]{:S(2)}) collective-permute-start(bf16[16,15,128]{2,1,0:T(8,128)(2,1)S(1)} %get-tuple-element.15), channel_id=1, source_target_pairs={{0,8},{8,16},{16,24},{24,32},{32,40},{40,48},{48,56},{56,64},{64,7... | collective-permute-start | bytes 184328 | tf_op jit(solution)/shard_map/ppermute | solution.py:16
  10.8 1.9 %collective-permute-start.2 = (bf16[16,15,128]{2,1,0:T(8,128)(2,1)S(1)}, bf16[16,15,128]{2,1,0:T(8,128)(2,1)S(1)}, u32[]{:S(2)}, u32[]{:S(2)}) collective-permute-start(bf16[16,15,128]{2,1,0:T(8,128)(2,1)S(1)} %get-tuple-element.16), channel_id=1, source_target_pairs={{8,0},{16,8},{24,16},{32,24},{40,32},{48,40},{56,48},{64,56},{72,6... | collective-permute-start | bytes 184328 | tf_op jit(solution)/shard_map/ppermute | solution.py:17
  12.7 2.7 %collective-permute-start.4 = (f32[2,121]{1,0:T(2,128)}, f32[2,121]{1,0:T(2,128)S(1)}, u32[]{:S(2)}, u32[]{:S(2)}) collective-permute-start(f32[2,121]{1,0:T(2,128)} %param.9), channel_id=1, source_target_pairs={{0,256},{256,0},{512,768},{768,512},{1,257},{257,1},{513,769},{769... | collective-permute-start | bytes 2912 | tf_op jit(solution)/shard_map/ppermute | solution.py:62
  15.5 0.5 copy-done.2
  16.1 0.1 fusion.64
  16.2 0.1 fusion.65
  16.9 0.1 reshape.129
  17.2 0.1 reshape.128
  17.4 0.1 reshape.131
  17.6 0.1 reshape.130
  17.9 0.3 reshape.127
  18.4 0.3 reshape.126
  18.9 0.3 reshape.125
  19.3 0.3 reshape.124
  19.7 0.1 fusion.66
  20.1 0.6 fusion.5
  20.7 0.8 pad_maximum_fusion.1
  21.6 17.0 %all-to-all-start = ((bf16[16,128,128]{2,1,0:T(8,128)(2,1)}), bf16[16,128,128]{2,1,0:T(8,128)(2,1)S(1)}, u32[]{:S(2)}, u32[]{:S(2)}) async-start(bf16[16,128,128]{2,1,0:T(8,128)(2,1)} %pad_maximum_fusion.1), calls=%async_computation | async-start | bytes 1048576 | tf_op jit(solution)/shard_map/all_to_all | solution.py:92
  38.6 0.1 copy.66
  38.7 0.4 reshape.136
  39.3 0.1 copy.67
  39.4 0.4 reshape.137
  40.1 0.1 copy.68
  40.2 0.4 reshape.138
  40.9 0.1 copy.69
  41.0 0.4 reshape.139
  41.7 11.7 %all-to-all-done = bf16[16,128,128]{2,1,0:T(8,128)(2,1)S(1)} async-done(((bf16[16,128,128]{2,1,0:T(8,128)(2,1)}), bf16[16,128,128]{2,1,0:T(8,128)(2,1)S(1)}, u32[]{:S(2)}, u32[]{:S(2)}) %all-to-all-start) | async-done | bytes 524320 | tf_op jit(solution)/shard_map/all_to_all | solution.py:92
  53.5 0.6 fusion.15
  54.1 0.7 copy.47
  54.9 5.4 %all-to-all-start.1 = ((bf16[16,64,128]{2,1,0:T(8,128)(2,1)}), bf16[16,64,128]{2,1,0:T(8,128)(2,1)S(1)}, u32[]{:S(2)}, u32[]{:S(2)}) async-start(bf16[16,64,128]{2,1,0:T(8,128)(2,1)} %bitcast.46), calls=%async_computation.1 | async-start | bytes 524288 | tf_op jit(solution)/shard_map/all_to_all | solution.py:92
  60.4 0.1 reshape.147
  60.6 0.1 reshape.146
  60.8 0.1 reshape.145
  60.9 9.0 %all-to-all-done.1 = bf16[16,64,128]{2,1,0:T(8,128)(2,1)S(1)} async-done(((bf16[16,64,128]{2,1,0:T(8,128)(2,1)}), bf16[16,64,128]{2,1,0:T(8,128)(2,1)S(1)}, u32[]{:S(2)}, u32[]{:S(2)}) %all-to-all-start.1) | async-done | bytes 262176 | tf_op jit(solution)/shard_map/all_to_all | solution.py:92
  70.1 0.1 fusion.78
  70.2 6.2 %collective-permute-start.5 = (bf16[4,16,15,128]{3,2,0,1:T(8,128)(2,1)S(1)}, bf16[4,16,15,128]{3,2,0,1:T(8,128)(2,1)S(1)}, u32[]{:S(2)}, u32[]{:S(2)}) collective-permute-start(bf16[4,16,15,128]{3,2,0,1:T(8,128)(2,1)S(1)} %get-tuple-element.11), channel_id=1, source_target_pairs={{0,8},{8,16},{16,24},{24,32},{32,40},{40,48},{48,56},{56,64},{64,7... | collective-permute-start | bytes 737288 | tf_op jit(solution)/shard_map/ppermute | solution.py:16
  76.3 1.9 %collective-permute-start.6 = (bf16[4,16,15,128]{3,2,0,1:T(8,128)(2,1)S(1)}, bf16[4,16,15,128]{3,2,0,1:T(8,128)(2,1)S(1)}, u32[]{:S(2)}, u32[]{:S(2)}) collective-permute-start(bf16[4,16,15,128]{3,2,0,1:T(8,128)(2,1)S(1)} %get-tuple-element.12), channel_id=1, source_target_pairs={{8,0},{16,8},{24,16},{32,24},{40,32},{48,40},{56,48},{64,56},{72,6... | collective-permute-start | bytes 737288 | tf_op jit(solution)/shard_map/ppermute | solution.py:17
  78.4 0.1 reshape.144
  78.5 2.7 %collective-permute-done.5 = bf16[4,16,15,128]{3,2,0,1:T(8,128)(2,1)S(1)} collective-permute-done((bf16[4,16,15,128]{3,2,0,1:T(8,128)(2,1)S(1)}, bf16[4,16,15,128]{3,2,0,1:T(8,128)(2,1)S(1)}, u32[]{:S(2)}, u32[]{:S(2)}) %collective-permute-start.5) | collective-permute-done | bytes 245792 | tf_op jit(solution)/shard_map/ppermute | solution.py:16
  81.2 6.5 %collective-permute-done.6 = bf16[4,16,15,128]{3,2,0,1:T(8,128)(2,1)S(1)} collective-permute-done((bf16[4,16,15,128]{3,2,0,1:T(8,128)(2,1)S(1)}, bf16[4,16,15,128]{3,2,0,1:T(8,128)(2,1)S(1)}, u32[]{:S(2)}, u32[]{:S(2)}) %collective-permute-start.6) | collective-permute-done | bytes 245792 | tf_op jit(solution)/shard_map/ppermute | solution.py:17
  87.7 0.5 fusion.17
  88.2 1.9 %collective-permute-start.7 = (f32[16,16,128]{2,1,0:T(8,128)S(1)}, f32[16,16,128]{2,1,0:T(8,128)S(1)}, u32[]{:S(2)}, u32[]{:S(2)}) collective-permute-start(f32[16,16,128]{2,1,0:T(8,128)S(1)} %fusion.17), channel_id=1, source_target_pairs={{0,512},{256,768},{512,0},{768,256},{1,513},{257,769},{513,1},{769... | collective-permute-start | bytes 393224 | tf_op jit(solution)/shard_map/ppermute | solution.py:153
  90.1 7.7 %collective-permute-done.7 = f32[16,16,128]{2,1,0:T(8,128)S(1)} collective-permute-done((f32[16,16,128]{2,1,0:T(8,128)S(1)}, f32[16,16,128]{2,1,0:T(8,128)S(1)}, u32[]{:S(2)}, u32[]{:S(2)}) %collective-permute-start.7) | collective-permute-done | bytes 131104 | tf_op jit(solution)/shard_map/ppermute | solution.py:153
  97.9 5.6 %collective-permute-start.8 = (bf16[16,15,128]{2,1,0:T(8,128)(2,1)S(1)}, bf16[16,15,128]{2,1,0:T(8,128)(2,1)S(1)}, u32[]{:S(2)}, u32[]{:S(2)}) collective-permute-start(bf16[16,15,128]{2,1,0:T(8,128)(2,1)S(1)} %get-tuple-element.13), channel_id=1, source_target_pairs={{0,8},{8,16},{16,24},{24,32},{32,40},{40,48},{48,56},{56,64},{64,7... | collective-permute-start | bytes 184328 | tf_op jit(solution)/shard_map/ppermute | solution.py:16
  103.5 1.9 %collective-permute-start.9 = (bf16[16,15,128]{2,1,0:T(8,128)(2,1)S(1)}, bf16[16,15,128]{2,1,0:T(8,128)(2,1)S(1)}, u32[]{:S(2)}, u32[]{:S(2)}) collective-permute-start(bf16[16,15,128]{2,1,0:T(8,128)(2,1)S(1)} %get-tuple-element.14), channel_id=1, source_target_pairs={{8,0},{16,8},{24,16},{32,24},{40,32},{48,40},{56,48},{64,56},{72,6... | collective-permute-start | bytes 184328 | tf_op jit(solution)/shard_map/ppermute | solution.py:17
  105.4 5.8 %collective-permute-done.9 = bf16[16,15,128]{2,1,0:T(8,128)(2,1)S(1)} collective-permute-done((bf16[16,15,128]{2,1,0:T(8,128)(2,1)S(1)}, bf16[16,15,128]{2,1,0:T(8,128)(2,1)S(1)}, u32[]{:S(2)}, u32[]{:S(2)}) %collective-permute-start.9) | collective-permute-done | bytes 61472 | tf_op jit(solution)/shard_map/ppermute | solution.py:17
  111.2 0.6 fusion.4
  111.9 20.5 %all_to_all.20 = bf16[16,64,128]{2,1,0:T(8,128)(2,1)S(1)} all-to-all(bf16[16,64,128]{2,1,0:T(8,128)(2,1)S(1)} %bitcast.225), channel_id=1, replica_groups={{0,1,2,3,4,5,6,7,256,257,258,259,260,261,262,263},{512,513,514,515,516,..., dimensions={0} | all-to-all | bytes 524288 | tf_op jit(solution)/shard_map/all_to_all | solution.py:92
  132.4 0.6 fusion.14
  133.0 14.4 %all_to_all.21 = bf16[16,64,128]{2,1,0:T(8,128)(2,1)S(1)} all-to-all(bf16[16,64,128]{2,1,0:T(8,128)(2,1)S(1)} %bitcast.226), channel_id=1, replica_groups={{0,1,2,3,4,5,6,7,256,257,258,259,260,261,262,263},{512,513,514,515,516,..., dimensions={0} | all-to-all | bytes 524288 | tf_op jit(solution)/shard_map/all_to_all | solution.py:92
  147.5 0.1 fusion.77
  147.6 1.9 %collective-permute-start.10 = (bf16[4,16,15,128]{3,2,0,1:T(8,128)(2,1)S(1)}, bf16[4,16,15,128]{3,2,0,1:T(8,128)(2,1)S(1)}, u32[]{:S(2)}, u32[]{:S(2)}) collective-permute-start(bf16[4,16,15,128]{3,2,0,1:T(8,128)(2,1)S(1)} %get-tuple-element.9), channel_id=1, source_target_pairs={{0,8},{8,16},{16,24},{24,32},{32,40},{40,48},{48,56},{56,64},{64,7... | collective-permute-start | bytes 737288 | tf_op jit(solution)/shard_map/ppermute | solution.py:16
  149.5 3.4 %collective-permute-start.11 = (bf16[4,16,15,128]{3,2,0,1:T(8,128)(2,1)S(1)}, bf16[4,16,15,128]{3,2,0,1:T(8,128)(2,1)S(1)}, u32[]{:S(2)}, u32[]{:S(2)}) collective-permute-start(bf16[4,16,15,128]{3,2,0,1:T(8,128)(2,1)S(1)} %get-tuple-element.10), channel_id=1, source_target_pairs={{8,0},{16,8},{24,16},{32,24},{40,32},{48,40},{56,48},{64,56},{72,6... | collective-permute-start | bytes 737288 | tf_op jit(solution)/shard_map/ppermute | solution.py:17
  152.9 3.6 %collective-permute-done.10 = bf16[4,16,15,128]{3,2,0,1:T(8,128)(2,1)S(1)} collective-permute-done((bf16[4,16,15,128]{3,2,0,1:T(8,128)(2,1)S(1)}, bf16[4,16,15,128]{3,2,0,1:T(8,128)(2,1)S(1)}, u32[]{:S(2)}, u32[]{:S(2)}) %collective-permute-start.10) | collective-permute-done | bytes 245792 | tf_op jit(solution)/shard_map/ppermute | solution.py:16
  156.6 4.6 %collective-permute-done.11 = bf16[4,16,15,128]{3,2,0,1:T(8,128)(2,1)S(1)} collective-permute-done((bf16[4,16,15,128]{3,2,0,1:T(8,128)(2,1)S(1)}, bf16[4,16,15,128]{3,2,0,1:T(8,128)(2,1)S(1)}, u32[]{:S(2)}, u32[]{:S(2)}) %collective-permute-start.11) | collective-permute-done | bytes 245792 | tf_op jit(solution)/shard_map/ppermute | solution.py:17
  161.2 0.5 fusion.16
  161.7 1.9 %collective-permute-start.12 = (f32[16,16,128]{2,1,0:T(8,128)S(1)}, f32[16,16,128]{2,1,0:T(8,128)S(1)}, u32[]{:S(2)}, u32[]{:S(2)}) collective-permute-start(f32[16,16,128]{2,1,0:T(8,128)S(1)} %fusion.16), channel_id=1, source_target_pairs={{0,512},{256,768},{512,0},{768,256},{1,513},{257,769},{513,1},{769... | collective-permute-start | bytes 393224 | tf_op jit(solution)/shard_map/ppermute | solution.py:153
  163.6 7.7 %collective-permute-done.12 = f32[16,16,128]{2,1,0:T(8,128)S(1)} collective-permute-done((f32[16,16,128]{2,1,0:T(8,128)S(1)}, f32[16,16,128]{2,1,0:T(8,128)S(1)}, u32[]{:S(2)}, u32[]{:S(2)}) %collective-permute-start.12) | collective-permute-done | bytes 131104 | tf_op jit(solution)/shard_map/ppermute | solution.py:153
  171.3 9.4 %collective-permute-start.13 = (f32[16,16,128]{2,1,0:T(8,128)S(1)}, f32[16,16,128]{2,1,0:T(8,128)S(1)}, u32[]{:S(2)}, u32[]{:S(2)}) collective-permute-start(f32[16,16,128]{2,1,0:T(8,128)S(1)} %multiply_multiply_fusion), channel_id=1, source_target_pairs={{0,256},{256,0},{512,768},{768,512},{1,257},{257,1},{513,769},{769... | collective-permute-start | bytes 393224 | tf_op jit(solution)/shard_map/ppermute | solution.py:155
  180.7 1.0 collective-permute-done.13
  181.7 0.7 maximum_select_fusion
  (109 shorter events, 3.7 us)
Async XLA Ops:
  0.0 15.4 %copy-start = (bf16[2,32,16,128]{3,2,1,0:T(8,128)(2,1)S(1)}, bf16[2,32,16,128]{3,2,1,0:T(8,128)(2,1)}, u32[]{:S(2)}) copy-start(bf16[2,32,16,128]{3,2,1,0:T(8,128)(2,1)} %param.6) | copy-start | bytes 786436
  0.0 15.5 %collective-permute-start.3 = (f32[2,31]{1,0:T(2,128)}, f32[2,31]{1,0:T(2,128)S(1)}, u32[]{:S(2)}, u32[]{:S(2)}) collective-permute-start(f32[2,31]{1,0:T(2,128)} %param.8), channel_id=1, source_target_pairs={{0,256},{256,0},{512,768},{768,512},{1,257},{257,1},{513,769},{769... | collective-permute-start | bytes 752 | tf_op jit(solution)/shard_map/ppermute | solution.py:62
  2.7 13.5 %collective-permute-start = (f32[2,31]{1,0:T(2,128)}, f32[2,31]{1,0:T(2,128)S(1)}, u32[]{:S(2)}, u32[]{:S(2)}) collective-permute-start(f32[2,31]{1,0:T(2,128)} %param.7), channel_id=1, source_target_pairs={{0,256},{256,0},{512,768},{768,512},{1,257},{257,1},{513,769},{769... | collective-permute-start | bytes 752 | tf_op jit(solution)/shard_map/ppermute | solution.py:62
  5.6 14.5 %collective-permute-start.1 = (bf16[16,15,128]{2,1,0:T(8,128)(2,1)S(1)}, bf16[16,15,128]{2,1,0:T(8,128)(2,1)S(1)}, u32[]{:S(2)}, u32[]{:S(2)}) collective-permute-start(bf16[16,15,128]{2,1,0:T(8,128)(2,1)S(1)} %get-tuple-element.15), channel_id=1, source_target_pairs={{0,8},{8,16},{16,24},{24,32},{32,40},{40,48},{48,56},{56,64},{64,7... | collective-permute-start | bytes 184328 | tf_op jit(solution)/shard_map/ppermute | solution.py:16
  10.8 9.3 %collective-permute-start.2 = (bf16[16,15,128]{2,1,0:T(8,128)(2,1)S(1)}, bf16[16,15,128]{2,1,0:T(8,128)(2,1)S(1)}, u32[]{:S(2)}, u32[]{:S(2)}) collective-permute-start(bf16[16,15,128]{2,1,0:T(8,128)(2,1)S(1)} %get-tuple-element.16), channel_id=1, source_target_pairs={{8,0},{16,8},{24,16},{32,24},{40,32},{48,40},{56,48},{64,56},{72,6... | collective-permute-start | bytes 184328 | tf_op jit(solution)/shard_map/ppermute | solution.py:17
  12.7 7.0 %collective-permute-start.4 = (f32[2,121]{1,0:T(2,128)}, f32[2,121]{1,0:T(2,128)S(1)}, u32[]{:S(2)}, u32[]{:S(2)}) collective-permute-start(f32[2,121]{1,0:T(2,128)} %param.9), channel_id=1, source_target_pairs={{0,256},{256,0},{512,768},{768,512},{1,257},{257,1},{513,769},{769... | collective-permute-start | bytes 2912 | tf_op jit(solution)/shard_map/ppermute | solution.py:62
  15.4 0.7 copy-start.2
  15.4 0.8 copy-start.3
  15.4 1.4 copy-start.5
  18.4 1.3 copy-start.4
  21.6 31.8 %all-to-all-start = ((bf16[16,128,128]{2,1,0:T(8,128)(2,1)}), bf16[16,128,128]{2,1,0:T(8,128)(2,1)S(1)}, u32[]{:S(2)}, u32[]{:S(2)}) async-start(bf16[16,128,128]{2,1,0:T(8,128)(2,1)} %pad_maximum_fusion.1), calls=%async_computation | async-start | bytes 1048576 | tf_op jit(solution)/shard_map/all_to_all | solution.py:92
  54.9 15.1 %all-to-all-start.1 = ((bf16[16,64,128]{2,1,0:T(8,128)(2,1)}), bf16[16,64,128]{2,1,0:T(8,128)(2,1)S(1)}, u32[]{:S(2)}, u32[]{:S(2)}) async-start(bf16[16,64,128]{2,1,0:T(8,128)(2,1)} %bitcast.46), calls=%async_computation.1 | async-start | bytes 524288 | tf_op jit(solution)/shard_map/all_to_all | solution.py:92
  70.2 11.1 %collective-permute-start.5 = (bf16[4,16,15,128]{3,2,0,1:T(8,128)(2,1)S(1)}, bf16[4,16,15,128]{3,2,0,1:T(8,128)(2,1)S(1)}, u32[]{:S(2)}, u32[]{:S(2)}) collective-permute-start(bf16[4,16,15,128]{3,2,0,1:T(8,128)(2,1)S(1)} %get-tuple-element.11), channel_id=1, source_target_pairs={{0,8},{8,16},{16,24},{24,32},{32,40},{40,48},{48,56},{56,64},{64,7... | collective-permute-start | bytes 737288 | tf_op jit(solution)/shard_map/ppermute | solution.py:16
  76.3 11.4 %collective-permute-start.6 = (bf16[4,16,15,128]{3,2,0,1:T(8,128)(2,1)S(1)}, bf16[4,16,15,128]{3,2,0,1:T(8,128)(2,1)S(1)}, u32[]{:S(2)}, u32[]{:S(2)}) collective-permute-start(bf16[4,16,15,128]{3,2,0,1:T(8,128)(2,1)S(1)} %get-tuple-element.12), channel_id=1, source_target_pairs={{8,0},{16,8},{24,16},{32,24},{40,32},{48,40},{56,48},{64,56},{72,6... | collective-permute-start | bytes 737288 | tf_op jit(solution)/shard_map/ppermute | solution.py:17
  78.5 19.3 %copy-start.1 = (f32[32,16,128]{2,1,0:T(8,128)S(1)}, f32[32,16,128]{2,1,0:T(8,128)}, u32[]{:S(2)}) copy-start(f32[32,16,128]{2,1,0:T(8,128)} %param.5) | copy-start | bytes 786436
  88.2 9.6 %collective-permute-start.7 = (f32[16,16,128]{2,1,0:T(8,128)S(1)}, f32[16,16,128]{2,1,0:T(8,128)S(1)}, u32[]{:S(2)}, u32[]{:S(2)}) collective-permute-start(f32[16,16,128]{2,1,0:T(8,128)S(1)} %fusion.17), channel_id=1, source_target_pairs={{0,512},{256,768},{512,0},{768,256},{1,513},{257,769},{513,1},{769... | collective-permute-start | bytes 393224 | tf_op jit(solution)/shard_map/ppermute | solution.py:153
  97.9 7.5 %collective-permute-start.8 = (bf16[16,15,128]{2,1,0:T(8,128)(2,1)S(1)}, bf16[16,15,128]{2,1,0:T(8,128)(2,1)S(1)}, u32[]{:S(2)}, u32[]{:S(2)}) collective-permute-start(bf16[16,15,128]{2,1,0:T(8,128)(2,1)S(1)} %get-tuple-element.13), channel_id=1, source_target_pairs={{0,8},{8,16},{16,24},{24,32},{32,40},{40,48},{48,56},{56,64},{64,7... | collective-permute-start | bytes 184328 | tf_op jit(solution)/shard_map/ppermute | solution.py:16
  103.5 7.7 %collective-permute-start.9 = (bf16[16,15,128]{2,1,0:T(8,128)(2,1)S(1)}, bf16[16,15,128]{2,1,0:T(8,128)(2,1)S(1)}, u32[]{:S(2)}, u32[]{:S(2)}) collective-permute-start(bf16[16,15,128]{2,1,0:T(8,128)(2,1)S(1)} %get-tuple-element.14), channel_id=1, source_target_pairs={{8,0},{16,8},{24,16},{32,24},{40,32},{48,40},{56,48},{64,56},{72,6... | collective-permute-start | bytes 184328 | tf_op jit(solution)/shard_map/ppermute | solution.py:17
  147.6 8.9 %collective-permute-start.10 = (bf16[4,16,15,128]{3,2,0,1:T(8,128)(2,1)S(1)}, bf16[4,16,15,128]{3,2,0,1:T(8,128)(2,1)S(1)}, u32[]{:S(2)}, u32[]{:S(2)}) collective-permute-start(bf16[4,16,15,128]{3,2,0,1:T(8,128)(2,1)S(1)} %get-tuple-element.9), channel_id=1, source_target_pairs={{0,8},{8,16},{16,24},{24,32},{32,40},{40,48},{48,56},{56,64},{64,7... | collective-permute-start | bytes 737288 | tf_op jit(solution)/shard_map/ppermute | solution.py:16
  149.5 11.6 %collective-permute-start.11 = (bf16[4,16,15,128]{3,2,0,1:T(8,128)(2,1)S(1)}, bf16[4,16,15,128]{3,2,0,1:T(8,128)(2,1)S(1)}, u32[]{:S(2)}, u32[]{:S(2)}) collective-permute-start(bf16[4,16,15,128]{3,2,0,1:T(8,128)(2,1)S(1)} %get-tuple-element.10), channel_id=1, source_target_pairs={{8,0},{16,8},{24,16},{32,24},{40,32},{48,40},{56,48},{64,56},{72,6... | collective-permute-start | bytes 737288 | tf_op jit(solution)/shard_map/ppermute | solution.py:17
  161.7 9.6 %collective-permute-start.12 = (f32[16,16,128]{2,1,0:T(8,128)S(1)}, f32[16,16,128]{2,1,0:T(8,128)S(1)}, u32[]{:S(2)}, u32[]{:S(2)}) collective-permute-start(f32[16,16,128]{2,1,0:T(8,128)S(1)} %fusion.16), channel_id=1, source_target_pairs={{0,512},{256,768},{512,0},{768,256},{1,513},{257,769},{513,1},{769... | collective-permute-start | bytes 393224 | tf_op jit(solution)/shard_map/ppermute | solution.py:153
  171.3 10.4 %collective-permute-start.13 = (f32[16,16,128]{2,1,0:T(8,128)S(1)}, f32[16,16,128]{2,1,0:T(8,128)S(1)}, u32[]{:S(2)}, u32[]{:S(2)}) collective-permute-start(f32[16,16,128]{2,1,0:T(8,128)S(1)} %multiply_multiply_fusion), channel_id=1, source_target_pairs={{0,256},{256,0},{512,768},{768,512},{1,257},{257,1},{513,769},{769... | collective-permute-start | bytes 393224 | tf_op jit(solution)/shard_map/ppermute | solution.py:155

commit v7 on v6

--- a/solution.py
+++ b/solution.py
@@ -58,12 +58,12 @@
             jnp.concatenate([theirs, mine], axis=0),
         )
 
-    def chip_taps(kernel):
-        return normalized(joined(kernel, lax.ppermute(kernel, "view", to_core)))
-
-    chip_x = chip_taps(kernel_xdir)
-    chip_y = chip_taps(kernel_ydir)
-    chip_z = chip_taps(kernel_axial)
+    own_taps = jnp.concatenate([kernel_xdir, kernel_ydir, kernel_axial], axis=1)
+    taps = joined(own_taps, lax.ppermute(own_taps, "view", to_core))
+    lateral_taps = kernel_xdir.shape[1]
+    chip_x = normalized(taps[:, :lateral_taps])
+    chip_y = normalized(taps[:, lateral_taps : 2 * lateral_taps])
+    chip_z = normalized(taps[:, 2 * lateral_taps :])
     chip_count = chip_x.shape[0]
     bands_x = jnp.stack(
         [toeplitz_band(chip_x[member], across, across, radius_lat) for member in range(chip_count)]

time: 183 us -> 179 us (0.978)
  starting transfers between devices: 70.9 us -> 65.4 us
    ppermute x3 -> x1, starting transfers between devices: 7.32 us -> 2.57 us  [on_device(): taps = joined(own_taps, lax.ppermute(own_taps, 'view', to_core))]
    ppermute x4, starting transfers between devices: 18.8 us -> 16.8 us  [extended(): before = lax.ppermute(last, axis, up)]
  transfers between devices with their start and end apart: 16 -> 14, of which waited for: 10 -> 11; matrix products, arithmetic and copies ran while one was open for 5% -> 5% of each run, Pallas kernels for 0% -> 0%
where the time goes in v7:
time: 179 us; the launch traced here: 178 us
  starting transfers between devices  65.4 us (37%)
  waiting for transfers between devices  61.5 us (34%)
  blocking collectives  34.3 us (19%)
  local copies, waits for them, and re-layouts  9.84 us (5%)
  other arithmetic  3.35 us (2%)
  matrix products  3.26 us (2%)
    all_to_all x2, blocking collectives, chip_exchange(): lax.all_to_all(chunks, ('view', 'col'), 0, 0, axis_index_groups=groups, t...  34.3 us
    all_to_all x2, starting transfers between devices, chip_exchange(): lax.all_to_all(chunks, ('view', 'col'), 0, 0, axis_index_groups=groups, t...  23.6 us
    all_to_all x2, waiting for transfers between devices, chip_exchange(): lax.all_to_all(chunks, ('view', 'col'), 0, 0, axis_index_groups=groups, t...  20.7 us
    ppermute x4, waiting for transfers between devices, extended(): after = lax.ppermute(initial, axis, down)  18.1 us
    ppermute x4, starting transfers between devices, extended(): before = lax.ppermute(last, axis, up)  16.8 us
    ppermute x2, waiting for transfers between devices, on_device(): summed = accumulated + lax.ppermute(accumulated, 'view', to_far)  15.4 us
    ppermute x1, starting transfers between devices, on_device(): return joined(restored_mine, lax.ppermute(restored_mine, 'view', to_core))  9.43 us
    ppermute x4, starting transfers between devices, extended(): after = lax.ppermute(initial, axis, down)  9.12 us
  transfers between devices with their start and end apart: 14, of which 11 were waited for; matrix products, arithmetic and copies ran while one was open for 5% of the time, Pallas kernels for 0%

profile of v7, /device:TPU:113, one launch (start us, length us, event | category | flops | bytes accessed | tf_op | source)
XLA Modules:
  0.0 178.4 jit_solution(5150442997266606204)
XLA Ops:
  0.0 0.8 pad_maximum_fusion.3
  0.8 2.6 %collective-permute-start = (f32[2,183]{1,0:T(2,128)S(1)}, f32[2,183]{1,0:T(2,128)S(1)}, u32[]{:S(2)}, u32[]{:S(2)}) collective-permute-start(f32[2,183]{1,0:T(2,128)S(1)} %pad_maximum_fusion.3), channel_id=1, source_target_pairs={{0,256},{256,0},{512,768},{768,512},{1,257},{257,1},{513,769},{769... | collective-permute-start | bytes 4400 | tf_op jit(solution)/shard_map/ppermute | solution.py:62
  3.4 0.9 dynamic-slice_convert_fusion
  4.4 5.1 %collective-permute-start.1 = (bf16[16,15,128]{2,1,0:T(8,128)(2,1)S(1)}, bf16[16,15,128]{2,1,0:T(8,128)(2,1)S(1)}, u32[]{:S(2)}, u32[]{:S(2)}) collective-permute-start(bf16[16,15,128]{2,1,0:T(8,128)(2,1)S(1)} %get-tuple-element.17), channel_id=1, source_target_pairs={{0,8},{8,16},{16,24},{24,32},{32,40},{40,48},{48,56},{56,64},{64,7... | collective-permute-start | bytes 184328 | tf_op jit(solution)/shard_map/ppermute | solution.py:16
  9.5 1.9 %collective-permute-start.2 = (bf16[16,15,128]{2,1,0:T(8,128)(2,1)S(1)}, bf16[16,15,128]{2,1,0:T(8,128)(2,1)S(1)}, u32[]{:S(2)}, u32[]{:S(2)}) collective-permute-start(bf16[16,15,128]{2,1,0:T(8,128)(2,1)S(1)} %get-tuple-element.18), channel_id=1, source_target_pairs={{8,0},{16,8},{24,16},{32,24},{40,32},{48,40},{56,48},{64,56},{72,6... | collective-permute-start | bytes 184328 | tf_op jit(solution)/shard_map/ppermute | solution.py:17
  11.6 0.5 copy-done.2
  12.3 0.2 slice_reduce_fusion.1
  12.4 0.2 slice_reduce_fusion.2
  13.2 0.1 reshape.129
  13.5 0.1 reshape.128
  13.7 0.1 reshape.131
  13.9 0.1 reshape.130
  14.2 0.3 reshape.127
  14.7 0.3 reshape.126
  15.1 0.3 reshape.125
  15.6 0.3 reshape.124
  16.2 1.0 collective-permute-done.2
  17.2 0.6 fusion.5
  17.9 0.9 pad_maximum_fusion.1
  18.7 18.1 %all-to-all-start = ((bf16[16,128,128]{2,1,0:T(8,128)(2,1)}), bf16[16,128,128]{2,1,0:T(8,128)(2,1)S(1)}, u32[]{:S(2)}, u32[]{:S(2)}) async-start(bf16[16,128,128]{2,1,0:T(8,128)(2,1)} %pad_maximum_fusion.1), calls=%async_computation | async-start | bytes 1048576 | tf_op jit(solution)/shard_map/all_to_all | solution.py:92
  36.9 0.1 copy.66
  37.0 0.4 reshape.136
  37.5 0.1 copy.41
  37.6 0.1 copy.67
  37.7 0.4 reshape.137
  38.4 0.1 copy.68
  38.5 0.4 reshape.138
  39.2 0.1 copy.69
  39.3 0.4 reshape.139
  40.0 11.7 %all-to-all-done = bf16[16,128,128]{2,1,0:T(8,128)(2,1)S(1)} async-done(((bf16[16,128,128]{2,1,0:T(8,128)(2,1)}), bf16[16,128,128]{2,1,0:T(8,128)(2,1)S(1)}, u32[]{:S(2)}, u32[]{:S(2)}) %all-to-all-start) | async-done | bytes 524320 | tf_op jit(solution)/shard_map/all_to_all | solution.py:92
  51.8 0.6 fusion.15
  52.4 0.7 copy.47
  53.2 5.4 %all-to-all-start.1 = ((bf16[16,64,128]{2,1,0:T(8,128)(2,1)}), bf16[16,64,128]{2,1,0:T(8,128)(2,1)S(1)}, u32[]{:S(2)}, u32[]{:S(2)}) async-start(bf16[16,64,128]{2,1,0:T(8,128)(2,1)} %bitcast.46), calls=%async_computation.1 | async-start | bytes 524288 | tf_op jit(solution)/shard_map/all_to_all | solution.py:92
  58.7 0.1 reshape.147
  58.9 0.1 reshape.146
  59.1 0.1 reshape.145
  59.2 9.0 %all-to-all-done.1 = bf16[16,64,128]{2,1,0:T(8,128)(2,1)S(1)} async-done(((bf16[16,64,128]{2,1,0:T(8,128)(2,1)}), bf16[16,64,128]{2,1,0:T(8,128)(2,1)S(1)}, u32[]{:S(2)}, u32[]{:S(2)}) %all-to-all-start.1) | async-done | bytes 262176 | tf_op jit(solution)/shard_map/all_to_all | solution.py:92
  68.3 0.1 fusion.75
  68.5 4.2 %collective-permute-start.3 = (bf16[4,16,15,128]{3,2,0,1:T(8,128)(2,1)S(1)}, bf16[4,16,15,128]{3,2,0,1:T(8,128)(2,1)S(1)}, u32[]{:S(2)}, u32[]{:S(2)}) collective-permute-start(bf16[4,16,15,128]{3,2,0,1:T(8,128)(2,1)S(1)} %get-tuple-element.13), channel_id=1, source_target_pairs={{0,8},{8,16},{16,24},{24,32},{32,40},{40,48},{48,56},{56,64},{64,7... | collective-permute-start | bytes 737288 | tf_op jit(solution)/shard_map/ppermute | solution.py:16
  72.7 1.9 %collective-permute-start.4 = (bf16[4,16,15,128]{3,2,0,1:T(8,128)(2,1)S(1)}, bf16[4,16,15,128]{3,2,0,1:T(8,128)(2,1)S(1)}, u32[]{:S(2)}, u32[]{:S(2)}) collective-permute-start(bf16[4,16,15,128]{3,2,0,1:T(8,128)(2,1)S(1)} %get-tuple-element.14), channel_id=1, source_target_pairs={{8,0},{16,8},{24,16},{32,24},{40,32},{48,40},{56,48},{64,56},{72,6... | collective-permute-start | bytes 737288 | tf_op jit(solution)/shard_map/ppermute | solution.py:17
  74.7 0.1 reshape.144
  74.8 2.7 %collective-permute-done.3 = bf16[4,16,15,128]{3,2,0,1:T(8,128)(2,1)S(1)} collective-permute-done((bf16[4,16,15,128]{3,2,0,1:T(8,128)(2,1)S(1)}, bf16[4,16,15,128]{3,2,0,1:T(8,128)(2,1)S(1)}, u32[]{:S(2)}, u32[]{:S(2)}) %collective-permute-start.3) | collective-permute-done | bytes 245792 | tf_op jit(solution)/shard_map/ppermute | solution.py:16
  77.6 6.5 %collective-permute-done.4 = bf16[4,16,15,128]{3,2,0,1:T(8,128)(2,1)S(1)} collective-permute-done((bf16[4,16,15,128]{3,2,0,1:T(8,128)(2,1)S(1)}, bf16[4,16,15,128]{3,2,0,1:T(8,128)(2,1)S(1)}, u32[]{:S(2)}, u32[]{:S(2)}) %collective-permute-start.4) | collective-permute-done | bytes 245792 | tf_op jit(solution)/shard_map/ppermute | solution.py:17
  84.0 0.5 fusion.17
  84.5 1.9 %collective-permute-start.5 = (f32[16,16,128]{2,1,0:T(8,128)S(1)}, f32[16,16,128]{2,1,0:T(8,128)S(1)}, u32[]{:S(2)}, u32[]{:S(2)}) collective-permute-start(f32[16,16,128]{2,1,0:T(8,128)S(1)} %fusion.17), channel_id=1, source_target_pairs={{0,512},{256,768},{512,0},{768,256},{1,513},{257,769},{513,1},{769... | collective-permute-start | bytes 393224 | tf_op jit(solution)/shard_map/ppermute | solution.py:153
  86.5 7.7 %collective-permute-done.5 = f32[16,16,128]{2,1,0:T(8,128)S(1)} collective-permute-done((f32[16,16,128]{2,1,0:T(8,128)S(1)}, f32[16,16,128]{2,1,0:T(8,128)S(1)}, u32[]{:S(2)}, u32[]{:S(2)}) %collective-permute-start.5) | collective-permute-done | bytes 131104 | tf_op jit(solution)/shard_map/ppermute | solution.py:153
  94.2 5.6 %collective-permute-start.6 = (bf16[16,15,128]{2,1,0:T(8,128)(2,1)S(1)}, bf16[16,15,128]{2,1,0:T(8,128)(2,1)S(1)}, u32[]{:S(2)}, u32[]{:S(2)}) collective-permute-start(bf16[16,15,128]{2,1,0:T(8,128)(2,1)S(1)} %get-tuple-element.15), channel_id=1, source_target_pairs={{0,8},{8,16},{16,24},{24,32},{32,40},{40,48},{48,56},{56,64},{64,7... | collective-permute-start | bytes 184328 | tf_op jit(solution)/shard_map/ppermute | solution.py:16
  99.8 1.9 %collective-permute-start.7 = (bf16[16,15,128]{2,1,0:T(8,128)(2,1)S(1)}, bf16[16,15,128]{2,1,0:T(8,128)(2,1)S(1)}, u32[]{:S(2)}, u32[]{:S(2)}) collective-permute-start(bf16[16,15,128]{2,1,0:T(8,128)(2,1)S(1)} %get-tuple-element.16), channel_id=1, source_target_pairs={{8,0},{16,8},{24,16},{32,24},{40,32},{48,40},{56,48},{64,56},{72,6... | collective-permute-start | bytes 184328 | tf_op jit(solution)/shard_map/ppermute | solution.py:17
  101.7 6.0 %collective-permute-done.7 = bf16[16,15,128]{2,1,0:T(8,128)(2,1)S(1)} collective-permute-done((bf16[16,15,128]{2,1,0:T(8,128)(2,1)S(1)}, bf16[16,15,128]{2,1,0:T(8,128)(2,1)S(1)}, u32[]{:S(2)}, u32[]{:S(2)}) %collective-permute-start.7) | collective-permute-done | bytes 61472 | tf_op jit(solution)/shard_map/ppermute | solution.py:17
  107.7 0.6 fusion.4
  108.4 19.9 %all_to_all.20 = bf16[16,64,128]{2,1,0:T(8,128)(2,1)S(1)} all-to-all(bf16[16,64,128]{2,1,0:T(8,128)(2,1)S(1)} %bitcast.225), channel_id=1, replica_groups={{0,1,2,3,4,5,6,7,256,257,258,259,260,261,262,263},{512,513,514,515,516,..., dimensions={0} | all-to-all | bytes 524288 | tf_op jit(solution)/shard_map/all_to_all | solution.py:92
  128.3 0.6 fusion.14
  128.9 14.4 %all_to_all.21 = bf16[16,64,128]{2,1,0:T(8,128)(2,1)S(1)} all-to-all(bf16[16,64,128]{2,1,0:T(8,128)(2,1)S(1)} %bitcast.226), channel_id=1, replica_groups={{0,1,2,3,4,5,6,7,256,257,258,259,260,261,262,263},{512,513,514,515,516,..., dimensions={0} | all-to-all | bytes 524288 | tf_op jit(solution)/shard_map/all_to_all | solution.py:92
  143.4 0.1 fusion.74
  143.5 1.9 %collective-permute-start.8 = (bf16[4,16,15,128]{3,2,0,1:T(8,128)(2,1)S(1)}, bf16[4,16,15,128]{3,2,0,1:T(8,128)(2,1)S(1)}, u32[]{:S(2)}, u32[]{:S(2)}) collective-permute-start(bf16[4,16,15,128]{3,2,0,1:T(8,128)(2,1)S(1)} %get-tuple-element.11), channel_id=1, source_target_pairs={{0,8},{8,16},{16,24},{24,32},{32,40},{40,48},{48,56},{56,64},{64,7... | collective-permute-start | bytes 737288 | tf_op jit(solution)/shard_map/ppermute | solution.py:16
  145.5 3.4 %collective-permute-start.9 = (bf16[4,16,15,128]{3,2,0,1:T(8,128)(2,1)S(1)}, bf16[4,16,15,128]{3,2,0,1:T(8,128)(2,1)S(1)}, u32[]{:S(2)}, u32[]{:S(2)}) collective-permute-start(bf16[4,16,15,128]{3,2,0,1:T(8,128)(2,1)S(1)} %get-tuple-element.12), channel_id=1, source_target_pairs={{8,0},{16,8},{24,16},{32,24},{40,32},{48,40},{56,48},{64,56},{72,6... | collective-permute-start | bytes 737288 | tf_op jit(solution)/shard_map/ppermute | solution.py:17
  148.8 3.6 %collective-permute-done.8 = bf16[4,16,15,128]{3,2,0,1:T(8,128)(2,1)S(1)} collective-permute-done((bf16[4,16,15,128]{3,2,0,1:T(8,128)(2,1)S(1)}, bf16[4,16,15,128]{3,2,0,1:T(8,128)(2,1)S(1)}, u32[]{:S(2)}, u32[]{:S(2)}) %collective-permute-start.8) | collective-permute-done | bytes 245792 | tf_op jit(solution)/shard_map/ppermute | solution.py:16
  152.5 4.6 %collective-permute-done.9 = bf16[4,16,15,128]{3,2,0,1:T(8,128)(2,1)S(1)} collective-permute-done((bf16[4,16,15,128]{3,2,0,1:T(8,128)(2,1)S(1)}, bf16[4,16,15,128]{3,2,0,1:T(8,128)(2,1)S(1)}, u32[]{:S(2)}, u32[]{:S(2)}) %collective-permute-start.9) | collective-permute-done | bytes 245792 | tf_op jit(solution)/shard_map/ppermute | solution.py:17
  157.1 0.5 fusion.16
  157.6 1.9 %collective-permute-start.10 = (f32[16,16,128]{2,1,0:T(8,128)S(1)}, f32[16,16,128]{2,1,0:T(8,128)S(1)}, u32[]{:S(2)}, u32[]{:S(2)}) collective-permute-start(f32[16,16,128]{2,1,0:T(8,128)S(1)} %fusion.16), channel_id=1, source_target_pairs={{0,512},{256,768},{512,0},{768,256},{1,513},{257,769},{513,1},{769... | collective-permute-start | bytes 393224 | tf_op jit(solution)/shard_map/ppermute | solution.py:153
  159.5 7.7 %collective-permute-done.10 = f32[16,16,128]{2,1,0:T(8,128)S(1)} collective-permute-done((f32[16,16,128]{2,1,0:T(8,128)S(1)}, f32[16,16,128]{2,1,0:T(8,128)S(1)}, u32[]{:S(2)}, u32[]{:S(2)}) %collective-permute-start.10) | collective-permute-done | bytes 131104 | tf_op jit(solution)/shard_map/ppermute | solution.py:153
  167.2 9.4 %collective-permute-start.11 = (f32[16,16,128]{2,1,0:T(8,128)S(1)}, f32[16,16,128]{2,1,0:T(8,128)S(1)}, u32[]{:S(2)}, u32[]{:S(2)}) collective-permute-start(f32[16,16,128]{2,1,0:T(8,128)S(1)} %multiply_multiply_fusion), channel_id=1, source_target_pairs={{0,256},{256,0},{512,768},{768,512},{1,257},{257,1},{513,769},{769... | collective-permute-start | bytes 393224 | tf_op jit(solution)/shard_map/ppermute | solution.py:155
  176.7 1.0 collective-permute-done.11
  177.6 0.7 maximum_select_fusion
  (105 shorter events, 3.7 us)
Async XLA Ops:
  0.0 11.5 %copy-start = (bf16[2,32,16,128]{3,2,1,0:T(8,128)(2,1)S(1)}, bf16[2,32,16,128]{3,2,1,0:T(8,128)(2,1)}, u32[]{:S(2)}) copy-start(bf16[2,32,16,128]{3,2,1,0:T(8,128)(2,1)} %param.6) | copy-start | bytes 786436
  0.8 10.8 %collective-permute-start = (f32[2,183]{1,0:T(2,128)S(1)}, f32[2,183]{1,0:T(2,128)S(1)}, u32[]{:S(2)}, u32[]{:S(2)}) collective-permute-start(f32[2,183]{1,0:T(2,128)S(1)} %pad_maximum_fusion.3), channel_id=1, source_target_pairs={{0,256},{256,0},{512,768},{768,512},{1,257},{257,1},{513,769},{769... | collective-permute-start | bytes 4400 | tf_op jit(solution)/shard_map/ppermute | solution.py:62
  4.4 11.8 %collective-permute-start.1 = (bf16[16,15,128]{2,1,0:T(8,128)(2,1)S(1)}, bf16[16,15,128]{2,1,0:T(8,128)(2,1)S(1)}, u32[]{:S(2)}, u32[]{:S(2)}) collective-permute-start(bf16[16,15,128]{2,1,0:T(8,128)(2,1)S(1)} %get-tuple-element.17), channel_id=1, source_target_pairs={{0,8},{8,16},{16,24},{24,32},{32,40},{40,48},{48,56},{56,64},{64,7... | collective-permute-start | bytes 184328 | tf_op jit(solution)/shard_map/ppermute | solution.py:16
  9.5 7.7 %collective-permute-start.2 = (bf16[16,15,128]{2,1,0:T(8,128)(2,1)S(1)}, bf16[16,15,128]{2,1,0:T(8,128)(2,1)S(1)}, u32[]{:S(2)}, u32[]{:S(2)}) collective-permute-start(bf16[16,15,128]{2,1,0:T(8,128)(2,1)S(1)} %get-tuple-element.18), channel_id=1, source_target_pairs={{8,0},{16,8},{24,16},{32,24},{40,32},{48,40},{56,48},{64,56},{72,6... | collective-permute-start | bytes 184328 | tf_op jit(solution)/shard_map/ppermute | solution.py:17
  11.5 0.7 copy-start.2
  11.5 0.7 copy-start.3
  11.5 0.7 copy-start.4
  11.5 1.6 copy-start.5
  18.7 32.9 %all-to-all-start = ((bf16[16,128,128]{2,1,0:T(8,128)(2,1)}), bf16[16,128,128]{2,1,0:T(8,128)(2,1)S(1)}, u32[]{:S(2)}, u32[]{:S(2)}) async-start(bf16[16,128,128]{2,1,0:T(8,128)(2,1)} %pad_maximum_fusion.1), calls=%async_computation | async-start | bytes 1048576 | tf_op jit(solution)/shard_map/all_to_all | solution.py:92
  53.2 15.1 %all-to-all-start.1 = ((bf16[16,64,128]{2,1,0:T(8,128)(2,1)}), bf16[16,64,128]{2,1,0:T(8,128)(2,1)S(1)}, u32[]{:S(2)}, u32[]{:S(2)}) async-start(bf16[16,64,128]{2,1,0:T(8,128)(2,1)} %bitcast.46), calls=%async_computation.1 | async-start | bytes 524288 | tf_op jit(solution)/shard_map/all_to_all | solution.py:92
  68.5 9.1 %collective-permute-start.3 = (bf16[4,16,15,128]{3,2,0,1:T(8,128)(2,1)S(1)}, bf16[4,16,15,128]{3,2,0,1:T(8,128)(2,1)S(1)}, u32[]{:S(2)}, u32[]{:S(2)}) collective-permute-start(bf16[4,16,15,128]{3,2,0,1:T(8,128)(2,1)S(1)} %get-tuple-element.13), channel_id=1, source_target_pairs={{0,8},{8,16},{16,24},{24,32},{32,40},{40,48},{48,56},{56,64},{64,7... | collective-permute-start | bytes 737288 | tf_op jit(solution)/shard_map/ppermute | solution.py:16
  72.7 11.4 %collective-permute-start.4 = (bf16[4,16,15,128]{3,2,0,1:T(8,128)(2,1)S(1)}, bf16[4,16,15,128]{3,2,0,1:T(8,128)(2,1)S(1)}, u32[]{:S(2)}, u32[]{:S(2)}) collective-permute-start(bf16[4,16,15,128]{3,2,0,1:T(8,128)(2,1)S(1)} %get-tuple-element.14), channel_id=1, source_target_pairs={{8,0},{16,8},{24,16},{32,24},{40,32},{48,40},{56,48},{64,56},{72,6... | collective-permute-start | bytes 737288 | tf_op jit(solution)/shard_map/ppermute | solution.py:17
  74.8 19.3 %copy-start.1 = (f32[32,16,128]{2,1,0:T(8,128)S(1)}, f32[32,16,128]{2,1,0:T(8,128)}, u32[]{:S(2)}) copy-start(f32[32,16,128]{2,1,0:T(8,128)} %param.5) | copy-start | bytes 786436
  84.5 9.6 %collective-permute-start.5 = (f32[16,16,128]{2,1,0:T(8,128)S(1)}, f32[16,16,128]{2,1,0:T(8,128)S(1)}, u32[]{:S(2)}, u32[]{:S(2)}) collective-permute-start(f32[16,16,128]{2,1,0:T(8,128)S(1)} %fusion.17), channel_id=1, source_target_pairs={{0,512},{256,768},{512,0},{768,256},{1,513},{257,769},{513,1},{769... | collective-permute-start | bytes 393224 | tf_op jit(solution)/shard_map/ppermute | solution.py:153
  94.2 7.5 %collective-permute-start.6 = (bf16[16,15,128]{2,1,0:T(8,128)(2,1)S(1)}, bf16[16,15,128]{2,1,0:T(8,128)(2,1)S(1)}, u32[]{:S(2)}, u32[]{:S(2)}) collective-permute-start(bf16[16,15,128]{2,1,0:T(8,128)(2,1)S(1)} %get-tuple-element.15), channel_id=1, source_target_pairs={{0,8},{8,16},{16,24},{24,32},{32,40},{40,48},{48,56},{56,64},{64,7... | collective-permute-start | bytes 184328 | tf_op jit(solution)/shard_map/ppermute | solution.py:16
  99.8 7.9 %collective-permute-start.7 = (bf16[16,15,128]{2,1,0:T(8,128)(2,1)S(1)}, bf16[16,15,128]{2,1,0:T(8,128)(2,1)S(1)}, u32[]{:S(2)}, u32[]{:S(2)}) collective-permute-start(bf16[16,15,128]{2,1,0:T(8,128)(2,1)S(1)} %get-tuple-element.16), channel_id=1, source_target_pairs={{8,0},{16,8},{24,16},{32,24},{40,32},{48,40},{56,48},{64,56},{72,6... | collective-permute-start | bytes 184328 | tf_op jit(solution)/shard_map/ppermute | solution.py:17
  143.5 8.9 %collective-permute-start.8 = (bf16[4,16,15,128]{3,2,0,1:T(8,128)(2,1)S(1)}, bf16[4,16,15,128]{3,2,0,1:T(8,128)(2,1)S(1)}, u32[]{:S(2)}, u32[]{:S(2)}) collective-permute-start(bf16[4,16,15,128]{3,2,0,1:T(8,128)(2,1)S(1)} %get-tuple-element.11), channel_id=1, source_target_pairs={{0,8},{8,16},{16,24},{24,32},{32,40},{40,48},{48,56},{56,64},{64,7... | collective-permute-start | bytes 737288 | tf_op jit(solution)/shard_map/ppermute | solution.py:16
  145.5 11.6 %collective-permute-start.9 = (bf16[4,16,15,128]{3,2,0,1:T(8,128)(2,1)S(1)}, bf16[4,16,15,128]{3,2,0,1:T(8,128)(2,1)S(1)}, u32[]{:S(2)}, u32[]{:S(2)}) collective-permute-start(bf16[4,16,15,128]{3,2,0,1:T(8,128)(2,1)S(1)} %get-tuple-element.12), channel_id=1, source_target_pairs={{8,0},{16,8},{24,16},{32,24},{40,32},{48,40},{56,48},{64,56},{72,6... | collective-permute-start | bytes 737288 | tf_op jit(solution)/shard_map/ppermute | solution.py:17
  157.6 9.6 %collective-permute-start.10 = (f32[16,16,128]{2,1,0:T(8,128)S(1)}, f32[16,16,128]{2,1,0:T(8,128)S(1)}, u32[]{:S(2)}, u32[]{:S(2)}) collective-permute-start(f32[16,16,128]{2,1,0:T(8,128)S(1)} %fusion.16), channel_id=1, source_target_pairs={{0,512},{256,768},{512,0},{768,256},{1,513},{257,769},{513,1},{769... | collective-permute-start | bytes 393224 | tf_op jit(solution)/shard_map/ppermute | solution.py:153
  167.2 10.4 %collective-permute-start.11 = (f32[16,16,128]{2,1,0:T(8,128)S(1)}, f32[16,16,128]{2,1,0:T(8,128)S(1)}, u32[]{:S(2)}, u32[]{:S(2)}) collective-permute-start(f32[16,16,128]{2,1,0:T(8,128)S(1)} %multiply_multiply_fusion), channel_id=1, source_target_pairs={{0,256},{256,0},{512,768},{768,512},{1,257},{257,1},{513,769},{769... | collective-permute-start | bytes 393224 | tf_op jit(solution)/shard_map/ppermute | solution.py:155

commit v8 on v7

--- a/solution.py
+++ b/solution.py
@@ -11,10 +11,8 @@
         count, length = (lax.axis_size(axis), shard.shape[dim])
         up = [(i, (i + 1) % count) for i in range(count - 1)]
         down = [(j, i) for i, j in up]
-        last = lax.slice_in_dim(shard, length - width, length, axis=dim)
-        initial = lax.slice_in_dim(shard, 0, width, axis=dim)
-        before = lax.ppermute(last, axis, up)
-        after = lax.ppermute(initial, axis, down)
+        before = lax.slice_in_dim(lax.ppermute(shard, axis, up), length - width, length, axis=dim)
+        after = lax.slice_in_dim(lax.ppermute(shard, axis, down), 0, width, axis=dim)
         shard = jnp.concatenate([before, shard, after], axis=dim)
     return shard
 

time: 179 us -> 179 us (level)
  no operation moved by 1% of the time
where the time goes in v8:
time: 179 us
  starting transfers between devices  65.9 us (37%)
  waiting for transfers between devices  61.2 us (34%)
  blocking collectives  34 us (19%)
  local copies, waits for them, and re-layouts  10.2 us (6%)
  other arithmetic  3.29 us (2%)
  matrix products  3.24 us (2%)
    all_to_all x2, blocking collectives, chip_exchange(): lax.all_to_all(chunks, ('view', 'col'), 0, 0, axis_index_groups=groups, t...  34 us
    all_to_all x2, starting transfers between devices, chip_exchange(): lax.all_to_all(chunks, ('view', 'col'), 0, 0, axis_index_groups=groups, t...  23.6 us
    all_to_all x2, waiting for transfers between devices, chip_exchange(): lax.all_to_all(chunks, ('view', 'col'), 0, 0, axis_index_groups=groups, t...  20.7 us
    ppermute x4, waiting for transfers between devices, extended(): lax.ppermute(shard, axis, down)  17.8 us
    ppermute x4, starting transfers between devices, extended(): lax.ppermute(shard, axis, up)  17.3 us
    ppermute x2, waiting for transfers between devices, on_device(): summed = accumulated + lax.ppermute(accumulated, 'view', to_far)  15.4 us
    ppermute x1, starting transfers between devices, on_device(): return joined(restored_mine, lax.ppermute(restored_mine, 'view', to_core))  9.53 us
    ppermute x4, starting transfers between devices, extended(): lax.ppermute(shard, axis, down)  9.12 us
  transfers between devices with their start and end apart: 14, of which 11 were waited for; matrix products, arithmetic and copies ran while one was open for 5% of the time, Pallas kernels for 0%

profile of v8, /device:TPU:113, one launch (start us, length us, event | category | flops | bytes accessed | tf_op | source)
XLA Modules:
  0.0 178.6 jit_solution(11241833185220840108)
XLA Ops:
  0.0 0.8 pad_maximum_fusion.3
  0.8 2.6 %collective-permute-start = (f32[2,183]{1,0:T(2,128)S(1)}, f32[2,183]{1,0:T(2,128)S(1)}, u32[]{:S(2)}, u32[]{:S(2)}) collective-permute-start(f32[2,183]{1,0:T(2,128)S(1)} %pad_maximum_fusion.3), channel_id=1, source_target_pairs={{0,256},{256,0},{512,768},{768,512},{1,257},{257,1},{513,769},{769... | collective-permute-start | bytes 4400 | tf_op jit(solution)/shard_map/ppermute | solution.py:60
  3.4 0.9 dynamic-slice_convert_fusion
  4.3 5.1 %collective-permute-start.1 = (bf16[16,16,128]{2,1,0:T(8,128)(2,1)S(1)}, bf16[16,16,128]{2,1,0:T(8,128)(2,1)S(1)}, u32[]{:S(2)}, u32[]{:S(2)}) collective-permute-start(bf16[16,16,128]{2,1,0:T(8,128)(2,1)S(1)} %dynamic-slice_convert_fusion), channel_id=1, source_target_pairs={{0,8},{8,16},{16,24},{24,32},{32,40},{40,48},{48,56},{56,64},{64,7... | collective-permute-start | bytes 196616 | tf_op jit(solution)/shard_map/ppermute | solution.py:14
  9.4 1.9 %collective-permute-start.2 = (bf16[16,16,128]{2,1,0:T(8,128)(2,1)S(1)}, bf16[16,16,128]{2,1,0:T(8,128)(2,1)S(1)}, u32[]{:S(2)}, u32[]{:S(2)}) collective-permute-start(bf16[16,16,128]{2,1,0:T(8,128)(2,1)S(1)} %dynamic-slice_convert_fusion), channel_id=1, source_target_pairs={{8,0},{16,8},{24,16},{32,24},{40,32},{48,40},{56,48},{64,56},{72,6... | collective-permute-start | bytes 196616 | tf_op jit(solution)/shard_map/ppermute | solution.py:15
  11.4 1.0 copy.38
  12.6 0.2 slice_reduce_fusion.1
  12.8 0.2 slice_reduce_fusion.2
  13.6 0.1 reshape.129
  13.8 0.1 reshape.128
  14.0 0.1 reshape.131
  14.3 0.1 reshape.130
  14.5 0.3 reshape.127
  15.0 0.3 reshape.126
  15.5 0.3 reshape.125
  16.0 0.3 reshape.124
  16.6 0.6 collective-permute-done.2
  17.2 0.6 fusion.5
  17.8 0.8 pad_maximum_fusion.1
  18.7 18.1 %all-to-all-start = ((bf16[16,128,128]{2,1,0:T(8,128)(2,1)}), bf16[16,128,128]{2,1,0:T(8,128)(2,1)S(1)}, u32[]{:S(2)}, u32[]{:S(2)}) async-start(bf16[16,128,128]{2,1,0:T(8,128)(2,1)} %pad_maximum_fusion.1), calls=%async_computation | async-start | bytes 1048576 | tf_op jit(solution)/shard_map/all_to_all | solution.py:90
  36.8 0.1 copy.66
  36.9 0.4 reshape.136
  37.4 0.1 copy.41
  37.5 0.1 copy.67
  37.6 0.4 reshape.137
  38.1 0.1 copy.42
  38.3 0.1 copy.68
  38.4 0.4 reshape.138
  38.9 0.1 copy.43
  39.1 0.1 copy.69
  39.2 0.4 reshape.139
  39.9 11.7 %all-to-all-done = bf16[16,128,128]{2,1,0:T(8,128)(2,1)S(1)} async-done(((bf16[16,128,128]{2,1,0:T(8,128)(2,1)}), bf16[16,128,128]{2,1,0:T(8,128)(2,1)S(1)}, u32[]{:S(2)}, u32[]{:S(2)}) %all-to-all-start) | async-done | bytes 524320 | tf_op jit(solution)/shard_map/all_to_all | solution.py:90
  51.7 0.6 fusion.15
  52.3 0.7 copy.47
  53.1 5.4 %all-to-all-start.1 = ((bf16[16,64,128]{2,1,0:T(8,128)(2,1)}), bf16[16,64,128]{2,1,0:T(8,128)(2,1)S(1)}, u32[]{:S(2)}, u32[]{:S(2)}) async-start(bf16[16,64,128]{2,1,0:T(8,128)(2,1)} %bitcast.46), calls=%async_computation.1 | async-start | bytes 524288 | tf_op jit(solution)/shard_map/all_to_all | solution.py:90
  58.6 0.1 reshape.147
  58.8 0.1 reshape.146
  59.0 0.1 reshape.145
  59.1 9.0 %all-to-all-done.1 = bf16[16,64,128]{2,1,0:T(8,128)(2,1)S(1)} async-done(((bf16[16,64,128]{2,1,0:T(8,128)(2,1)}), bf16[16,64,128]{2,1,0:T(8,128)(2,1)S(1)}, u32[]{:S(2)}, u32[]{:S(2)}) %all-to-all-start.1) | async-done | bytes 262176 | tf_op jit(solution)/shard_map/all_to_all | solution.py:90
  68.2 4.6 %collective-permute-start.3 = (bf16[4,16,16,128]{3,2,0,1:T(8,128)(2,1)S(1)}, bf16[4,16,16,128]{3,2,0,1:T(8,128)(2,1)S(1)}, u32[]{:S(2)}, u32[]{:S(2)}) collective-permute-start(bf16[4,16,16,128]{3,2,0,1:T(8,128)(2,1)S(1)} %copy.49), channel_id=1, source_target_pairs={{0,8},{8,16},{16,24},{24,32},{32,40},{40,48},{48,56},{56,64},{64,7... | collective-permute-start | bytes 786440 | tf_op jit(solution)/shard_map/ppermute | solution.py:14
  72.9 1.9 %collective-permute-start.4 = (bf16[4,16,16,128]{3,2,0,1:T(8,128)(2,1)S(1)}, bf16[4,16,16,128]{3,2,0,1:T(8,128)(2,1)S(1)}, u32[]{:S(2)}, u32[]{:S(2)}) collective-permute-start(bf16[4,16,16,128]{3,2,0,1:T(8,128)(2,1)S(1)} %copy.49), channel_id=1, source_target_pairs={{8,0},{16,8},{24,16},{32,24},{40,32},{48,40},{56,48},{64,56},{72,6... | collective-permute-start | bytes 786440 | tf_op jit(solution)/shard_map/ppermute | solution.py:15
  74.9 0.1 reshape.144
  75.1 2.8 %collective-permute-done.3 = bf16[4,16,16,128]{3,2,0,1:T(8,128)(2,1)S(1)} collective-permute-done((bf16[4,16,16,128]{3,2,0,1:T(8,128)(2,1)S(1)}, bf16[4,16,16,128]{3,2,0,1:T(8,128)(2,1)S(1)}, u32[]{:S(2)}, u32[]{:S(2)}) %collective-permute-start.3) | collective-permute-done | bytes 262176 | tf_op jit(solution)/shard_map/ppermute | solution.py:14
  77.9 6.4 %collective-permute-done.4 = bf16[4,16,16,128]{3,2,0,1:T(8,128)(2,1)S(1)} collective-permute-done((bf16[4,16,16,128]{3,2,0,1:T(8,128)(2,1)S(1)}, bf16[4,16,16,128]{3,2,0,1:T(8,128)(2,1)S(1)}, u32[]{:S(2)}, u32[]{:S(2)}) %collective-permute-start.4) | collective-permute-done | bytes 262176 | tf_op jit(solution)/shard_map/ppermute | solution.py:15
  84.3 0.5 fusion.17
  84.8 1.9 %collective-permute-start.5 = (f32[16,16,128]{2,1,0:T(8,128)S(1)}, f32[16,16,128]{2,1,0:T(8,128)S(1)}, u32[]{:S(2)}, u32[]{:S(2)}) collective-permute-start(f32[16,16,128]{2,1,0:T(8,128)S(1)} %fusion.17), channel_id=1, source_target_pairs={{0,512},{256,768},{512,0},{768,256},{1,513},{257,769},{513,1},{769... | collective-permute-start | bytes 393224 | tf_op jit(solution)/shard_map/ppermute | solution.py:151
  86.7 7.7 %collective-permute-done.5 = f32[16,16,128]{2,1,0:T(8,128)S(1)} collective-permute-done((f32[16,16,128]{2,1,0:T(8,128)S(1)}, f32[16,16,128]{2,1,0:T(8,128)S(1)}, u32[]{:S(2)}, u32[]{:S(2)}) %collective-permute-start.5) | collective-permute-done | bytes 131104 | tf_op jit(solution)/shard_map/ppermute | solution.py:151
  94.4 5.6 %collective-permute-start.6 = (bf16[16,16,128]{2,1,0:T(8,128)(2,1)S(1)}, bf16[16,16,128]{2,1,0:T(8,128)(2,1)S(1)}, u32[]{:S(2)}, u32[]{:S(2)}) collective-permute-start(bf16[16,16,128]{2,1,0:T(8,128)(2,1)S(1)} %get-tuple-element.7), channel_id=1, source_target_pairs={{0,8},{8,16},{16,24},{24,32},{32,40},{40,48},{48,56},{56,64},{64,7... | collective-permute-start | bytes 196616 | tf_op jit(solution)/shard_map/ppermute | solution.py:14
  100.0 1.9 %collective-permute-start.7 = (bf16[16,16,128]{2,1,0:T(8,128)(2,1)S(1)}, bf16[16,16,128]{2,1,0:T(8,128)(2,1)S(1)}, u32[]{:S(2)}, u32[]{:S(2)}) collective-permute-start(bf16[16,16,128]{2,1,0:T(8,128)(2,1)S(1)} %get-tuple-element.7), channel_id=1, source_target_pairs={{8,0},{16,8},{24,16},{32,24},{40,32},{48,40},{56,48},{64,56},{72,6... | collective-permute-start | bytes 196616 | tf_op jit(solution)/shard_map/ppermute | solution.py:15
  102.0 6.3 %collective-permute-done.7 = bf16[16,16,128]{2,1,0:T(8,128)(2,1)S(1)} collective-permute-done((bf16[16,16,128]{2,1,0:T(8,128)(2,1)S(1)}, bf16[16,16,128]{2,1,0:T(8,128)(2,1)S(1)}, u32[]{:S(2)}, u32[]{:S(2)}) %collective-permute-start.7) | collective-permute-done | bytes 65568 | tf_op jit(solution)/shard_map/ppermute | solution.py:15
  108.3 0.6 fusion.4
  108.9 19.6 %all_to_all.20 = bf16[16,64,128]{2,1,0:T(8,128)(2,1)S(1)} all-to-all(bf16[16,64,128]{2,1,0:T(8,128)(2,1)S(1)} %bitcast.229), channel_id=1, replica_groups={{0,1,2,3,4,5,6,7,256,257,258,259,260,261,262,263},{512,513,514,515,516,..., dimensions={0} | all-to-all | bytes 524288 | tf_op jit(solution)/shard_map/all_to_all | solution.py:90
  128.5 0.6 fusion.14
  129.2 14.4 %all_to_all.21 = bf16[16,64,128]{2,1,0:T(8,128)(2,1)S(1)} all-to-all(bf16[16,64,128]{2,1,0:T(8,128)(2,1)S(1)} %bitcast.230), channel_id=1, replica_groups={{0,1,2,3,4,5,6,7,256,257,258,259,260,261,262,263},{512,513,514,515,516,..., dimensions={0} | all-to-all | bytes 524288 | tf_op jit(solution)/shard_map/all_to_all | solution.py:90
  143.6 1.9 %collective-permute-start.8 = (bf16[4,16,16,128]{3,2,0,1:T(8,128)(2,1)S(1)}, bf16[4,16,16,128]{3,2,0,1:T(8,128)(2,1)S(1)}, u32[]{:S(2)}, u32[]{:S(2)}) collective-permute-start(bf16[4,16,16,128]{3,2,0,1:T(8,128)(2,1)S(1)} %copy.57), channel_id=1, source_target_pairs={{0,8},{8,16},{16,24},{24,32},{32,40},{40,48},{48,56},{56,64},{64,7... | collective-permute-start | bytes 786440 | tf_op jit(solution)/shard_map/ppermute | solution.py:14
  145.6 3.4 %collective-permute-start.9 = (bf16[4,16,16,128]{3,2,0,1:T(8,128)(2,1)S(1)}, bf16[4,16,16,128]{3,2,0,1:T(8,128)(2,1)S(1)}, u32[]{:S(2)}, u32[]{:S(2)}) collective-permute-start(bf16[4,16,16,128]{3,2,0,1:T(8,128)(2,1)S(1)} %copy.57), channel_id=1, source_target_pairs={{8,0},{16,8},{24,16},{32,24},{40,32},{48,40},{56,48},{64,56},{72,6... | collective-permute-start | bytes 786440 | tf_op jit(solution)/shard_map/ppermute | solution.py:15
  148.9 3.6 %collective-permute-done.8 = bf16[4,16,16,128]{3,2,0,1:T(8,128)(2,1)S(1)} collective-permute-done((bf16[4,16,16,128]{3,2,0,1:T(8,128)(2,1)S(1)}, bf16[4,16,16,128]{3,2,0,1:T(8,128)(2,1)S(1)}, u32[]{:S(2)}, u32[]{:S(2)}) %collective-permute-start.8) | collective-permute-done | bytes 262176 | tf_op jit(solution)/shard_map/ppermute | solution.py:14
  152.7 4.5 %collective-permute-done.9 = bf16[4,16,16,128]{3,2,0,1:T(8,128)(2,1)S(1)} collective-permute-done((bf16[4,16,16,128]{3,2,0,1:T(8,128)(2,1)S(1)}, bf16[4,16,16,128]{3,2,0,1:T(8,128)(2,1)S(1)}, u32[]{:S(2)}, u32[]{:S(2)}) %collective-permute-start.9) | collective-permute-done | bytes 262176 | tf_op jit(solution)/shard_map/ppermute | solution.py:15
  157.2 0.5 fusion.16
  157.7 1.9 %collective-permute-start.10 = (f32[16,16,128]{2,1,0:T(8,128)S(1)}, f32[16,16,128]{2,1,0:T(8,128)S(1)}, u32[]{:S(2)}, u32[]{:S(2)}) collective-permute-start(f32[16,16,128]{2,1,0:T(8,128)S(1)} %fusion.16), channel_id=1, source_target_pairs={{0,512},{256,768},{512,0},{768,256},{1,513},{257,769},{513,1},{769... | collective-permute-start | bytes 393224 | tf_op jit(solution)/shard_map/ppermute | solution.py:151
  159.6 7.7 %collective-permute-done.10 = f32[16,16,128]{2,1,0:T(8,128)S(1)} collective-permute-done((f32[16,16,128]{2,1,0:T(8,128)S(1)}, f32[16,16,128]{2,1,0:T(8,128)S(1)}, u32[]{:S(2)}, u32[]{:S(2)}) %collective-permute-start.10) | collective-permute-done | bytes 131104 | tf_op jit(solution)/shard_map/ppermute | solution.py:151
  167.3 9.5 %collective-permute-start.11 = (f32[16,16,128]{2,1,0:T(8,128)S(1)}, f32[16,16,128]{2,1,0:T(8,128)S(1)}, u32[]{:S(2)}, u32[]{:S(2)}) collective-permute-start(f32[16,16,128]{2,1,0:T(8,128)S(1)} %multiply_multiply_fusion), channel_id=1, source_target_pairs={{0,256},{256,0},{512,768},{768,512},{1,257},{257,1},{513,769},{769... | collective-permute-start | bytes 393224 | tf_op jit(solution)/shard_map/ppermute | solution.py:153
  176.9 1.0 collective-permute-done.11
  177.8 0.7 maximum_select_fusion
  (103 shorter events, 3.6 us)
Async XLA Ops:
  0.8 11.7 %collective-permute-start = (f32[2,183]{1,0:T(2,128)S(1)}, f32[2,183]{1,0:T(2,128)S(1)}, u32[]{:S(2)}, u32[]{:S(2)}) collective-permute-start(f32[2,183]{1,0:T(2,128)S(1)} %pad_maximum_fusion.3), channel_id=1, source_target_pairs={{0,256},{256,0},{512,768},{768,512},{1,257},{257,1},{513,769},{769... | collective-permute-start | bytes 4400 | tf_op jit(solution)/shard_map/ppermute | solution.py:60
  4.3 12.2 %collective-permute-start.1 = (bf16[16,16,128]{2,1,0:T(8,128)(2,1)S(1)}, bf16[16,16,128]{2,1,0:T(8,128)(2,1)S(1)}, u32[]{:S(2)}, u32[]{:S(2)}) collective-permute-start(bf16[16,16,128]{2,1,0:T(8,128)(2,1)S(1)} %dynamic-slice_convert_fusion), channel_id=1, source_target_pairs={{0,8},{8,16},{16,24},{24,32},{32,40},{40,48},{48,56},{56,64},{64,7... | collective-permute-start | bytes 196616 | tf_op jit(solution)/shard_map/ppermute | solution.py:14
  9.4 7.7 %collective-permute-start.2 = (bf16[16,16,128]{2,1,0:T(8,128)(2,1)S(1)}, bf16[16,16,128]{2,1,0:T(8,128)(2,1)S(1)}, u32[]{:S(2)}, u32[]{:S(2)}) collective-permute-start(bf16[16,16,128]{2,1,0:T(8,128)(2,1)S(1)} %dynamic-slice_convert_fusion), channel_id=1, source_target_pairs={{8,0},{16,8},{24,16},{32,24},{40,32},{48,40},{56,48},{64,56},{72,6... | collective-permute-start | bytes 196616 | tf_op jit(solution)/shard_map/ppermute | solution.py:15
  11.4 1.1 copy-start.1
  11.4 1.1 copy-start.2
  11.4 1.1 copy-start.3
  11.4 2.1 %copy-start.4 = (pred[62]{0:T(512)(128)(4,1)S(1)}, pred[62]{0:T(512)(128)(4,1)}, u32[]{:S(2)}) copy-start(pred[62]{0:T(512)(128)(4,1)} %constant.42.clone.1) | copy-start | bytes 190
  18.7 32.9 %all-to-all-start = ((bf16[16,128,128]{2,1,0:T(8,128)(2,1)}), bf16[16,128,128]{2,1,0:T(8,128)(2,1)S(1)}, u32[]{:S(2)}, u32[]{:S(2)}) async-start(bf16[16,128,128]{2,1,0:T(8,128)(2,1)} %pad_maximum_fusion.1), calls=%async_computation | async-start | bytes 1048576 | tf_op jit(solution)/shard_map/all_to_all | solution.py:90
  53.1 15.1 %all-to-all-start.1 = ((bf16[16,64,128]{2,1,0:T(8,128)(2,1)}), bf16[16,64,128]{2,1,0:T(8,128)(2,1)S(1)}, u32[]{:S(2)}, u32[]{:S(2)}) async-start(bf16[16,64,128]{2,1,0:T(8,128)(2,1)} %bitcast.46), calls=%async_computation.1 | async-start | bytes 524288 | tf_op jit(solution)/shard_map/all_to_all | solution.py:90
  68.2 9.6 %collective-permute-start.3 = (bf16[4,16,16,128]{3,2,0,1:T(8,128)(2,1)S(1)}, bf16[4,16,16,128]{3,2,0,1:T(8,128)(2,1)S(1)}, u32[]{:S(2)}, u32[]{:S(2)}) collective-permute-start(bf16[4,16,16,128]{3,2,0,1:T(8,128)(2,1)S(1)} %copy.49), channel_id=1, source_target_pairs={{0,8},{8,16},{16,24},{24,32},{32,40},{40,48},{48,56},{56,64},{64,7... | collective-permute-start | bytes 786440 | tf_op jit(solution)/shard_map/ppermute | solution.py:14
  72.9 11.4 %collective-permute-start.4 = (bf16[4,16,16,128]{3,2,0,1:T(8,128)(2,1)S(1)}, bf16[4,16,16,128]{3,2,0,1:T(8,128)(2,1)S(1)}, u32[]{:S(2)}, u32[]{:S(2)}) collective-permute-start(bf16[4,16,16,128]{3,2,0,1:T(8,128)(2,1)S(1)} %copy.49), channel_id=1, source_target_pairs={{8,0},{16,8},{24,16},{32,24},{40,32},{48,40},{56,48},{64,56},{72,6... | collective-permute-start | bytes 786440 | tf_op jit(solution)/shard_map/ppermute | solution.py:15
  84.3 10.1 %copy-start = (f32[32,16,128]{2,1,0:T(8,128)S(1)}, f32[32,16,128]{2,1,0:T(8,128)}, u32[]{:S(2)}) copy-start(f32[32,16,128]{2,1,0:T(8,128)} %param.5) | copy-start | bytes 786436
  84.8 9.6 %collective-permute-start.5 = (f32[16,16,128]{2,1,0:T(8,128)S(1)}, f32[16,16,128]{2,1,0:T(8,128)S(1)}, u32[]{:S(2)}, u32[]{:S(2)}) collective-permute-start(f32[16,16,128]{2,1,0:T(8,128)S(1)} %fusion.17), channel_id=1, source_target_pairs={{0,512},{256,768},{512,0},{768,256},{1,513},{257,769},{513,1},{769... | collective-permute-start | bytes 393224 | tf_op jit(solution)/shard_map/ppermute | solution.py:151
  94.4 7.5 %collective-permute-start.6 = (bf16[16,16,128]{2,1,0:T(8,128)(2,1)S(1)}, bf16[16,16,128]{2,1,0:T(8,128)(2,1)S(1)}, u32[]{:S(2)}, u32[]{:S(2)}) collective-permute-start(bf16[16,16,128]{2,1,0:T(8,128)(2,1)S(1)} %get-tuple-element.7), channel_id=1, source_target_pairs={{0,8},{8,16},{16,24},{24,32},{32,40},{40,48},{48,56},{56,64},{64,7... | collective-permute-start | bytes 196616 | tf_op jit(solution)/shard_map/ppermute | solution.py:14
  100.0 8.2 %collective-permute-start.7 = (bf16[16,16,128]{2,1,0:T(8,128)(2,1)S(1)}, bf16[16,16,128]{2,1,0:T(8,128)(2,1)S(1)}, u32[]{:S(2)}, u32[]{:S(2)}) collective-permute-start(bf16[16,16,128]{2,1,0:T(8,128)(2,1)S(1)} %get-tuple-element.7), channel_id=1, source_target_pairs={{8,0},{16,8},{24,16},{32,24},{40,32},{48,40},{56,48},{64,56},{72,6... | collective-permute-start | bytes 196616 | tf_op jit(solution)/shard_map/ppermute | solution.py:15
  143.6 8.9 %collective-permute-start.8 = (bf16[4,16,16,128]{3,2,0,1:T(8,128)(2,1)S(1)}, bf16[4,16,16,128]{3,2,0,1:T(8,128)(2,1)S(1)}, u32[]{:S(2)}, u32[]{:S(2)}) collective-permute-start(bf16[4,16,16,128]{3,2,0,1:T(8,128)(2,1)S(1)} %copy.57), channel_id=1, source_target_pairs={{0,8},{8,16},{16,24},{24,32},{32,40},{40,48},{48,56},{56,64},{64,7... | collective-permute-start | bytes 786440 | tf_op jit(solution)/shard_map/ppermute | solution.py:14
  145.6 11.6 %collective-permute-start.9 = (bf16[4,16,16,128]{3,2,0,1:T(8,128)(2,1)S(1)}, bf16[4,16,16,128]{3,2,0,1:T(8,128)(2,1)S(1)}, u32[]{:S(2)}, u32[]{:S(2)}) collective-permute-start(bf16[4,16,16,128]{3,2,0,1:T(8,128)(2,1)S(1)} %copy.57), channel_id=1, source_target_pairs={{8,0},{16,8},{24,16},{32,24},{40,32},{48,40},{56,48},{64,56},{72,6... | collective-permute-start | bytes 786440 | tf_op jit(solution)/shard_map/ppermute | solution.py:15
  157.7 9.6 %collective-permute-start.10 = (f32[16,16,128]{2,1,0:T(8,128)S(1)}, f32[16,16,128]{2,1,0:T(8,128)S(1)}, u32[]{:S(2)}, u32[]{:S(2)}) collective-permute-start(f32[16,16,128]{2,1,0:T(8,128)S(1)} %fusion.16), channel_id=1, source_target_pairs={{0,512},{256,768},{512,0},{768,256},{1,513},{257,769},{513,1},{769... | collective-permute-start | bytes 393224 | tf_op jit(solution)/shard_map/ppermute | solution.py:151
  167.3 10.5 %collective-permute-start.11 = (f32[16,16,128]{2,1,0:T(8,128)S(1)}, f32[16,16,128]{2,1,0:T(8,128)S(1)}, u32[]{:S(2)}, u32[]{:S(2)}) collective-permute-start(f32[16,16,128]{2,1,0:T(8,128)S(1)} %multiply_multiply_fusion), channel_id=1, source_target_pairs={{0,256},{256,0},{512,768},{768,512},{1,257},{257,1},{513,769},{769... | collective-permute-start | bytes 393224 | tf_op jit(solution)/shard_map/ppermute | solution.py:153

commit v9 on v7

--- a/solution.py
+++ b/solution.py
@@ -65,24 +65,13 @@
     chip_y = normalized(taps[:, lateral_taps : 2 * lateral_taps])
     chip_z = normalized(taps[:, 2 * lateral_taps :])
     chip_count = chip_x.shape[0]
-    bands_x = jnp.stack(
-        [toeplitz_band(chip_x[member], across, across, radius_lat) for member in range(chip_count)]
-    )
-    bands_y = jnp.stack(
-        [toeplitz_band(chip_y[member], height, framed_rows, 0) for member in range(chip_count)]
-    )
-    bands_yback = jnp.stack(
-        [
-            toeplitz_band(chip_y[member][::-1], height, framed_rows, 0)
-            for member in range(chip_count)
-        ]
-    )
-    bands_z = jnp.stack(
-        [
-            toeplitz_band(chip_z[member], planes, planes, radius_ax)
-            for member in range(chip_count)
-        ]
-    )
+    def banded(taps, height_, breadth, offset):
+        return jax.vmap(lambda row: toeplitz_band(row, height_, breadth, offset))(taps)
+
+    bands_x = banded(chip_x, across, across, radius_lat)
+    bands_y = banded(chip_y, height, framed_rows, 0)
+    bands_yback = banded(chip_y[:, ::-1], height, framed_rows, 0)
+    bands_z = banded(chip_z, planes, planes, radius_ax)
     bands_z = bands_z.reshape(chip_count, planes, blocks, 2, half)
 
     def framed(field):

time: 179 us -> 178 us (level)
  blocking collectives: 34.3 us -> 49.3 us
  waiting for transfers between devices: 61.5 us -> 52.6 us
  starting transfers between devices: 65.4 us -> 59.2 us
  local copies, waits for them, and re-layouts: 9.84 us -> 7.62 us
    all_to_all x2 -> x3, blocking collectives: 34.3 us -> 49.3 us  [chip_exchange(): lax.all_to_all(chunks, ('view', 'col'), 0, 0, axis_index_groups=groups, t...]
    all_to_all x2 -> x1, waiting for transfers between devices: 20.7 us -> 11.1 us  [chip_exchange(): lax.all_to_all(chunks, ('view', 'col'), 0, 0, axis_index_groups=groups, t...]
    all_to_all x2 -> x1, starting transfers between devices: 23.6 us -> 18.1 us  [chip_exchange(): lax.all_to_all(chunks, ('view', 'col'), 0, 0, axis_index_groups=groups, t...]
    ppermute x4, starting transfers between devices: 16.8 us -> 15 us  [extended(): before = lax.ppermute(last, axis, up)]
    reshape x16 -> x4, local copies, waits for them, and re-layouts: 3.82 us -> 2.64 us  [toeplitz_band(): return tiled.reshape(height, extent - 1)[:, :breadth]]
  transfers between devices with their start and end apart: 14 -> 13, of which waited for: 11 -> 10; matrix products, arithmetic and copies ran while one was open for 5% -> 4% of each run, Pallas kernels for 0% -> 0%
where the time goes in v9:
time: 178 us; the launch traced here: 177 us
  starting transfers between devices  59.2 us (33%)
  waiting for transfers between devices  52.6 us (30%)
  blocking collectives  49.3 us (28%)
  local copies, waits for them, and re-layouts  7.62 us (4%)
  matrix products  4.16 us (2%)
  other arithmetic  3.21 us (2%)
    all_to_all x3, blocking collectives, chip_exchange(): lax.all_to_all(chunks, ('view', 'col'), 0, 0, axis_index_groups=groups, t...  49.3 us
    all_to_all x1, starting transfers between devices, chip_exchange(): lax.all_to_all(chunks, ('view', 'col'), 0, 0, axis_index_groups=groups, t...  18.1 us
    ppermute x4, waiting for transfers between devices, extended(): after = lax.ppermute(initial, axis, down)  18 us
    ppermute x2, waiting for transfers between devices, on_device(): summed = accumulated + lax.ppermute(accumulated, 'view', to_far)  15.4 us
    ppermute x4, starting transfers between devices, extended(): before = lax.ppermute(last, axis, up)  15 us
    all_to_all x1, waiting for transfers between devices, chip_exchange(): lax.all_to_all(chunks, ('view', 'col'), 0, 0, axis_index_groups=groups, t...  11.1 us
    ppermute x4, starting transfers between devices, extended(): after = lax.ppermute(initial, axis, down)  10.2 us
    ppermute x1, starting transfers between devices, on_device(): return joined(restored_mine, lax.ppermute(restored_mine, 'view', to_core))  9.43 us
  transfers between devices with their start and end apart: 13, of which 10 were waited for; matrix products, arithmetic and copies ran while one was open for 4% of the time, Pallas kernels for 0%

profile of v9, /device:TPU:113, one launch (start us, length us, event | category | flops | bytes accessed | tf_op | source)
XLA Modules:
  0.0 176.6 jit_solution(15017334742430390678)
XLA Ops:
  0.0 0.8 pad_maximum_fusion.2
  0.8 2.6 %collective-permute-start = (f32[2,183]{1,0:T(2,128)S(1)}, f32[2,183]{1,0:T(2,128)S(1)}, u32[]{:S(2)}, u32[]{:S(2)}) collective-permute-start(f32[2,183]{1,0:T(2,128)S(1)} %pad_maximum_fusion.2), channel_id=1, source_target_pairs={{0,256},{256,0},{512,768},{768,512},{1,257},{257,1},{513,769},{769... | collective-permute-start | bytes 4400 | tf_op jit(solution)/shard_map/ppermute | solution.py:62
  3.4 0.9 dynamic-slice_convert_fusion
  4.4 5.1 %collective-permute-start.1 = (bf16[16,15,128]{2,1,0:T(8,128)(2,1)S(1)}, bf16[16,15,128]{2,1,0:T(8,128)(2,1)S(1)}, u32[]{:S(2)}, u32[]{:S(2)}) collective-permute-start(bf16[16,15,128]{2,1,0:T(8,128)(2,1)S(1)} %get-tuple-element.17), channel_id=1, source_target_pairs={{0,8},{8,16},{16,24},{24,32},{32,40},{40,48},{48,56},{56,64},{64,7... | collective-permute-start | bytes 184328 | tf_op jit(solution)/shard_map/ppermute | solution.py:16
  9.5 1.9 %collective-permute-start.2 = (bf16[16,15,128]{2,1,0:T(8,128)(2,1)S(1)}, bf16[16,15,128]{2,1,0:T(8,128)(2,1)S(1)}, u32[]{:S(2)}, u32[]{:S(2)}) collective-permute-start(bf16[16,15,128]{2,1,0:T(8,128)(2,1)S(1)} %get-tuple-element.18), channel_id=1, source_target_pairs={{8,0},{16,8},{24,16},{32,24},{40,32},{48,40},{56,48},{64,56},{72,6... | collective-permute-start | bytes 184328 | tf_op jit(solution)/shard_map/ppermute | solution.py:17
  11.5 1.0 copy.31
  12.6 0.1 maximum_select_fusion.1
  12.6 0.2 slice_reduce_fusion
  12.8 0.1 divide_convert_fusion.1
  12.9 0.1 pad_slice_fusion.3
  13.0 0.1 rev.3
  13.1 0.2 copy.57
  13.4 0.1 slice.118
  13.5 0.7 reshape.82
  14.2 0.1 tile.19
  14.3 0.1 reshape.83
  14.4 2.9 %collective-permute-done.2 = bf16[16,15,128]{2,1,0:T(8,128)(2,1)S(1)} collective-permute-done((bf16[16,15,128]{2,1,0:T(8,128)(2,1)S(1)}, bf16[16,15,128]{2,1,0:T(8,128)(2,1)S(1)}, u32[]{:S(2)}, u32[]{:S(2)}) %collective-permute-start.2) | collective-permute-done | bytes 61472 | tf_op jit(solution)/shard_map/ppermute | solution.py:17
  17.2 0.6 fusion.5
  17.8 0.1 copy.30
  17.9 0.8 pad_maximum_fusion
  18.7 18.1 %all-to-all-start = ((bf16[16,128,128]{2,1,0:T(8,128)(2,1)}), bf16[16,128,128]{2,1,0:T(8,128)(2,1)S(1)}, u32[]{:S(2)}, u32[]{:S(2)}) async-start(bf16[16,128,128]{2,1,0:T(8,128)(2,1)} %pad_maximum_fusion), calls=%async_computation | async-start | bytes 1048576 | tf_op jit(solution)/shard_map/all_to_all | solution.py:81
  36.9 0.2 slice_reduce_fusion.2
  37.1 0.1 divide_convert_fusion
  37.1 0.1 pad_slice_fusion.1
  37.2 0.1 broadcast_bitcast_fusion
  37.3 0.8 copy.56
  38.1 0.4 slice.115
  38.5 1.8 reshape.88
  40.3 0.2 copy.34
  40.5 11.1 %all-to-all-done = bf16[16,128,128]{2,1,0:T(8,128)(2,1)S(1)} async-done(((bf16[16,128,128]{2,1,0:T(8,128)(2,1)}), bf16[16,128,128]{2,1,0:T(8,128)(2,1)S(1)}, u32[]{:S(2)}, u32[]{:S(2)}) %all-to-all-start) | async-done | bytes 524320 | tf_op jit(solution)/shard_map/all_to_all | solution.py:81
  51.7 0.1 convert_bitcast_fusion
  51.8 0.5 fusion.15
  52.4 14.9 %all_to_all.20 = bf16[16,64,128]{2,1,0:T(8,128)(2,1)S(1)} all-to-all(bf16[16,64,128]{2,1,0:T(8,128)(2,1)S(1)} %bitcast.136), channel_id=1, replica_groups={{0,1,2,3,4,5,6,7,256,257,258,259,260,261,262,263},{512,513,514,515,516,..., dimensions={0} | all-to-all | bytes 524288 | tf_op jit(solution)/shard_map/all_to_all | solution.py:81
  67.3 0.1 copy.39
  67.4 0.1 fusion.87
  67.5 2.3 %collective-permute-start.3 = (bf16[4,16,15,128]{3,2,0,1:T(8,128)(2,1)S(1)}, bf16[4,16,15,128]{3,2,0,1:T(8,128)(2,1)}, u32[]{:S(2)}, u32[]{:S(2)}) collective-permute-start(bf16[4,16,15,128]{3,2,0,1:T(8,128)(2,1)S(1)} %get-tuple-element.13), channel_id=1, source_target_pairs={{0,8},{8,16},{16,24},{24,32},{32,40},{40,48},{48,56},{56,64},{64,7... | collective-permute-start | bytes 737288 | tf_op jit(solution)/shard_map/ppermute | solution.py:16
  69.8 3.0 %collective-permute-start.4 = (bf16[4,16,15,128]{3,2,0,1:T(8,128)(2,1)S(1)}, bf16[4,16,15,128]{3,2,0,1:T(8,128)(2,1)}, u32[]{:S(2)}, u32[]{:S(2)}) collective-permute-start(bf16[4,16,15,128]{3,2,0,1:T(8,128)(2,1)S(1)} %get-tuple-element.14), channel_id=1, source_target_pairs={{8,0},{16,8},{24,16},{32,24},{40,32},{48,40},{56,48},{64,56},{72,6... | collective-permute-start | bytes 737288 | tf_op jit(solution)/shard_map/ppermute | solution.py:17
  72.8 0.1 tile.43
  72.9 0.1 reshape.94
  73.0 3.5 %collective-permute-done.3 = bf16[4,16,15,128]{3,2,0,1:T(8,128)(2,1)} collective-permute-done((bf16[4,16,15,128]{3,2,0,1:T(8,128)(2,1)S(1)}, bf16[4,16,15,128]{3,2,0,1:T(8,128)(2,1)}, u32[]{:S(2)}, u32[]{:S(2)}) %collective-permute-start.3) | collective-permute-done | bytes 245792 | tf_op jit(solution)/shard_map/ppermute | solution.py:16
  76.5 4.7 %collective-permute-done.4 = bf16[4,16,15,128]{3,2,0,1:T(8,128)(2,1)} collective-permute-done((bf16[4,16,15,128]{3,2,0,1:T(8,128)(2,1)S(1)}, bf16[4,16,15,128]{3,2,0,1:T(8,128)(2,1)}, u32[]{:S(2)}, u32[]{:S(2)}) %collective-permute-start.4) | collective-permute-done | bytes 245792 | tf_op jit(solution)/shard_map/ppermute | solution.py:17
  81.3 1.5 fusion.17
  82.8 1.9 %collective-permute-start.5 = (f32[16,16,128]{2,1,0:T(8,128)S(1)}, f32[16,16,128]{2,1,0:T(8,128)S(1)}, u32[]{:S(2)}, u32[]{:S(2)}) collective-permute-start(f32[16,16,128]{2,1,0:T(8,128)S(1)} %fusion.17), channel_id=1, source_target_pairs={{0,512},{256,768},{512,0},{768,256},{1,513},{257,769},{513,1},{769... | collective-permute-start | bytes 393224 | tf_op jit(solution)/shard_map/ppermute | solution.py:142
  84.7 7.7 %collective-permute-done.5 = f32[16,16,128]{2,1,0:T(8,128)S(1)} collective-permute-done((f32[16,16,128]{2,1,0:T(8,128)S(1)}, f32[16,16,128]{2,1,0:T(8,128)S(1)}, u32[]{:S(2)}, u32[]{:S(2)}) %collective-permute-start.5) | collective-permute-done | bytes 131104 | tf_op jit(solution)/shard_map/ppermute | solution.py:142
  92.5 5.6 %collective-permute-start.6 = (bf16[16,15,128]{2,1,0:T(8,128)(2,1)S(1)}, bf16[16,15,128]{2,1,0:T(8,128)(2,1)S(1)}, u32[]{:S(2)}, u32[]{:S(2)}) collective-permute-start(bf16[16,15,128]{2,1,0:T(8,128)(2,1)S(1)} %get-tuple-element.15), channel_id=1, source_target_pairs={{0,8},{8,16},{16,24},{24,32},{32,40},{40,48},{48,56},{56,64},{64,7... | collective-permute-start | bytes 184328 | tf_op jit(solution)/shard_map/ppermute | solution.py:16
  98.1 1.9 %collective-permute-start.7 = (bf16[16,15,128]{2,1,0:T(8,128)(2,1)S(1)}, bf16[16,15,128]{2,1,0:T(8,128)(2,1)S(1)}, u32[]{:S(2)}, u32[]{:S(2)}) collective-permute-start(bf16[16,15,128]{2,1,0:T(8,128)(2,1)S(1)} %get-tuple-element.16), channel_id=1, source_target_pairs={{8,0},{16,8},{24,16},{32,24},{40,32},{48,40},{56,48},{64,56},{72,6... | collective-permute-start | bytes 184328 | tf_op jit(solution)/shard_map/ppermute | solution.py:17
  100.1 5.8 %collective-permute-done.7 = bf16[16,15,128]{2,1,0:T(8,128)(2,1)S(1)} collective-permute-done((bf16[16,15,128]{2,1,0:T(8,128)(2,1)S(1)}, bf16[16,15,128]{2,1,0:T(8,128)(2,1)S(1)}, u32[]{:S(2)}, u32[]{:S(2)}) %collective-permute-start.7) | collective-permute-done | bytes 61472 | tf_op jit(solution)/shard_map/ppermute | solution.py:17
  105.8 0.6 fusion.4
  106.4 0.1 copy.42
  106.5 20.1 %all_to_all.21 = bf16[16,64,128]{2,1,0:T(8,128)(2,1)S(1)} all-to-all(bf16[16,64,128]{2,1,0:T(8,128)(2,1)S(1)} %bitcast.139), channel_id=1, replica_groups={{0,1,2,3,4,5,6,7,256,257,258,259,260,261,262,263},{512,513,514,515,516,..., dimensions={0} | all-to-all | bytes 524288 | tf_op jit(solution)/shard_map/all_to_all | solution.py:81
  126.5 0.5 fusion.14
  127.2 14.4 %all_to_all.22 = bf16[16,64,128]{2,1,0:T(8,128)(2,1)S(1)} all-to-all(bf16[16,64,128]{2,1,0:T(8,128)(2,1)S(1)} %bitcast.140), channel_id=1, replica_groups={{0,1,2,3,4,5,6,7,256,257,258,259,260,261,262,263},{512,513,514,515,516,..., dimensions={0} | all-to-all | bytes 524288 | tf_op jit(solution)/shard_map/all_to_all | solution.py:81
  141.5 0.1 copy.47
  141.6 0.1 fusion.86
  141.7 1.9 %collective-permute-start.8 = (bf16[4,16,15,128]{3,2,0,1:T(8,128)(2,1)S(1)}, bf16[4,16,15,128]{3,2,0,1:T(8,128)(2,1)S(1)}, u32[]{:S(2)}, u32[]{:S(2)}) collective-permute-start(bf16[4,16,15,128]{3,2,0,1:T(8,128)(2,1)S(1)} %get-tuple-element.11), channel_id=1, source_target_pairs={{0,8},{8,16},{16,24},{24,32},{32,40},{40,48},{48,56},{56,64},{64,7... | collective-permute-start | bytes 737288 | tf_op jit(solution)/shard_map/ppermute | solution.py:16
  143.7 3.4 %collective-permute-start.9 = (bf16[4,16,15,128]{3,2,0,1:T(8,128)(2,1)S(1)}, bf16[4,16,15,128]{3,2,0,1:T(8,128)(2,1)S(1)}, u32[]{:S(2)}, u32[]{:S(2)}) collective-permute-start(bf16[4,16,15,128]{3,2,0,1:T(8,128)(2,1)S(1)} %get-tuple-element.12), channel_id=1, source_target_pairs={{8,0},{16,8},{24,16},{32,24},{40,32},{48,40},{56,48},{64,56},{72,6... | collective-permute-start | bytes 737288 | tf_op jit(solution)/shard_map/ppermute | solution.py:17
  147.0 3.6 %collective-permute-done.8 = bf16[4,16,15,128]{3,2,0,1:T(8,128)(2,1)S(1)} collective-permute-done((bf16[4,16,15,128]{3,2,0,1:T(8,128)(2,1)S(1)}, bf16[4,16,15,128]{3,2,0,1:T(8,128)(2,1)S(1)}, u32[]{:S(2)}, u32[]{:S(2)}) %collective-permute-start.8) | collective-permute-done | bytes 245792 | tf_op jit(solution)/shard_map/ppermute | solution.py:16
  150.7 4.6 %collective-permute-done.9 = bf16[4,16,15,128]{3,2,0,1:T(8,128)(2,1)S(1)} collective-permute-done((bf16[4,16,15,128]{3,2,0,1:T(8,128)(2,1)S(1)}, bf16[4,16,15,128]{3,2,0,1:T(8,128)(2,1)S(1)}, u32[]{:S(2)}, u32[]{:S(2)}) %collective-permute-start.9) | collective-permute-done | bytes 245792 | tf_op jit(solution)/shard_map/ppermute | solution.py:17
  155.3 0.5 fusion.16
  155.8 1.9 %collective-permute-start.10 = (f32[16,16,128]{2,1,0:T(8,128)S(1)}, f32[16,16,128]{2,1,0:T(8,128)S(1)}, u32[]{:S(2)}, u32[]{:S(2)}) collective-permute-start(f32[16,16,128]{2,1,0:T(8,128)S(1)} %fusion.16), channel_id=1, source_target_pairs={{0,512},{256,768},{512,0},{768,256},{1,513},{257,769},{513,1},{769... | collective-permute-start | bytes 393224 | tf_op jit(solution)/shard_map/ppermute | solution.py:142
  157.7 7.7 %collective-permute-done.10 = f32[16,16,128]{2,1,0:T(8,128)S(1)} collective-permute-done((f32[16,16,128]{2,1,0:T(8,128)S(1)}, f32[16,16,128]{2,1,0:T(8,128)S(1)}, u32[]{:S(2)}, u32[]{:S(2)}) %collective-permute-start.10) | collective-permute-done | bytes 131104 | tf_op jit(solution)/shard_map/ppermute | solution.py:142
  165.4 9.4 %collective-permute-start.11 = (f32[16,16,128]{2,1,0:T(8,128)S(1)}, f32[16,16,128]{2,1,0:T(8,128)S(1)}, u32[]{:S(2)}, u32[]{:S(2)}) collective-permute-start(f32[16,16,128]{2,1,0:T(8,128)S(1)} %multiply_multiply_fusion), channel_id=1, source_target_pairs={{0,256},{256,0},{512,768},{768,512},{1,257},{257,1},{513,769},{769... | collective-permute-start | bytes 393224 | tf_op jit(solution)/shard_map/ppermute | solution.py:144
  174.9 1.0 collective-permute-done.11
  175.8 0.7 maximum_select_fusion
  (37 shorter events, 0.5 us)
Async XLA Ops:
  0.0 13.1 %copy-start.6 = (pred[62]{0:T(512)(128)(4,1)S(1)}, pred[62]{0:T(512)(128)(4,1)}, u32[]{:S(2)}) copy-start(pred[62]{0:T(512)(128)(4,1)} %constant.36.clone.1) | copy-start | bytes 190
  0.0 12.5 %copy-start.5 = (f32[2,31]{1,0:T(2,128)S(1)}, f32[2,31]{1,0:T(2,128)}, u32[]{:S(2)}) copy-start(f32[2,31]{1,0:T(2,128)} %param.7) | copy-start | bytes 748
  0.0 12.5 %copy-start.4 = (f32[2,31]{1,0:T(2,128)S(1)}, f32[2,31]{1,0:T(2,128)}, u32[]{:S(2)}) copy-start(f32[2,31]{1,0:T(2,128)} %param.8) | copy-start | bytes 748
  0.0 12.5 %copy-start.3 = (f32[2,121]{1,0:T(2,128)S(1)}, f32[2,121]{1,0:T(2,128)}, u32[]{:S(2)}) copy-start(f32[2,121]{1,0:T(2,128)} %param.9) | copy-start | bytes 2908
  0.8 11.7 %collective-permute-start = (f32[2,183]{1,0:T(2,128)S(1)}, f32[2,183]{1,0:T(2,128)S(1)}, u32[]{:S(2)}, u32[]{:S(2)}) collective-permute-start(f32[2,183]{1,0:T(2,128)S(1)} %pad_maximum_fusion.2), channel_id=1, source_target_pairs={{0,256},{256,0},{512,768},{768,512},{1,257},{257,1},{513,769},{769... | collective-permute-start | bytes 4400 | tf_op jit(solution)/shard_map/ppermute | solution.py:62
  4.4 10.0 %collective-permute-start.1 = (bf16[16,15,128]{2,1,0:T(8,128)(2,1)S(1)}, bf16[16,15,128]{2,1,0:T(8,128)(2,1)S(1)}, u32[]{:S(2)}, u32[]{:S(2)}) collective-permute-start(bf16[16,15,128]{2,1,0:T(8,128)(2,1)S(1)} %get-tuple-element.17), channel_id=1, source_target_pairs={{0,8},{8,16},{16,24},{24,32},{32,40},{40,48},{48,56},{56,64},{64,7... | collective-permute-start | bytes 184328 | tf_op jit(solution)/shard_map/ppermute | solution.py:16
  9.5 7.7 %collective-permute-start.2 = (bf16[16,15,128]{2,1,0:T(8,128)(2,1)S(1)}, bf16[16,15,128]{2,1,0:T(8,128)(2,1)S(1)}, u32[]{:S(2)}, u32[]{:S(2)}) collective-permute-start(bf16[16,15,128]{2,1,0:T(8,128)(2,1)S(1)} %get-tuple-element.18), channel_id=1, source_target_pairs={{8,0},{16,8},{24,16},{32,24},{40,32},{48,40},{56,48},{64,56},{72,6... | collective-permute-start | bytes 184328 | tf_op jit(solution)/shard_map/ppermute | solution.py:17
  18.7 32.9 %all-to-all-start = ((bf16[16,128,128]{2,1,0:T(8,128)(2,1)}), bf16[16,128,128]{2,1,0:T(8,128)(2,1)S(1)}, u32[]{:S(2)}, u32[]{:S(2)}) async-start(bf16[16,128,128]{2,1,0:T(8,128)(2,1)} %pad_maximum_fusion), calls=%async_computation | async-start | bytes 1048576 | tf_op jit(solution)/shard_map/all_to_all | solution.py:81
  67.5 9.0 %collective-permute-start.3 = (bf16[4,16,15,128]{3,2,0,1:T(8,128)(2,1)S(1)}, bf16[4,16,15,128]{3,2,0,1:T(8,128)(2,1)}, u32[]{:S(2)}, u32[]{:S(2)}) collective-permute-start(bf16[4,16,15,128]{3,2,0,1:T(8,128)(2,1)S(1)} %get-tuple-element.13), channel_id=1, source_target_pairs={{0,8},{8,16},{16,24},{24,32},{32,40},{40,48},{48,56},{56,64},{64,7... | collective-permute-start | bytes 737288 | tf_op jit(solution)/shard_map/ppermute | solution.py:16
  69.8 11.5 %collective-permute-start.4 = (bf16[4,16,15,128]{3,2,0,1:T(8,128)(2,1)S(1)}, bf16[4,16,15,128]{3,2,0,1:T(8,128)(2,1)}, u32[]{:S(2)}, u32[]{:S(2)}) collective-permute-start(bf16[4,16,15,128]{3,2,0,1:T(8,128)(2,1)S(1)} %get-tuple-element.14), channel_id=1, source_target_pairs={{8,0},{16,8},{24,16},{32,24},{40,32},{48,40},{56,48},{64,56},{72,6... | collective-permute-start | bytes 737288 | tf_op jit(solution)/shard_map/ppermute | solution.py:17
  73.0 9.8 %copy-start.1 = (bf16[4,16,61]{2,1,0:T(8,128)(2,1)}, bf16[4,16,61]{2,1,0:T(8,128)(2,1)S(1)}, u32[]{:S(2)}) copy-start(bf16[4,16,61]{2,1,0:T(8,128)(2,1)S(1)} %reshape.94) | copy-start | bytes 23428
  73.0 19.4 %copy-start = (f32[32,16,128]{2,1,0:T(8,128)S(1)}, f32[32,16,128]{2,1,0:T(8,128)}, u32[]{:S(2)}) copy-start(f32[32,16,128]{2,1,0:T(8,128)} %param.5) | copy-start | bytes 786436
  82.8 9.6 %collective-permute-start.5 = (f32[16,16,128]{2,1,0:T(8,128)S(1)}, f32[16,16,128]{2,1,0:T(8,128)S(1)}, u32[]{:S(2)}, u32[]{:S(2)}) collective-permute-start(f32[16,16,128]{2,1,0:T(8,128)S(1)} %fusion.17), channel_id=1, source_target_pairs={{0,512},{256,768},{512,0},{768,256},{1,513},{257,769},{513,1},{769... | collective-permute-start | bytes 393224 | tf_op jit(solution)/shard_map/ppermute | solution.py:142
  92.5 7.6 %collective-permute-start.6 = (bf16[16,15,128]{2,1,0:T(8,128)(2,1)S(1)}, bf16[16,15,128]{2,1,0:T(8,128)(2,1)S(1)}, u32[]{:S(2)}, u32[]{:S(2)}) collective-permute-start(bf16[16,15,128]{2,1,0:T(8,128)(2,1)S(1)} %get-tuple-element.15), channel_id=1, source_target_pairs={{0,8},{8,16},{16,24},{24,32},{32,40},{40,48},{48,56},{56,64},{64,7... | collective-permute-start | bytes 184328 | tf_op jit(solution)/shard_map/ppermute | solution.py:16
  98.1 7.7 %collective-permute-start.7 = (bf16[16,15,128]{2,1,0:T(8,128)(2,1)S(1)}, bf16[16,15,128]{2,1,0:T(8,128)(2,1)S(1)}, u32[]{:S(2)}, u32[]{:S(2)}) collective-permute-start(bf16[16,15,128]{2,1,0:T(8,128)(2,1)S(1)} %get-tuple-element.16), channel_id=1, source_target_pairs={{8,0},{16,8},{24,16},{32,24},{40,32},{48,40},{56,48},{64,56},{72,6... | collective-permute-start | bytes 184328 | tf_op jit(solution)/shard_map/ppermute | solution.py:17
  141.5 13.8 %copy-start.2 = (bf16[4,16,61]{2,1,0:T(8,128)(2,1)S(1)}, bf16[4,16,61]{2,1,0:T(8,128)(2,1)}, u32[]{:S(2)}) copy-start(bf16[4,16,61]{2,1,0:T(8,128)(2,1)} %copy-done.1) | copy-start | bytes 23428
  141.7 8.9 %collective-permute-start.8 = (bf16[4,16,15,128]{3,2,0,1:T(8,128)(2,1)S(1)}, bf16[4,16,15,128]{3,2,0,1:T(8,128)(2,1)S(1)}, u32[]{:S(2)}, u32[]{:S(2)}) collective-permute-start(bf16[4,16,15,128]{3,2,0,1:T(8,128)(2,1)S(1)} %get-tuple-element.11), channel_id=1, source_target_pairs={{0,8},{8,16},{16,24},{24,32},{32,40},{40,48},{48,56},{56,64},{64,7... | collective-permute-start | bytes 737288 | tf_op jit(solution)/shard_map/ppermute | solution.py:16
  143.7 11.6 %collective-permute-start.9 = (bf16[4,16,15,128]{3,2,0,1:T(8,128)(2,1)S(1)}, bf16[4,16,15,128]{3,2,0,1:T(8,128)(2,1)S(1)}, u32[]{:S(2)}, u32[]{:S(2)}) collective-permute-start(bf16[4,16,15,128]{3,2,0,1:T(8,128)(2,1)S(1)} %get-tuple-element.12), channel_id=1, source_target_pairs={{8,0},{16,8},{24,16},{32,24},{40,32},{48,40},{56,48},{64,56},{72,6... | collective-permute-start | bytes 737288 | tf_op jit(solution)/shard_map/ppermute | solution.py:17
  155.8 9.6 %collective-permute-start.10 = (f32[16,16,128]{2,1,0:T(8,128)S(1)}, f32[16,16,128]{2,1,0:T(8,128)S(1)}, u32[]{:S(2)}, u32[]{:S(2)}) collective-permute-start(f32[16,16,128]{2,1,0:T(8,128)S(1)} %fusion.16), channel_id=1, source_target_pairs={{0,512},{256,768},{512,0},{768,256},{1,513},{257,769},{513,1},{769... | collective-permute-start | bytes 393224 | tf_op jit(solution)/shard_map/ppermute | solution.py:142
  165.4 10.4 %collective-permute-start.11 = (f32[16,16,128]{2,1,0:T(8,128)S(1)}, f32[16,16,128]{2,1,0:T(8,128)S(1)}, u32[]{:S(2)}, u32[]{:S(2)}) collective-permute-start(f32[16,16,128]{2,1,0:T(8,128)S(1)} %multiply_multiply_fusion), channel_id=1, source_target_pairs={{0,256},{256,0},{512,768},{768,512},{1,257},{257,1},{513,769},{769... | collective-permute-start | bytes 393224 | tf_op jit(solution)/shard_map/ppermute | solution.py:144

commit v10 on v9

--- a/solution.py
+++ b/solution.py
@@ -11,10 +11,8 @@
         count, length = (lax.axis_size(axis), shard.shape[dim])
         up = [(i, (i + 1) % count) for i in range(count - 1)]
         down = [(j, i) for i, j in up]
-        last = lax.slice_in_dim(shard, length - width, length, axis=dim)
-        initial = lax.slice_in_dim(shard, 0, width, axis=dim)
-        before = lax.ppermute(last, axis, up)
-        after = lax.ppermute(initial, axis, down)
+        before = lax.slice_in_dim(lax.ppermute(shard, axis, up), length - width, length, axis=dim)
+        after = lax.slice_in_dim(lax.ppermute(shard, axis, down), 0, width, axis=dim)
         shard = jnp.concatenate([before, shard, after], axis=dim)
     return shard
 

time: 178 us -> 177 us (level)
  no operation moved by 1% of the time
where the time goes in v10:
time: 177 us; the launch traced here: 176 us
  starting transfers between devices  59.3 us (34%)
  waiting for transfers between devices  52.4 us (30%)
  blocking collectives  49.3 us (28%)
  local copies, waits for them, and re-layouts  7.54 us (4%)
  matrix products  4.13 us (2%)
  other arithmetic  3.2 us (2%)
    all_to_all x3, blocking collectives, chip_exchange(): lax.all_to_all(chunks, ('view', 'col'), 0, 0, axis_index_groups=groups, t...  49.3 us
    all_to_all x1, starting transfers between devices, chip_exchange(): lax.all_to_all(chunks, ('view', 'col'), 0, 0, axis_index_groups=groups, t...  18.1 us
    ppermute x4, waiting for transfers between devices, extended(): lax.ppermute(shard, axis, down)  17.9 us
    ppermute x2, waiting for transfers between devices, on_device(): summed = accumulated + lax.ppermute(accumulated, 'view', to_far)  15.4 us
    ppermute x4, starting transfers between devices, extended(): lax.ppermute(shard, axis, up)  15 us
    all_to_all x1, waiting for transfers between devices, chip_exchange(): lax.all_to_all(chunks, ('view', 'col'), 0, 0, axis_index_groups=groups, t...  11.1 us
    ppermute x4, starting transfers between devices, extended(): lax.ppermute(shard, axis, down)  10.1 us
    ppermute x1, starting transfers between devices, on_device(): return joined(restored_mine, lax.ppermute(restored_mine, 'view', to_core))  9.53 us
  transfers between devices with their start and end apart: 13, of which 10 were waited for; matrix products, arithmetic and copies ran while one was open for 4% of the time, Pallas kernels for 0%

profile of v10, /device:TPU:113, one launch (start us, length us, event | category | flops | bytes accessed | tf_op | source)
XLA Modules:
  0.0 176.3 jit_solution(8147218506458266505)
XLA Ops:
  0.0 0.8 pad_maximum_fusion.2
  0.8 2.6 %collective-permute-start = (f32[2,183]{1,0:T(2,128)S(1)}, f32[2,183]{1,0:T(2,128)S(1)}, u32[]{:S(2)}, u32[]{:S(2)}) collective-permute-start(f32[2,183]{1,0:T(2,128)S(1)} %pad_maximum_fusion.2), channel_id=1, source_target_pairs={{0,256},{256,0},{512,768},{768,512},{1,257},{257,1},{513,769},{769... | collective-permute-start | bytes 4400 | tf_op jit(solution)/shard_map/ppermute | solution.py:60
  3.4 0.9 dynamic-slice_convert_fusion
  4.4 5.1 %collective-permute-start.1 = (bf16[16,16,128]{2,1,0:T(8,128)(2,1)S(1)}, bf16[16,16,128]{2,1,0:T(8,128)(2,1)S(1)}, u32[]{:S(2)}, u32[]{:S(2)}) collective-permute-start(bf16[16,16,128]{2,1,0:T(8,128)(2,1)S(1)} %dynamic-slice_convert_fusion), channel_id=1, source_target_pairs={{0,8},{8,16},{16,24},{24,32},{32,40},{40,48},{48,56},{56,64},{64,7... | collective-permute-start | bytes 196616 | tf_op jit(solution)/shard_map/ppermute | solution.py:14
  9.5 1.9 %collective-permute-start.2 = (bf16[16,16,128]{2,1,0:T(8,128)(2,1)S(1)}, bf16[16,16,128]{2,1,0:T(8,128)(2,1)S(1)}, u32[]{:S(2)}, u32[]{:S(2)}) collective-permute-start(bf16[16,16,128]{2,1,0:T(8,128)(2,1)S(1)} %dynamic-slice_convert_fusion), channel_id=1, source_target_pairs={{8,0},{16,8},{24,16},{32,24},{40,32},{48,40},{56,48},{64,56},{72,6... | collective-permute-start | bytes 196616 | tf_op jit(solution)/shard_map/ppermute | solution.py:15
  11.4 1.0 copy.31
  12.5 0.1 maximum_select_fusion.1
  12.6 0.2 slice_reduce_fusion
  12.8 0.1 divide_convert_fusion.1
  12.9 0.1 pad_slice_fusion.3
  13.0 0.1 rev.3
  13.1 0.2 copy.57
  13.3 0.1 slice.118
  13.4 0.7 reshape.82
  14.1 0.1 tile.19
  14.2 0.1 reshape.83
  14.4 2.9 %collective-permute-done.2 = bf16[16,16,128]{2,1,0:T(8,128)(2,1)S(1)} collective-permute-done((bf16[16,16,128]{2,1,0:T(8,128)(2,1)S(1)}, bf16[16,16,128]{2,1,0:T(8,128)(2,1)S(1)}, u32[]{:S(2)}, u32[]{:S(2)}) %collective-permute-start.2) | collective-permute-done | bytes 65568 | tf_op jit(solution)/shard_map/ppermute | solution.py:15
  17.2 0.6 fusion.5
  17.8 0.1 copy.30
  17.9 0.8 pad_maximum_fusion
  18.7 18.1 %all-to-all-start = ((bf16[16,128,128]{2,1,0:T(8,128)(2,1)}), bf16[16,128,128]{2,1,0:T(8,128)(2,1)S(1)}, u32[]{:S(2)}, u32[]{:S(2)}) async-start(bf16[16,128,128]{2,1,0:T(8,128)(2,1)} %pad_maximum_fusion), calls=%async_computation | async-start | bytes 1048576 | tf_op jit(solution)/shard_map/all_to_all | solution.py:79
  36.8 0.2 slice_reduce_fusion.2
  37.0 0.1 divide_convert_fusion
  37.1 0.1 pad_slice_fusion.1
  37.2 0.1 broadcast_bitcast_fusion
  37.3 0.8 copy.56
  38.1 0.4 slice.115
  38.5 1.8 reshape.88
  40.3 0.2 copy.34
  40.5 11.1 %all-to-all-done = bf16[16,128,128]{2,1,0:T(8,128)(2,1)S(1)} async-done(((bf16[16,128,128]{2,1,0:T(8,128)(2,1)}), bf16[16,128,128]{2,1,0:T(8,128)(2,1)S(1)}, u32[]{:S(2)}, u32[]{:S(2)}) %all-to-all-start) | async-done | bytes 524320 | tf_op jit(solution)/shard_map/all_to_all | solution.py:79
  51.6 0.1 convert_bitcast_fusion
  51.7 0.5 fusion.15
  52.4 14.9 %all_to_all.20 = bf16[16,64,128]{2,1,0:T(8,128)(2,1)S(1)} all-to-all(bf16[16,64,128]{2,1,0:T(8,128)(2,1)S(1)} %bitcast.140), channel_id=1, replica_groups={{0,1,2,3,4,5,6,7,256,257,258,259,260,261,262,263},{512,513,514,515,516,..., dimensions={0} | all-to-all | bytes 524288 | tf_op jit(solution)/shard_map/all_to_all | solution.py:79
  67.3 0.1 copy.39
  67.3 2.4 %collective-permute-start.3 = (bf16[4,16,16,128]{3,2,0,1:T(8,128)(2,1)S(1)}, bf16[4,16,16,128]{3,2,0,1:T(8,128)(2,1)S(1)}, u32[]{:S(2)}, u32[]{:S(2)}) collective-permute-start(bf16[4,16,16,128]{3,2,0,1:T(8,128)(2,1)S(1)} %copy.39), channel_id=1, source_target_pairs={{0,8},{8,16},{16,24},{24,32},{32,40},{40,48},{48,56},{56,64},{64,7... | collective-permute-start | bytes 786440 | tf_op jit(solution)/shard_map/ppermute | solution.py:14
  69.7 2.9 %collective-permute-start.4 = (bf16[4,16,16,128]{3,2,0,1:T(8,128)(2,1)S(1)}, bf16[4,16,16,128]{3,2,0,1:T(8,128)(2,1)}, u32[]{:S(2)}, u32[]{:S(2)}) collective-permute-start(bf16[4,16,16,128]{3,2,0,1:T(8,128)(2,1)S(1)} %copy.39), channel_id=1, source_target_pairs={{8,0},{16,8},{24,16},{32,24},{40,32},{48,40},{56,48},{64,56},{72,6... | collective-permute-start | bytes 786440 | tf_op jit(solution)/shard_map/ppermute | solution.py:15
  72.6 0.1 tile.43
  72.7 0.1 reshape.94
  72.8 3.4 %collective-permute-done.3 = bf16[4,16,16,128]{3,2,0,1:T(8,128)(2,1)S(1)} collective-permute-done((bf16[4,16,16,128]{3,2,0,1:T(8,128)(2,1)S(1)}, bf16[4,16,16,128]{3,2,0,1:T(8,128)(2,1)S(1)}, u32[]{:S(2)}, u32[]{:S(2)}) %collective-permute-start.3) | collective-permute-done | bytes 262176 | tf_op jit(solution)/shard_map/ppermute | solution.py:14
  76.3 0.1 slice.127
  76.4 4.8 %collective-permute-done.4 = bf16[4,16,16,128]{3,2,0,1:T(8,128)(2,1)} collective-permute-done((bf16[4,16,16,128]{3,2,0,1:T(8,128)(2,1)S(1)}, bf16[4,16,16,128]{3,2,0,1:T(8,128)(2,1)}, u32[]{:S(2)}, u32[]{:S(2)}) %collective-permute-start.4) | collective-permute-done | bytes 262176 | tf_op jit(solution)/shard_map/ppermute | solution.py:15
  81.2 1.5 fusion.17
  82.6 1.9 %collective-permute-start.5 = (f32[16,16,128]{2,1,0:T(8,128)S(1)}, f32[16,16,128]{2,1,0:T(8,128)S(1)}, u32[]{:S(2)}, u32[]{:S(2)}) collective-permute-start(f32[16,16,128]{2,1,0:T(8,128)S(1)} %fusion.17), channel_id=1, source_target_pairs={{0,512},{256,768},{512,0},{768,256},{1,513},{257,769},{513,1},{769... | collective-permute-start | bytes 393224 | tf_op jit(solution)/shard_map/ppermute | solution.py:140
  84.5 7.7 %collective-permute-done.5 = f32[16,16,128]{2,1,0:T(8,128)S(1)} collective-permute-done((f32[16,16,128]{2,1,0:T(8,128)S(1)}, f32[16,16,128]{2,1,0:T(8,128)S(1)}, u32[]{:S(2)}, u32[]{:S(2)}) %collective-permute-start.5) | collective-permute-done | bytes 131104 | tf_op jit(solution)/shard_map/ppermute | solution.py:140
  92.3 5.6 %collective-permute-start.6 = (bf16[16,16,128]{2,1,0:T(8,128)(2,1)S(1)}, bf16[16,16,128]{2,1,0:T(8,128)(2,1)S(1)}, u32[]{:S(2)}, u32[]{:S(2)}) collective-permute-start(bf16[16,16,128]{2,1,0:T(8,128)(2,1)S(1)} %get-tuple-element.7), channel_id=1, source_target_pairs={{0,8},{8,16},{16,24},{24,32},{32,40},{40,48},{48,56},{56,64},{64,7... | collective-permute-start | bytes 196616 | tf_op jit(solution)/shard_map/ppermute | solution.py:14
  97.9 1.9 %collective-permute-start.7 = (bf16[16,16,128]{2,1,0:T(8,128)(2,1)S(1)}, bf16[16,16,128]{2,1,0:T(8,128)(2,1)S(1)}, u32[]{:S(2)}, u32[]{:S(2)}) collective-permute-start(bf16[16,16,128]{2,1,0:T(8,128)(2,1)S(1)} %get-tuple-element.7), channel_id=1, source_target_pairs={{8,0},{16,8},{24,16},{32,24},{40,32},{48,40},{56,48},{64,56},{72,6... | collective-permute-start | bytes 196616 | tf_op jit(solution)/shard_map/ppermute | solution.py:15
  99.9 5.7 %collective-permute-done.7 = bf16[16,16,128]{2,1,0:T(8,128)(2,1)S(1)} collective-permute-done((bf16[16,16,128]{2,1,0:T(8,128)(2,1)S(1)}, bf16[16,16,128]{2,1,0:T(8,128)(2,1)S(1)}, u32[]{:S(2)}, u32[]{:S(2)}) %collective-permute-start.7) | collective-permute-done | bytes 65568 | tf_op jit(solution)/shard_map/ppermute | solution.py:15
  105.6 0.6 fusion.4
  106.2 0.1 copy.42
  106.3 20.1 %all_to_all.21 = bf16[16,64,128]{2,1,0:T(8,128)(2,1)S(1)} all-to-all(bf16[16,64,128]{2,1,0:T(8,128)(2,1)S(1)} %bitcast.143), channel_id=1, replica_groups={{0,1,2,3,4,5,6,7,256,257,258,259,260,261,262,263},{512,513,514,515,516,..., dimensions={0} | all-to-all | bytes 524288 | tf_op jit(solution)/shard_map/all_to_all | solution.py:79
  126.3 0.5 fusion.14
  126.9 14.4 %all_to_all.22 = bf16[16,64,128]{2,1,0:T(8,128)(2,1)S(1)} all-to-all(bf16[16,64,128]{2,1,0:T(8,128)(2,1)S(1)} %bitcast.144), channel_id=1, replica_groups={{0,1,2,3,4,5,6,7,256,257,258,259,260,261,262,263},{512,513,514,515,516,..., dimensions={0} | all-to-all | bytes 524288 | tf_op jit(solution)/shard_map/all_to_all | solution.py:79
  141.3 0.1 copy.47
  141.4 1.9 %collective-permute-start.8 = (bf16[4,16,16,128]{3,2,0,1:T(8,128)(2,1)S(1)}, bf16[4,16,16,128]{3,2,0,1:T(8,128)(2,1)S(1)}, u32[]{:S(2)}, u32[]{:S(2)}) collective-permute-start(bf16[4,16,16,128]{3,2,0,1:T(8,128)(2,1)S(1)} %copy.47), channel_id=1, source_target_pairs={{0,8},{8,16},{16,24},{24,32},{32,40},{40,48},{48,56},{56,64},{64,7... | collective-permute-start | bytes 786440 | tf_op jit(solution)/shard_map/ppermute | solution.py:14
  143.3 3.4 %collective-permute-start.9 = (bf16[4,16,16,128]{3,2,0,1:T(8,128)(2,1)S(1)}, bf16[4,16,16,128]{3,2,0,1:T(8,128)(2,1)S(1)}, u32[]{:S(2)}, u32[]{:S(2)}) collective-permute-start(bf16[4,16,16,128]{3,2,0,1:T(8,128)(2,1)S(1)} %copy.47), channel_id=1, source_target_pairs={{8,0},{16,8},{24,16},{32,24},{40,32},{48,40},{56,48},{64,56},{72,6... | collective-permute-start | bytes 786440 | tf_op jit(solution)/shard_map/ppermute | solution.py:15
  146.7 3.6 %collective-permute-done.8 = bf16[4,16,16,128]{3,2,0,1:T(8,128)(2,1)S(1)} collective-permute-done((bf16[4,16,16,128]{3,2,0,1:T(8,128)(2,1)S(1)}, bf16[4,16,16,128]{3,2,0,1:T(8,128)(2,1)S(1)}, u32[]{:S(2)}, u32[]{:S(2)}) %collective-permute-start.8) | collective-permute-done | bytes 262176 | tf_op jit(solution)/shard_map/ppermute | solution.py:14
  150.3 0.1 slice.133
  150.4 4.5 %collective-permute-done.9 = bf16[4,16,16,128]{3,2,0,1:T(8,128)(2,1)S(1)} collective-permute-done((bf16[4,16,16,128]{3,2,0,1:T(8,128)(2,1)S(1)}, bf16[4,16,16,128]{3,2,0,1:T(8,128)(2,1)S(1)}, u32[]{:S(2)}, u32[]{:S(2)}) %collective-permute-start.9) | collective-permute-done | bytes 262176 | tf_op jit(solution)/shard_map/ppermute | solution.py:15
  155.0 0.5 fusion.16
  155.4 1.9 %collective-permute-start.10 = (f32[16,16,128]{2,1,0:T(8,128)S(1)}, f32[16,16,128]{2,1,0:T(8,128)S(1)}, u32[]{:S(2)}, u32[]{:S(2)}) collective-permute-start(f32[16,16,128]{2,1,0:T(8,128)S(1)} %fusion.16), channel_id=1, source_target_pairs={{0,512},{256,768},{512,0},{768,256},{1,513},{257,769},{513,1},{769... | collective-permute-start | bytes 393224 | tf_op jit(solution)/shard_map/ppermute | solution.py:140
  157.4 7.7 %collective-permute-done.10 = f32[16,16,128]{2,1,0:T(8,128)S(1)} collective-permute-done((f32[16,16,128]{2,1,0:T(8,128)S(1)}, f32[16,16,128]{2,1,0:T(8,128)S(1)}, u32[]{:S(2)}, u32[]{:S(2)}) %collective-permute-start.10) | collective-permute-done | bytes 131104 | tf_op jit(solution)/shard_map/ppermute | solution.py:140
  165.1 9.5 %collective-permute-start.11 = (f32[16,16,128]{2,1,0:T(8,128)S(1)}, f32[16,16,128]{2,1,0:T(8,128)S(1)}, u32[]{:S(2)}, u32[]{:S(2)}) collective-permute-start(f32[16,16,128]{2,1,0:T(8,128)S(1)} %multiply_multiply_fusion), channel_id=1, source_target_pairs={{0,256},{256,0},{512,768},{768,512},{1,257},{257,1},{513,769},{769... | collective-permute-start | bytes 393224 | tf_op jit(solution)/shard_map/ppermute | solution.py:142
  174.6 1.0 collective-permute-done.11
  175.6 0.7 maximum_select_fusion
  (33 shorter events, 0.5 us)
Async XLA Ops:
  0.0 13.1 %copy-start.4 = (pred[62]{0:T(512)(128)(4,1)S(1)}, pred[62]{0:T(512)(128)(4,1)}, u32[]{:S(2)}) copy-start(pred[62]{0:T(512)(128)(4,1)} %constant.36.clone.1) | copy-start | bytes 190
  0.0 12.5 %copy-start.3 = (f32[2,31]{1,0:T(2,128)S(1)}, f32[2,31]{1,0:T(2,128)}, u32[]{:S(2)}) copy-start(f32[2,31]{1,0:T(2,128)} %param.7) | copy-start | bytes 748
  0.0 12.5 %copy-start.2 = (f32[2,31]{1,0:T(2,128)S(1)}, f32[2,31]{1,0:T(2,128)}, u32[]{:S(2)}) copy-start(f32[2,31]{1,0:T(2,128)} %param.8) | copy-start | bytes 748
  0.0 12.5 %copy-start.1 = (f32[2,121]{1,0:T(2,128)S(1)}, f32[2,121]{1,0:T(2,128)}, u32[]{:S(2)}) copy-start(f32[2,121]{1,0:T(2,128)} %param.9) | copy-start | bytes 2908
  0.8 11.6 %collective-permute-start = (f32[2,183]{1,0:T(2,128)S(1)}, f32[2,183]{1,0:T(2,128)S(1)}, u32[]{:S(2)}, u32[]{:S(2)}) collective-permute-start(f32[2,183]{1,0:T(2,128)S(1)} %pad_maximum_fusion.2), channel_id=1, source_target_pairs={{0,256},{256,0},{512,768},{768,512},{1,257},{257,1},{513,769},{769... | collective-permute-start | bytes 4400 | tf_op jit(solution)/shard_map/ppermute | solution.py:60
  4.4 10.0 %collective-permute-start.1 = (bf16[16,16,128]{2,1,0:T(8,128)(2,1)S(1)}, bf16[16,16,128]{2,1,0:T(8,128)(2,1)S(1)}, u32[]{:S(2)}, u32[]{:S(2)}) collective-permute-start(bf16[16,16,128]{2,1,0:T(8,128)(2,1)S(1)} %dynamic-slice_convert_fusion), channel_id=1, source_target_pairs={{0,8},{8,16},{16,24},{24,32},{32,40},{40,48},{48,56},{56,64},{64,7... | collective-permute-start | bytes 196616 | tf_op jit(solution)/shard_map/ppermute | solution.py:14
  9.5 7.7 %collective-permute-start.2 = (bf16[16,16,128]{2,1,0:T(8,128)(2,1)S(1)}, bf16[16,16,128]{2,1,0:T(8,128)(2,1)S(1)}, u32[]{:S(2)}, u32[]{:S(2)}) collective-permute-start(bf16[16,16,128]{2,1,0:T(8,128)(2,1)S(1)} %dynamic-slice_convert_fusion), channel_id=1, source_target_pairs={{8,0},{16,8},{24,16},{32,24},{40,32},{48,40},{56,48},{64,56},{72,6... | collective-permute-start | bytes 196616 | tf_op jit(solution)/shard_map/ppermute | solution.py:15
  18.7 32.9 %all-to-all-start = ((bf16[16,128,128]{2,1,0:T(8,128)(2,1)}), bf16[16,128,128]{2,1,0:T(8,128)(2,1)S(1)}, u32[]{:S(2)}, u32[]{:S(2)}) async-start(bf16[16,128,128]{2,1,0:T(8,128)(2,1)} %pad_maximum_fusion), calls=%async_computation | async-start | bytes 1048576 | tf_op jit(solution)/shard_map/all_to_all | solution.py:79
  67.3 8.9 %collective-permute-start.3 = (bf16[4,16,16,128]{3,2,0,1:T(8,128)(2,1)S(1)}, bf16[4,16,16,128]{3,2,0,1:T(8,128)(2,1)S(1)}, u32[]{:S(2)}, u32[]{:S(2)}) collective-permute-start(bf16[4,16,16,128]{3,2,0,1:T(8,128)(2,1)S(1)} %copy.39), channel_id=1, source_target_pairs={{0,8},{8,16},{16,24},{24,32},{32,40},{40,48},{48,56},{56,64},{64,7... | collective-permute-start | bytes 786440 | tf_op jit(solution)/shard_map/ppermute | solution.py:14
  69.7 11.5 %collective-permute-start.4 = (bf16[4,16,16,128]{3,2,0,1:T(8,128)(2,1)S(1)}, bf16[4,16,16,128]{3,2,0,1:T(8,128)(2,1)}, u32[]{:S(2)}, u32[]{:S(2)}) collective-permute-start(bf16[4,16,16,128]{3,2,0,1:T(8,128)(2,1)S(1)} %copy.39), channel_id=1, source_target_pairs={{8,0},{16,8},{24,16},{32,24},{40,32},{48,40},{56,48},{64,56},{72,6... | collective-permute-start | bytes 786440 | tf_op jit(solution)/shard_map/ppermute | solution.py:15
  81.1 11.1 %copy-start = (f32[32,16,128]{2,1,0:T(8,128)S(1)}, f32[32,16,128]{2,1,0:T(8,128)}, u32[]{:S(2)}) copy-start(f32[32,16,128]{2,1,0:T(8,128)} %param.5) | copy-start | bytes 786436
  82.6 9.6 %collective-permute-start.5 = (f32[16,16,128]{2,1,0:T(8,128)S(1)}, f32[16,16,128]{2,1,0:T(8,128)S(1)}, u32[]{:S(2)}, u32[]{:S(2)}) collective-permute-start(f32[16,16,128]{2,1,0:T(8,128)S(1)} %fusion.17), channel_id=1, source_target_pairs={{0,512},{256,768},{512,0},{768,256},{1,513},{257,769},{513,1},{769... | collective-permute-start | bytes 393224 | tf_op jit(solution)/shard_map/ppermute | solution.py:140
  92.3 7.6 %collective-permute-start.6 = (bf16[16,16,128]{2,1,0:T(8,128)(2,1)S(1)}, bf16[16,16,128]{2,1,0:T(8,128)(2,1)S(1)}, u32[]{:S(2)}, u32[]{:S(2)}) collective-permute-start(bf16[16,16,128]{2,1,0:T(8,128)(2,1)S(1)} %get-tuple-element.7), channel_id=1, source_target_pairs={{0,8},{8,16},{16,24},{24,32},{32,40},{40,48},{48,56},{56,64},{64,7... | collective-permute-start | bytes 196616 | tf_op jit(solution)/shard_map/ppermute | solution.py:14
  97.9 7.7 %collective-permute-start.7 = (bf16[16,16,128]{2,1,0:T(8,128)(2,1)S(1)}, bf16[16,16,128]{2,1,0:T(8,128)(2,1)S(1)}, u32[]{:S(2)}, u32[]{:S(2)}) collective-permute-start(bf16[16,16,128]{2,1,0:T(8,128)(2,1)S(1)} %get-tuple-element.7), channel_id=1, source_target_pairs={{8,0},{16,8},{24,16},{32,24},{40,32},{48,40},{56,48},{64,56},{72,6... | collective-permute-start | bytes 196616 | tf_op jit(solution)/shard_map/ppermute | solution.py:15
  141.4 8.9 %collective-permute-start.8 = (bf16[4,16,16,128]{3,2,0,1:T(8,128)(2,1)S(1)}, bf16[4,16,16,128]{3,2,0,1:T(8,128)(2,1)S(1)}, u32[]{:S(2)}, u32[]{:S(2)}) collective-permute-start(bf16[4,16,16,128]{3,2,0,1:T(8,128)(2,1)S(1)} %copy.47), channel_id=1, source_target_pairs={{0,8},{8,16},{16,24},{24,32},{32,40},{40,48},{48,56},{56,64},{64,7... | collective-permute-start | bytes 786440 | tf_op jit(solution)/shard_map/ppermute | solution.py:14
  143.3 11.6 %collective-permute-start.9 = (bf16[4,16,16,128]{3,2,0,1:T(8,128)(2,1)S(1)}, bf16[4,16,16,128]{3,2,0,1:T(8,128)(2,1)S(1)}, u32[]{:S(2)}, u32[]{:S(2)}) collective-permute-start(bf16[4,16,16,128]{3,2,0,1:T(8,128)(2,1)S(1)} %copy.47), channel_id=1, source_target_pairs={{8,0},{16,8},{24,16},{32,24},{40,32},{48,40},{56,48},{64,56},{72,6... | collective-permute-start | bytes 786440 | tf_op jit(solution)/shard_map/ppermute | solution.py:15
  155.4 9.6 %collective-permute-start.10 = (f32[16,16,128]{2,1,0:T(8,128)S(1)}, f32[16,16,128]{2,1,0:T(8,128)S(1)}, u32[]{:S(2)}, u32[]{:S(2)}) collective-permute-start(f32[16,16,128]{2,1,0:T(8,128)S(1)} %fusion.16), channel_id=1, source_target_pairs={{0,512},{256,768},{512,0},{768,256},{1,513},{257,769},{513,1},{769... | collective-permute-start | bytes 393224 | tf_op jit(solution)/shard_map/ppermute | solution.py:140
  165.1 10.5 %collective-permute-start.11 = (f32[16,16,128]{2,1,0:T(8,128)S(1)}, f32[16,16,128]{2,1,0:T(8,128)S(1)}, u32[]{:S(2)}, u32[]{:S(2)}) collective-permute-start(f32[16,16,128]{2,1,0:T(8,128)S(1)} %multiply_multiply_fusion), channel_id=1, source_target_pairs={{0,256},{256,0},{512,768},{768,512},{1,257},{257,1},{513,769},{769... | collective-permute-start | bytes 393224 | tf_op jit(solution)/shard_map/ppermute | solution.py:142
